TPU v7x, 512 devices: a whole 4x8x8 slice. The times are simulated.
512 devices in a mesh: dom: 64 (over z_hi, y, core), cls: 8 (over z_lo, x).
Axes of the slice: x: 4, y: 8, z: 8 (z_hi: 4, z_lo: 2; z = z_hi * 2 + z_lo), core: 2. Of those that a mesh axis runs over, the one named last changes fastest.
Arguments:
- particles: bfloat16 [512, 64, 64], P(('dom', 'cls')), as said below
- group_ids: int32 [512], P(('dom', 'cls')), may hold values from 0 to 15
- references: float32 [96, 4096], P('cls', 'dom'), as said below
- ctf_profile: float32 [16, 23], replicated, may hold values from 0.1 to 1
- noise_power: float32 [23], replicated, may hold values from 2 to 16
Outputs:
- new_refs: float32 [2, 96, 1024], P(None, 'cls', 'dom')
- log_evidence: float32 [512], P('dom')
Inputs may be any that keep to these rules, and one draw needn't show every extreme that they name: `particles`: pixel values. `references`: pixel values.
All inputs are finite; a program needn't handle non-finite values.
Results may differ from a plain program's by a relative error of at most 0.011.
Values may be sent and summed in bfloat16 or wider, within the bound.
No kernel may reach another device: no remote copies, remote signals or barrier semaphores. Data moves between devices by JAX's collectives and lax.ppermute only.
A program may use at most 64 MiB of HBM per device.

v0:
```python
import math

import jax
import jax.numpy as jnp
from jax import lax
from jax.sharding import PartitionSpec as P

L = 64
BAND = 32
ROT = 8
NRAD = 23
GROUPS = 16


HIGHEST = lax.Precision.HIGHEST


def phase_tables(size, band):
    pixel = jnp.arange(size, dtype=jnp.int32)
    freq = jnp.arange(band, dtype=jnp.int32) - band // 2
    turned = freq[:, None] * pixel[None, :] % size
    angle = turned.astype(jnp.float32) * (2.0 * math.pi / size)
    return (jnp.cos(angle), jnp.sin(angle))


def forward_tables(cosine, sine):
    fcos = cosine / 8.0
    fsin = sine / 8.0
    first_table_part = jnp.stack([fcos.T, -fsin.T], axis=1)
    second_table_part = jnp.stack(
        [jnp.stack([fcos.T, -fsin.T], axis=1), jnp.stack([fsin.T, fcos.T], axis=1)], axis=1
    )
    return (first_table_part, second_table_part)


def inverse_tables(cosine, sine):
    icos = cosine.astype(jnp.bfloat16)
    isin = sine.astype(jnp.bfloat16)
    tab_c = jnp.stack([jnp.stack([icos, isin], axis=1), jnp.stack([-isin, icos], axis=1)], axis=0)
    tab_d = jnp.stack([icos, -isin], axis=0)
    tab_e = jnp.stack([icos.T, isin.T], axis=1)
    tab_f = jnp.stack(
        [jnp.stack([icos.T, isin.T], axis=1), jnp.stack([-isin.T, icos.T], axis=1)], axis=1
    )
    return (tab_c, tab_d, tab_e, tab_f)


def product(form, left, right):
    return jnp.einsum(form, left, right, preferred_element_type=jnp.float32)


def orient(images):
    turned = jnp.swapaxes(images, 1, 2)
    views = [jnp.rot90(images, j, axes=(1, 2)) for j in range(4)]
    views = views + [jnp.rot90(turned, j, axes=(1, 2)) for j in range(4)]
    return jnp.stack(views, axis=1)


def particle_band_rows(images, first_table_part, second_table_part):
    count = images.shape[0]
    oriented = orient(images)
    half = product("nryx,xdb->nrydb", oriented, first_table_part).astype(jnp.bfloat16)
    full = product("nrydb,ydca->nrcab", half, second_table_part).astype(jnp.bfloat16)
    return full.reshape(count, ROT, 2, BAND * BAND)


def class_bands(maps, first_table_part, second_table_part):
    count = maps.shape[0]
    images = maps.reshape(count, L, L)
    half = jnp.einsum("kyx,xdb->kydb", images, first_table_part, precision=HIGHEST)
    full = jnp.einsum("kydb,ydca->kcab", half, second_table_part, precision=HIGHEST)
    return full.reshape(count, 2, BAND * BAND)


def shell_onehot():
    freq = jnp.arange(BAND, dtype=jnp.int32) - BAND // 2
    square = (freq[:, None] ** 2 + freq[None, :] ** 2).reshape(-1)
    bounds = jnp.arange(1, NRAD, dtype=jnp.int32) ** 2
    shell = jnp.sum((square[None, :] >= bounds[:, None]).astype(jnp.int32), axis=0)
    return (shell[None, :] == jnp.arange(NRAD, dtype=jnp.int32)[:, None]).astype(jnp.float32)


def group_onehot(group_ids):
    return (group_ids[:, None] == jnp.arange(GROUPS, dtype=jnp.int32)[None, :]).astype(jnp.float32)


def spectra(ctf_profile, noise_power, group_ids):
    shells = shell_onehot()
    groups = group_onehot(group_ids)
    profile = jnp.dot(groups, ctf_profile, precision=HIGHEST)
    contrast_transfer = jnp.dot(profile, shells, precision=HIGHEST)
    noise_deviation = jnp.dot(noise_power, shells, precision=HIGHEST)
    return (contrast_transfer, noise_deviation)


def class_step(abstract_value, output_value, ref_band, offset, tabs):
    tab_c, tab_d, tab_e, tab_f = tabs
    count = abstract_value.shape[0]
    real_ref = ref_band[0]
    imag_ref = ref_band[1]
    breal = abstract_value[:, :, 0] * real_ref + abstract_value[:, :, 1] * imag_ref
    bimag = abstract_value[:, :, 1] * real_ref - abstract_value[:, :, 0] * imag_ref
    bmat = jnp.stack([breal, bimag], axis=2).astype(jnp.bfloat16).reshape(count, ROT, 2, BAND, BAND)
    edge = product("nrcab,cbdx->nradx", bmat, tab_c).astype(jnp.bfloat16)
    score = product("nradx,day->nyrx", edge, tab_d) - offset[:, None, None, None]
    peak = jnp.max(score, axis=(1, 2, 3))
    expo = jnp.exp(score - peak[:, None, None, None])
    total = jnp.sum(expo, axis=(1, 2, 3))
    uhalf = product("nyrx,xdb->nrydb", expo.astype(jnp.bfloat16), tab_e).astype(jnp.bfloat16)
    what = product("nrydb,ydca->nrcab", uhalf, tab_f).astype(jnp.bfloat16)
    what = what.reshape(count, ROT, 2, BAND * BAND).astype(jnp.float32)
    preal = jnp.sum(
        output_value[:, :, 0] * what[:, :, 0] - output_value[:, :, 1] * what[:, :, 1], axis=1
    )
    pimag = jnp.sum(
        output_value[:, :, 0] * what[:, :, 1] + output_value[:, :, 1] * what[:, :, 0], axis=1
    )
    return (peak, total, jnp.stack([preal, pimag], axis=1))


def shards(particles, group_ids, references, ctf_profile, noise_power):
    cosine, sine = phase_tables(L, BAND)
    first_table_part, second_table_part = forward_tables(cosine, sine)
    tabs = inverse_tables(cosine, sine)
    first_low = first_table_part.astype(jnp.bfloat16)
    second_low = second_table_part.astype(jnp.bfloat16)
    own_bands = particle_band_rows(particles, first_low, second_low)
    fourier_input, block_labels = (
        lax.all_gather(own_bands, "cls", axis=0, tiled=True),
        lax.all_gather(group_ids, "cls", axis=0, tiled=True),
    )
    maps = lax.all_gather(references, "dom", axis=1, tiled=True)
    complete_input = fourier_input.astype(jnp.float32)
    contrast_transfer, noise_deviation = spectra(ctf_profile, noise_power, block_labels)
    abstract_value = (
        complete_input * (contrast_transfer / noise_deviation[None, :])[:, None, None, :]
    )
    output_value = complete_input * contrast_transfer[:, None, None, :]
    rbands = class_bands(maps, first_table_part, second_table_part)
    power = rbands[:, 0] ** 2 + rbands[:, 1] ** 2
    offset = 0.5 * jnp.dot(
        contrast_transfer * contrast_transfer / noise_deviation[None, :], power.T, precision=HIGHEST
    )
    peaks, totals, projs = lax.map(
        lambda item: class_step(abstract_value, output_value, item[0], item[1], tabs),
        (rbands, offset.T),
    )
    local_top = jnp.max(peaks, axis=0)
    top = lax.pmax(local_top, "cls")
    mass = lax.psum(jnp.sum(jnp.exp(peaks - top[None, :]) * totals, axis=0), "cls")
    log_evidence = top + jnp.log(mass)
    share = jnp.exp(peaks - top[None, :]) / mass[None, :]
    numer = jnp.einsum("kp,kpcf->ckf", share, projs, precision=HIGHEST)
    denom = jnp.dot(share * totals, contrast_transfer * contrast_transfer, precision=HIGHEST)
    stacked = jnp.concatenate([numer, denom[None]], axis=0)
    owned = lax.psum_scatter(stacked, "dom", scatter_dimension=2, tiled=True)
    new_refs = owned[:2] / (owned[2] + 1.0)[None]
    return (new_refs, log_evidence)


def solution(mesh):
    in_specs = (P(("dom", "cls"), None, None), P(("dom", "cls")), P("cls", "dom"), P(), P())
    out_specs = (P(None, "cls", "dom"), P("dom"))
    return jax.shard_map(shards, mesh=mesh, in_specs=in_specs, out_specs=out_specs, check_vma=False)
```

profile of v0, /device:TPU:1, one launch (start us, length us, event | category | flops | bytes accessed | tf_op | source)
XLA Modules:
  0.0 474.5 jit_solution(10457496222113710703)
XLA Ops:
  12.3 1.3 dynamic-slice
  14.4 10.8 %all-reduce = s32[8]{0:T(128)S(1)} all-reduce(s32[8]{0:T(128)S(1)} %dynamic-update-slice), channel_id=1, replica_groups=mesh['dom'=64,'cls'=8] {'cls'}, use_global_device_ids=true, to_apply=%add | all-reduce | flops 8 | bytes 64
  26.1 22.7 %all_gather.9 = bf16[8,8,2,1024]{3,1,2,0:T(8,128)(2,1)S(1)} all-gather(bf16[1,8,2,1024]{3,1,2,0:T(8,128)(2,1)S(1)} %reshape.517), channel_id=1, replica_groups=mesh['dom'=64,'cls'=8] {'cls'}, dimensions={0}, use_global_device_ids=true | all-gather | bytes 294912 | tf_op jit(solution)/shard_map/all_gather | solution.py:129
  51.0 98.3 %all-gather = f32[64,64,12]{1,2,0:T(8,128)S(1)} all-gather(f32[1,64,12]{1,2,0:T(8,128)S(1)} %bitcast.282), channel_id=1, replica_groups=mesh['dom'=64,'cls'=8] {'dom'}, dimensions={0}, use_global_device_ids=true | all-gather | bytes 199680 | tf_op jit(solution)/shard_map/all_gather | solution.py:132
  149.7 1.2 convolution_bitcast_fusion.1
  152.8 140.1 %while.14 = (s32[]{:T(128)}, f32[12,8]{1,0:T(8,128)S(1)}, f32[12,8]{1,0:T(8,128)S(1)}, f32[12,8,2,1024]{3,1,2,0:T(8,128)}, f32[8,8,2,1024]{3,1,0,2:T(8,128)}, /*...) while((s32[]{:T(128)}, f32[12,8]{1,0:T(8,128)S(1)}, ...), condition=%wide.region_6.7_spmd, body=%wide.region_1.6_spmd.sunk | while | flops 138674160 | bytes 8921689 | solution.py:144
  154.3 1.2 stack.143
  155.5 2.3 fusion.116
  158.4 2.2 convert_bitcast_fusion.2
  160.6 1.9 copy.111
  164.5 1.1 add_convert_fusion.2
  166.0 1.2 stack.143
  167.1 2.3 fusion.116
  170.1 2.2 convert_bitcast_fusion.2
  172.3 1.9 copy.111
  176.2 1.1 add_convert_fusion.2
  177.7 1.2 stack.143
  178.8 2.3 fusion.116
  181.8 2.2 convert_bitcast_fusion.2
  184.0 1.9 copy.111
  187.9 1.1 add_convert_fusion.2
  189.3 1.2 stack.143
  190.5 2.3 fusion.116
  193.4 2.2 convert_bitcast_fusion.2
  195.6 1.9 copy.111
  199.5 1.1 add_convert_fusion.2
  201.0 1.2 stack.143
  202.2 2.3 fusion.116
  205.1 2.2 convert_bitcast_fusion.2
  207.3 1.9 copy.111
  211.2 1.1 add_convert_fusion.2
  212.7 1.2 stack.143
  213.8 2.3 fusion.116
  216.8 2.2 convert_bitcast_fusion.2
  219.0 1.9 copy.111
  224.4 1.2 stack.143
  225.5 2.3 fusion.116
  228.5 2.2 convert_bitcast_fusion.2
  230.7 1.9 copy.111
  236.0 1.2 stack.143
  237.2 2.3 fusion.116
  240.1 2.2 convert_bitcast_fusion.2
  242.3 1.9 copy.111
  247.7 1.2 stack.143
  248.8 2.3 fusion.116
  251.8 2.2 convert_bitcast_fusion.2
  254.0 1.9 copy.111
  259.4 1.2 stack.143
  260.5 2.3 fusion.116
  263.5 2.2 convert_bitcast_fusion.2
  265.7 1.9 copy.111
  271.0 1.2 stack.143
  272.2 2.3 fusion.116
  275.1 2.2 convert_bitcast_fusion.2
  277.3 1.9 copy.111
  282.7 1.2 stack.143
  283.9 2.3 fusion.116
  286.8 2.2 convert_bitcast_fusion.2
  289.0 1.9 copy.111
  292.9 13.2 %pmax.7 = f32[8]{0:T(128)S(1)} all-reduce(f32[8]{0:T(128)S(1)} %reduce_max.18), channel_id=1, replica_groups=mesh['dom'=64,'cls'=8] {'cls'}, use_global_device_ids=true, to_apply=%region_8.9 | all-reduce | flops 8 | bytes 64 | tf_op jit(solution)/shard_map/pmax | solution.py:149
  306.2 13.4 %psum.7 = f32[8]{0:T(128)S(1)} all-reduce(f32[8]{0:T(128)S(1)} %multiply_reduce_fusion), channel_id=1, replica_groups=mesh['dom'=64,'cls'=8] {'cls'}, use_global_device_ids=true, to_apply=%region_10.11 | all-reduce | flops 8 | bytes 64 | tf_op jit(solution)/shard_map/psum | solution.py:150
  319.9 1.9 fusion.79
  322.7 1.5 reshape.554
  324.8 141.2 %reduce-scatter.4.cloned.1.call-done = f32[16,36]{1,0:T(8,128)} async-done(((f32[1024,36]{1,0:T(8,128)}), f32[16,36]{1,0:T(8,128)}) %reduce-scatter.4.cloned.1.call-update) | async-done | bytes 2320
  (228 shorter events, 56.9 us)
Async XLA Ops:
  7.2 42.5 %copy-start = (f32[16,23]{1,0:T(8,128)S(1)}, f32[16,23]{1,0:T(8,128)}, u32[]{:S(2)}) copy-start(f32[16,23]{1,0:T(8,128)} %param.10) | copy-start | bytes 4420
  7.2 458.8 %reduce-scatter.4.cloned.1.call-start = ((), (), s32[]{:S(2)}) async-start(), calls=%async_computation.1 | async-start | bytes 532480
  9.6 41.4 %copy-start.1 = (f32[12,64]{1,0:T(8,128)S(1)}, f32[12,64]{1,0:T(8,128)}, u32[]{:S(2)}) copy-start(f32[12,64]{1,0:T(8,128)} %param.9) | copy-start | bytes 9220
Sparse Core Ops, SparseCore 0:
  324.4 141.5 reduce-scatter.3
where the time goes:
time: 480 us; the launch traced here: 474 us
  blocking collectives  158 us (33%)
  waiting for transfers between devices  141 us (29%)
  local copies, waits for them, and re-layouts  73.4 us (15%)
  matrix products  60.1 us (13%)
  other arithmetic  25.5 us (5%)
  between operations  15 us (3%)
    unnamed x2, waiting for transfers between devices  141 us
    all_gather x1, blocking collectives, shards(): maps = lax.all_gather(references, 'dom', axis=1, tiled=True)  98.3 us
    dot_general x25, matrix products, product(): return jnp.einsum(form, left, right, preferred_element_type=jnp.float32)  54.3 us
    convert_element_type x24, local copies, waits for them, and re-layouts, class_step(): what = what.reshape(count, ROT, 2, BAND * BAND).astype(jnp.float32)  34.5 us
    all_gather x1, blocking collectives, shards(): lax.all_gather(own_bands, 'cls', axis=0, tiled=True)  22.7 us
    another operation x24, local copies, waits for them, and re-layouts, class_step(): jnp.stack([breal, bimag], axis=2).astype(jnp.bfloat16)  18.2 us
    psum x1, blocking collectives, shards(): lax.psum(jnp.sum(jnp.exp(peaks - top[None, :]) * totals, axis=0), 'cls')  13.4 us
    pmax x1, blocking collectives, shards(): top = lax.pmax(local_top, 'cls')  13.2 us
  transfers between devices with their start and end apart: 1, of which 1 were waited for; matrix products, arithmetic and copies ran while one was open for 0% of the time, Pallas kernels for 0%

commit v1 on v0

--- a/solution.py
+++ b/solution.py
@@ -125,11 +125,17 @@
     first_low = first_table_part.astype(jnp.bfloat16)
     second_low = second_table_part.astype(jnp.bfloat16)
     own_bands = particle_band_rows(particles, first_low, second_low)
-    fourier_input, block_labels = (
-        lax.all_gather(own_bands, "cls", axis=0, tiled=True),
-        lax.all_gather(group_ids, "cls", axis=0, tiled=True),
-    )
-    maps = lax.all_gather(references, "dom", axis=1, tiled=True)
+    count = own_bands.shape[0]
+    width = ROT * 2 * BAND * BAND
+    label_row = jnp.broadcast_to(group_ids.astype(jnp.bfloat16)[:, None], (count, 128))
+    payload = jnp.concatenate([own_bands.reshape(count, width), label_row], axis=1)
+    gathered = lax.all_gather(payload, "cls", axis=0, tiled=True)
+    fourier_input = gathered[:, :width].reshape(-1, ROT, 2, BAND * BAND)
+    block_labels = gathered[:, width].astype(jnp.int32)
+    rows = lax.psum(1, "dom")
+    spread = jnp.broadcast_to(references[None], (rows,) + references.shape)
+    pieces = lax.all_to_all(spread, "dom", 0, 0, tiled=True)
+    maps = jnp.transpose(pieces, (1, 0, 2)).reshape(references.shape[0], -1)
     complete_input = fourier_input.astype(jnp.float32)
     contrast_transfer, noise_deviation = spectra(ctf_profile, noise_power, block_labels)
     abstract_value = (
@@ -146,14 +152,18 @@
         (rbands, offset.T),
     )
     local_top = jnp.max(peaks, axis=0)
-    top = lax.pmax(local_top, "cls")
-    mass = lax.psum(jnp.sum(jnp.exp(peaks - top[None, :]) * totals, axis=0), "cls")
+    local_mass = jnp.sum(jnp.exp(peaks - local_top[None, :]) * totals, axis=0)
+    summary = lax.all_gather(jnp.stack([local_top, local_mass]), "cls", axis=0)
+    top = jnp.max(summary[:, 0], axis=0)
+    mass = jnp.sum(jnp.exp(summary[:, 0] - top[None, :]) * summary[:, 1], axis=0)
     log_evidence = top + jnp.log(mass)
     share = jnp.exp(peaks - top[None, :]) / mass[None, :]
     numer = jnp.einsum("kp,kpcf->ckf", share, projs, precision=HIGHEST)
     denom = jnp.dot(share * totals, contrast_transfer * contrast_transfer, precision=HIGHEST)
     stacked = jnp.concatenate([numer, denom[None]], axis=0)
-    owned = lax.psum_scatter(stacked, "dom", scatter_dimension=2, tiled=True)
+    lanes = stacked.shape[2] // rows
+    parts = jnp.moveaxis(stacked.reshape(3, stacked.shape[1], rows, lanes), 2, 0)
+    owned = jnp.sum(lax.all_to_all(parts, "dom", 0, 0, tiled=True), axis=0)
     new_refs = owned[:2] / (owned[2] + 1.0)[None]
     return (new_refs, log_evidence)
 

time: 480 us -> 257 us (0.54)
  waiting for transfers between devices: 141 us -> 12.5 us
  blocking collectives: 158 us -> 38.6 us
  starting transfers between devices: 0.04 us -> 39.8 us
  between operations: 15 us -> 1.69 us
  other arithmetic: 25.5 us -> 30.5 us
    unnamed x2 -> x0, waiting for transfers between devices: 141 us -> none
    all_gather x2, blocking collectives: 121 us -> 38.6 us  [the longest x1 24.2 us: shards(): gathered = lax.all_gather(payload, 'cls', axis=0, tiled=True)]
    all_to_all x0 -> x2, starting transfers between devices: none -> 39.8 us  [the longest x1 22.2 us: shards(): owned = jnp.sum(lax.all_to_all(parts, 'dom', 0, 0, tiled=True), axis=0)]
    psum x1 -> x0, blocking collectives: 13.4 us -> none  [shards(): lax.psum(jnp.sum(jnp.exp(peaks - top[None, :]) * totals, axis=0), 'cls')]
    pmax x1 -> x0, blocking collectives: 13.2 us -> none  [shards(): top = lax.pmax(local_top, 'cls')]
    reduce_sum x12, other arithmetic: 2.43 us -> 15.1 us  [class_step(): jnp.sum(output_value[:, :, 0] * what[:, :, 0] - output_value[:, :, 1] * w...]
    all_to_all x0 -> x2, waiting for transfers between devices: none -> 12.5 us  [the longest x1 12.5 us: shards(): owned = jnp.sum(lax.all_to_all(parts, 'dom', 0, 0, tiled=True), axis=0)]
    another operation x14, other arithmetic: 13.2 us -> 0.83 us
  transfers between devices with their start and end apart: 1 -> 2, of which waited for: 1 -> 1; matrix products, arithmetic and copies ran while one was open for 0% -> 3% of each run, Pallas kernels for 0% -> 0%
where the time goes in v1:
time: 257 us; the launch traced here: 256 us
  local copies, waits for them, and re-layouts  72.5 us (28%)
  matrix products  59.5 us (23%)
  starting transfers between devices  39.8 us (15%)
  blocking collectives  38.6 us (15%)
  other arithmetic  30.5 us (12%)
  waiting for transfers between devices  12.5 us (5%)
    dot_general x25, matrix products, product(): return jnp.einsum(form, left, right, preferred_element_type=jnp.float32)  54.3 us
    convert_element_type x24, local copies, waits for them, and re-layouts, class_step(): what = what.reshape(count, ROT, 2, BAND * BAND).astype(jnp.float32)  34.5 us
    all_gather x1, blocking collectives, shards(): gathered = lax.all_gather(payload, 'cls', axis=0, tiled=True)  24.2 us
    all_to_all x1, starting transfers between devices, shards(): owned = jnp.sum(lax.all_to_all(parts, 'dom', 0, 0, tiled=True), axis=0)  22.2 us
    another operation x24, local copies, waits for them, and re-layouts, class_step(): jnp.stack([breal, bimag], axis=2).astype(jnp.bfloat16)  18.2 us
    all_to_all x1, starting transfers between devices, shards(): pieces = lax.all_to_all(spread, 'dom', 0, 0, tiled=True)  17.6 us
    reduce_sum x12, other arithmetic, class_step(): jnp.sum(output_value[:, :, 0] * what[:, :, 0] - output_value[:, :, 1] * w...  15.1 us
    all_gather x1, blocking collectives, shards(): summary = lax.all_gather(jnp.stack([local_top, local_mass]), 'cls', axis=0)  14.3 us
  transfers between devices with their start and end apart: 2, of which 1 were waited for; matrix products, arithmetic and copies ran while one was open for 3% of the time, Pallas kernels for 0%

profile of v1, /device:TPU:1, one launch (start us, length us, event | category | flops | bytes accessed | tf_op | source)
XLA Modules:
  0.0 255.8 jit_solution(17236546618829717232)
XLA Ops:
  2.3 17.6 %all-to-all-start = ((f32[64,1,768]{2,1,0:T(1,128)}), f32[64,1,768]{2,1,0:T(1,128)S(1)}, u32[]{:S(2)}, u32[]{:S(2)}) async-start(f32[64,1,768]{2,1,0:T(1,128)} %reshape.558), calls=%async_computation | async-start | bytes 393216 | tf_op jit(solution)/shard_map/all_to_all | solution.py:137
  25.1 24.2 %all-gather.1 = bf16[8,1,16512]{2,1,0:T(2,128)(2,1)S(1)} all-gather(bf16[1,1,16512]{2,1,0:T(2,128)(2,1)S(1)} %pad_bitcast_fusion), channel_id=1, replica_groups=mesh['dom'=64,'cls'=8] {'cls'}, dimensions={0}, use_global_device_ids=true | all-gather | bytes 297216 | tf_op jit(solution)/shard_map/all_gather | solution.py:132
  54.4 1.3 convolution_bitcast_fusion.1
  57.4 140.5 %while.14 = (s32[]{:T(128)}, f32[12,8]{1,0:T(8,128)S(1)}, f32[12,8]{1,0:T(8,128)S(1)}, f32[12,8,2,1024]{3,1,2,0:T(8,128)}, f32[8,8,2,1024]{3,1,0,2:T(8,128)S(1)}...) while((s32[]{:T(128)}, f32[12,8]{1,0:T(8,128)S(1)}, ...), condition=%wide.region_6.7_spmd, body=%wide.region_1.6_spmd.sunk | while | flops 138674160 | bytes 8921689 | solution.py:150
  57.9 1.2 stack.155
  59.0 2.3 fusion.117
  62.0 2.2 convert_bitcast_fusion.2
  64.2 1.9 copy.161
  67.1 1.3 subtract_reduce_fusion.2
  69.6 1.2 stack.155
  70.7 2.3 fusion.117
  73.7 2.2 convert_bitcast_fusion.2
  75.9 1.9 copy.161
  78.8 1.3 subtract_reduce_fusion.2
  81.3 1.2 stack.155
  82.4 2.3 fusion.117
  85.4 2.2 convert_bitcast_fusion.2
  87.6 1.9 copy.161
  90.5 1.3 subtract_reduce_fusion.2
  93.0 1.2 stack.155
  94.1 2.3 fusion.117
  97.1 2.2 convert_bitcast_fusion.2
  99.3 1.9 copy.161
  102.2 1.3 subtract_reduce_fusion.2
  105.9 2.3 fusion.117
  108.8 2.2 convert_bitcast_fusion.2
  111.0 1.9 copy.161
  113.9 1.3 subtract_reduce_fusion.2
  117.6 2.3 fusion.117
  120.5 2.2 convert_bitcast_fusion.2
  122.7 1.9 copy.161
  125.6 1.3 subtract_reduce_fusion.2
  129.3 2.3 fusion.117
  132.2 2.2 convert_bitcast_fusion.2
  134.4 1.9 copy.161
  137.3 1.3 subtract_reduce_fusion.2
  139.8 1.2 stack.155
  141.0 2.3 fusion.117
  143.9 2.2 convert_bitcast_fusion.2
  146.1 1.9 copy.161
  149.0 1.3 subtract_reduce_fusion.2
  151.5 1.2 stack.155
  152.7 2.3 fusion.117
  155.6 2.2 convert_bitcast_fusion.2
  157.8 1.9 copy.161
  160.7 1.3 subtract_reduce_fusion.2
  164.4 2.3 fusion.117
  167.3 2.2 convert_bitcast_fusion.2
  169.5 1.9 copy.161
  172.4 1.3 subtract_reduce_fusion.2
  176.1 2.3 fusion.117
  179.0 2.2 convert_bitcast_fusion.2
  181.2 1.9 copy.161
  184.1 1.3 subtract_reduce_fusion.2
  186.6 1.2 stack.155
  187.8 2.3 fusion.117
  190.7 2.2 convert_bitcast_fusion.2
  192.9 1.9 copy.161
  195.8 1.3 subtract_reduce_fusion.2
  197.9 14.3 %all-gather.2 = f32[8,2,8]{2,1,0:T(2,128)S(1)} all-gather(f32[1,2,8]{2,1,0:T(2,128)S(1)} %maximum_bitcast_fusion.9), channel_id=2, replica_groups=mesh['dom'=64,'cls'=8] {'cls'}, dimensions={0}, use_global_device_ids=true | all-gather | bytes 576 | tf_op jit(solution)/shard_map/all_gather | solution.py:156
  212.7 1.9 fusion.80
  215.9 1.6 reshape.560
  217.6 22.2 %all-to-all-start.1 = ((f32[64,1,576]{2,1,0:T(1,128)}), f32[64,1,576]{2,1,0:T(1,128)S(1)}, u32[]{:S(2)}, u32[]{:S(2)}) async-start(f32[64,1,576]{2,1,0:T(1,128)} %reshape.560), calls=%async_computation.1 | async-start | bytes 327680 | tf_op jit(solution)/shard_map/all_to_all | solution.py:166
  240.3 12.5 %all-to-all-done.1 = f32[64,1,576]{2,1,0:T(1,128)S(1)} async-done(((f32[64,1,576]{2,1,0:T(1,128)}), f32[64,1,576]{2,1,0:T(1,128)S(1)}, u32[]{:S(2)}, u32[]{:S(2)}) %all-to-all-start.1) | async-done | bytes 147488 | tf_op jit(solution)/shard_map/all_to_all | solution.py:166
  (235 shorter events, 57.5 us)
Async XLA Ops:
  0.6 50.1 %copy-start = (f32[16,23]{1,0:T(8,128)S(1)}, f32[16,23]{1,0:T(8,128)}, u32[]{:S(2)}) copy-start(f32[16,23]{1,0:T(8,128)} %param.10) | copy-start | bytes 4420
  2.3 50.3 %all-to-all-start = ((f32[64,1,768]{2,1,0:T(1,128)}), f32[64,1,768]{2,1,0:T(1,128)S(1)}, u32[]{:S(2)}, u32[]{:S(2)}) async-start(f32[64,1,768]{2,1,0:T(1,128)} %reshape.558), calls=%async_computation | async-start | bytes 393216 | tf_op jit(solution)/shard_map/all_to_all | solution.py:137
  23.4 27.2 %copy-start.1 = (f32[23]{0:T(128)S(1)}, f32[23]{0:T(128)}, u32[]{:S(2)}) copy-start(f32[23]{0:T(128)} %param.11) | copy-start | bytes 280
  217.6 35.2 %all-to-all-start.1 = ((f32[64,1,576]{2,1,0:T(1,128)}), f32[64,1,576]{2,1,0:T(1,128)S(1)}, u32[]{:S(2)}, u32[]{:S(2)}) async-start(f32[64,1,576]{2,1,0:T(1,128)} %reshape.560), calls=%async_computation.1 | async-start | bytes 327680 | tf_op jit(solution)/shard_map/all_to_all | solution.py:166

commit v2 on v1

--- a/solution.py
+++ b/solution.py
@@ -93,29 +93,35 @@
     return (contrast_transfer, noise_deviation)
 
 
-def class_step(abstract_value, output_value, ref_band, offset, tabs):
+def class_step(abstract_value, output_value, ref_bands, offset, tabs):
     tab_c, tab_d, tab_e, tab_f = tabs
+    classes = ref_bands.shape[0]
     count = abstract_value.shape[0]
-    real_ref = ref_band[0]
-    imag_ref = ref_band[1]
-    breal = abstract_value[:, :, 0] * real_ref + abstract_value[:, :, 1] * imag_ref
-    bimag = abstract_value[:, :, 1] * real_ref - abstract_value[:, :, 0] * imag_ref
-    bmat = jnp.stack([breal, bimag], axis=2).astype(jnp.bfloat16).reshape(count, ROT, 2, BAND, BAND)
-    edge = product("nrcab,cbdx->nradx", bmat, tab_c).astype(jnp.bfloat16)
-    score = product("nradx,day->nyrx", edge, tab_d) - offset[:, None, None, None]
-    peak = jnp.max(score, axis=(1, 2, 3))
-    expo = jnp.exp(score - peak[:, None, None, None])
-    total = jnp.sum(expo, axis=(1, 2, 3))
-    uhalf = product("nyrx,xdb->nrydb", expo.astype(jnp.bfloat16), tab_e).astype(jnp.bfloat16)
-    what = product("nrydb,ydca->nrcab", uhalf, tab_f).astype(jnp.bfloat16)
-    what = what.reshape(count, ROT, 2, BAND * BAND).astype(jnp.float32)
+    real_ref = ref_bands[:, None, None, 0]
+    imag_ref = ref_bands[:, None, None, 1]
+    breal = abstract_value[None, :, :, 0] * real_ref + abstract_value[None, :, :, 1] * imag_ref
+    bimag = abstract_value[None, :, :, 1] * real_ref - abstract_value[None, :, :, 0] * imag_ref
+    bmat = jnp.stack([breal, bimag], axis=3).astype(jnp.bfloat16)
+    bmat = bmat.reshape(classes, count, ROT, 2, BAND, BAND)
+    edge = product("knrcab,cbdx->knradx", bmat, tab_c).astype(jnp.bfloat16)
+    score = product("knradx,day->knyrx", edge, tab_d) - offset[:, :, None, None, None]
+    peak = jnp.max(score, axis=(2, 3, 4))
+    expo = jnp.exp(score - peak[:, :, None, None, None])
+    total = jnp.sum(expo, axis=(2, 3, 4))
+    uhalf = product("knyrx,xdb->knrydb", expo.astype(jnp.bfloat16), tab_e).astype(jnp.bfloat16)
+    what = product("knrydb,ydca->knrcab", uhalf, tab_f).astype(jnp.bfloat16)
+    what = what.reshape(classes, count, ROT, 2, BAND * BAND).astype(jnp.float32)
     preal = jnp.sum(
-        output_value[:, :, 0] * what[:, :, 0] - output_value[:, :, 1] * what[:, :, 1], axis=1
+        output_value[None, :, :, 0] * what[:, :, :, 0]
+        - output_value[None, :, :, 1] * what[:, :, :, 1],
+        axis=2,
     )
     pimag = jnp.sum(
-        output_value[:, :, 0] * what[:, :, 1] + output_value[:, :, 1] * what[:, :, 0], axis=1
+        output_value[None, :, :, 0] * what[:, :, :, 1]
+        + output_value[None, :, :, 1] * what[:, :, :, 0],
+        axis=2,
     )
-    return (peak, total, jnp.stack([preal, pimag], axis=1))
+    return (peak, total, jnp.stack([preal, pimag], axis=2))
 
 
 def shards(particles, group_ids, references, ctf_profile, noise_power):
@@ -147,10 +153,7 @@
     offset = 0.5 * jnp.dot(
         contrast_transfer * contrast_transfer / noise_deviation[None, :], power.T, precision=HIGHEST
     )
-    peaks, totals, projs = lax.map(
-        lambda item: class_step(abstract_value, output_value, item[0], item[1], tabs),
-        (rbands, offset.T),
-    )
+    peaks, totals, projs = class_step(abstract_value, output_value, rbands, offset.T, tabs)
     local_top = jnp.max(peaks, axis=0)
     local_mass = jnp.sum(jnp.exp(peaks - local_top[None, :]) * totals, axis=0)
     summary = lax.all_gather(jnp.stack([local_top, local_mass]), "cls", axis=0)

time: 257 us -> 217 us (0.84)
  local copies, waits for them, and re-layouts: 72.5 us -> 36.4 us
  matrix products: 59.5 us -> 52 us
  other arithmetic: 30.5 us -> 34.9 us
    another operation x48 -> x0, local copies, waits for them, and re-layouts: 18.8 us -> none  [the longest x24 18.2 us: class_step(): jnp.stack([breal, bimag], axis=2).astype(jnp.bfloat16)]
    convert_element_type x24 -> x1, local copies, waits for them, and re-layouts: 34.5 us -> 19.9 us  [class_step(): what = what.reshape(classes, count, ROT, 2, BAND * BAND).astype(jnp.float32)]
    reduce_sum x24 -> x2, other arithmetic: 22.3 us -> 11.2 us  [the longest x1 5.99 us: class_step(): total = jnp.sum(expo, axis=(2, 3, 4))]
    reduce_max x1, other arithmetic: 0.02 us -> 11.1 us  [shards(): local_top = jnp.max(peaks, axis=0)]
    dynamic_update_slice x36 -> x0, local copies, waits for them, and re-layouts: 8.4 us -> none  [shards(): lax.map(lambda item: class_step(abstract_value, output_value, item[0], it...]
    dot_general x25 -> x3, matrix products: 54.3 us -> 46.7 us  [product(): return jnp.einsum(form, left, right, preferred_element_type=jnp.float32)]
    another operation x15 -> x1, other arithmetic: 0.84 us -> 6.34 us
    unnamed x19 -> x27, local copies, waits for them, and re-layouts: 5.45 us -> 9.75 us
  transfers between devices with their start and end apart: 2 -> 2, of which waited for: 1 -> 1; matrix products, arithmetic and copies ran while one was open for 3% -> 5% of each run, Pallas kernels for 0% -> 0%
where the time goes in v2:
time: 217 us; the launch traced here: 216 us
  matrix products  52 us (24%)
  starting transfers between devices  39.8 us (18%)
  blocking collectives  38.8 us (18%)
  local copies, waits for them, and re-layouts  36.4 us (17%)
  other arithmetic  34.9 us (16%)
  waiting for transfers between devices  12.5 us (6%)
    dot_general x3, matrix products, product(): return jnp.einsum(form, left, right, preferred_element_type=jnp.float32)  46.7 us
    all_gather x1, blocking collectives, shards(): gathered = lax.all_gather(payload, 'cls', axis=0, tiled=True)  24.3 us
    all_to_all x1, starting transfers between devices, shards(): owned = jnp.sum(lax.all_to_all(parts, 'dom', 0, 0, tiled=True), axis=0)  22.1 us
    convert_element_type x1, local copies, waits for them, and re-layouts, class_step(): what = what.reshape(classes, count, ROT, 2, BAND * BAND).astype(jnp.float32)  19.9 us
    all_to_all x1, starting transfers between devices, shards(): pieces = lax.all_to_all(spread, 'dom', 0, 0, tiled=True)  17.6 us
    all_gather x1, blocking collectives, shards(): summary = lax.all_gather(jnp.stack([local_top, local_mass]), 'cls', axis=0)  14.5 us
    all_to_all x1, waiting for transfers between devices, shards(): owned = jnp.sum(lax.all_to_all(parts, 'dom', 0, 0, tiled=True), axis=0)  12.5 us
    reduce_max x1, other arithmetic, shards(): local_top = jnp.max(peaks, axis=0)  11.1 us
  transfers between devices with their start and end apart: 2, of which 1 were waited for; matrix products, arithmetic and copies ran while one was open for 5% of the time, Pallas kernels for 0%

profile of v2, /device:TPU:1, one launch (start us, length us, event | category | flops | bytes accessed | tf_op | source)
XLA Modules:
  0.0 216.1 jit_solution(14800951419204630193)
XLA Ops:
  0.6 0.7 broadcast_in_dim.5
  1.4 0.9 reshape.591
  2.3 17.6 %all-to-all-start = ((f32[64,1,768]{2,1,0:T(1,128)}), f32[64,1,768]{2,1,0:T(1,128)S(1)}, u32[]{:S(2)}, u32[]{:S(2)}) async-start(f32[64,1,768]{2,1,0:T(1,128)} %reshape.591), calls=%async_computation | async-start | bytes 393216 | tf_op jit(solution)/shard_map/all_to_all | solution.py:143
  20.0 0.1 fusion.82
  20.1 0.1 fusion.93
  20.3 0.1 fusion.92
  20.4 0.8 rev.22
  21.2 0.8 copy.71
  22.1 0.1 rev.25
  22.2 0.8 rev.23
  23.0 0.2 sine_convert_fusion
  23.2 0.2 fusion.87
  23.4 0.7 constant_dynamic-update-slice_fusion.7
  24.7 0.1 copy.73
  24.8 0.1 copy.72
  25.0 0.4 fusion.24
  25.5 0.1 reshape_reshape.3
  25.7 24.3 %all-gather.1 = bf16[8,1,16512]{2,1,0:T(2,128)(2,1)S(1)} all-gather(bf16[1,1,16512]{2,1,0:T(2,128)(2,1)S(1)} %pad_bitcast_fusion), channel_id=1, replica_groups=mesh['dom'=64,'cls'=8] {'cls'}, dimensions={0}, use_global_device_ids=true | all-gather | bytes 297216 | tf_op jit(solution)/shard_map/all_gather | solution.py:138
  50.0 0.1 convert_reduce_fusion.1
  50.3 0.1 convert_reduce_fusion
  50.4 0.8 fusion.31
  51.2 0.2 fusion.90
  51.4 0.2 broadcast_divide_fusion
  51.6 0.1 convert_multiply_fusion.1
  51.8 0.6 maximum_bitcast_fusion.15
  52.4 0.2 copy.76
  52.6 0.2 copy.85
  52.8 0.2 copy.77
  52.9 0.2 copy.81
  53.1 0.3 mul.414
  53.4 0.3 mul.409
  53.8 0.7 cosine_convert_fusion.1
  54.5 0.5 broadcast.686
  55.1 1.1 reduce.7
  56.2 0.1 reshape.592
  56.3 1.3 convolution_bitcast_fusion.1
  57.6 1.1 convolution_bitcast_fusion
  58.7 0.2 reshape.583
  58.9 0.1 mul.411
  59.1 0.1 mul.416
  59.2 0.8 convolution_multiply_fusion
  60.1 6.3 %add_convert_fusion = (bf16[12,8,8,1,32,32]{5,4,3,2,1,0:T(8,128)(2,1)}, bf16[12,8,8,1,32,32]{5,4,3,2,1,0:T(8,128)(2,1)}) fusion(f32[12,32,32]{2,1,0:T(8,128)S(1)} %mul.416, f32[8,8,32,32]{3,2,1,0:T(8,128)S(1)} %mul.414, f32[12,32,32]{2,1,0:T(8,128)S(1)} %mul.411, f32[8,8,32,32]{3,2,1,0:T(8,128)S(1)} %mul.409), kind=kLoop, calls=%fused_computation.23 | loop fusion | flops 6291456 | bytes 3768320 | tf_op jit(solution)/shard_map/convert.4
  66.4 16.8 %bitcast_reduce_fusion = (f32[12,8]{1,0:T(8,128)S(1)}, f32[64,12,8,8,64,1]{4,0,5,3,2,1:T(8,128)}) fusion(f32[12,8]{1,0:T(8,128)S(1)} %copy.83, bf16[12,8,8,1,32,32]{5,4,3,2,1,0:T(8,128)(2,1)} %get-tuple-element.9, bf16[12,8,8,1,32,32]{5,4,3,2,1,0:T(8,128)(2,1)} %get-tuple-element.8, bf16[1,32,2,64]{3,1,0,2:T(8,128)(2,1)S(1)} %copy-done.3, ...), kind=kOutput, calls=%fused_computation.2 | convolution fusion | flops 821084032 | bytes 15753984 | tf_op jit(solution)/shard_map/knradx,day->knyrx/dot_general | solution.py:49
  83.3 11.1 %fusion.1 = f32[8]{0:T(128)S(1)} fusion(f32[64,12,8,8,64,1]{4,0,5,3,2,1:T(8,128)} %get-tuple-element.36, f32[12,8]{1,0:T(8,128)S(1)} %copy.83), kind=kLoop, calls=%fused_computation.7 | loop fusion | flops 6291448 | bytes 12583328 | tf_op jit(solution)/shard_map/reduce_max | solution.py:157
  94.4 4.3 %copy-done.2 = f32[64,12,8,8,64,1]{4,0,5,3,2,1:T(8,128)S(1)} copy-done((f32[64,12,8,8,64,1]{4,0,5,3,2,1:T(8,128)S(1)}, f32[64,12,8,8,64,1]{4,0,5,3,2,1:T(8,128)}, u32[]{:S(2)}) %copy-start.2) | copy-done | bytes 12582936
  98.7 6.0 %fusion.2 = f32[12,8]{1,0:T(8,128)S(1)} fusion(f32[64,12,8,8,64,1]{4,0,5,3,2,1:T(8,128)S(1)} %copy-done.2, f32[12,8]{1,0:T(8,128)S(1)} %get-tuple-element.35, f32[12,8]{1,0:T(8,128)S(1)} %copy.83), kind=kLoop, calls=%fused_computation.8 | loop fusion | flops 9437088 | bytes 12584064 | tf_op jit(solution)/shard_map/reduce_sum | solution.py:110
  104.7 14.5 %all-gather.2 = f32[8,2,8]{2,1,0:T(2,128)S(1)} all-gather(f32[1,2,8]{2,1,0:T(2,128)S(1)} %maximum_bitcast_fusion.17), channel_id=2, replica_groups=mesh['dom'=64,'cls'=8] {'cls'}, dimensions={0}, use_global_device_ids=true | all-gather | bytes 576 | tf_op jit(solution)/shard_map/all_gather | solution.py:159
  119.3 0.2 fusion.50
  119.5 29.4 %convert_bitcast_fusion = f32[12,8,8,2,32,32]{5,4,2,1,0,3:T(8,128)} fusion(f32[64,12,8,8,64,1]{4,0,5,3,2,1:T(8,128)} %get-tuple-element.36, f32[12,8]{1,0:T(8,128)S(1)} %get-tuple-element.35, f32[12,8]{1,0:T(8,128)S(1)} %copy.83, bf16[64,1,32]{0,2,1:T(8,128)(2,1)S(1)} %get-tuple-element.26, bf16[64,1,32]{0,2,1:T(8,128)(2,1)S(1)} %get-tuple-element.28, ...), kind=kOutput, calls=%fused_computation.6 | convolution fusion | flops 821059584 | bytes 18899712 | tf_op jit(solution)/shard_map/knrydb,ydca->knrcab/dot_general | solution.py:49
  149.0 19.9 %reshape.552 = f32[12,8,8,2,1024]{4,2,1,0,3:T(8,128)} reshape(f32[12,8,8,2,32,32]{5,4,2,1,0,3:T(8,128)} %convert_bitcast_fusion) | data formatting | bytes 12582912 | tf_op jit(solution)/shard_map/convert_element_type | solution.py:113
  168.9 5.2 %subtract_reduce_fusion = (f32[12,8,1024]{2,1,0:T(8,128)S(1)}, f32[12,8,1024]{2,1,0:T(8,128)S(1)}) fusion(f32[12,8,8,2,1024]{4,2,1,0,3:T(8,128)} %reshape.552, f32[8,8,1024]{2,1,0:T(8,128)S(1)} %copy.85, f32[8,8,1024]{2,1,0:T(8,128)S(1)} %copy.76), kind=kLoop, calls=%fused_computation.27 | loop fusion | flops 6094848 | bytes 7602176 | tf_op jit(solution)/shard_map/reduce_sum | solution.py:114
  174.1 0.8 fusion.25
  174.9 0.2 concatenate.15
  175.1 0.3 concatenate.14
  175.4 0.1 maximum_bitcast_fusion.6
  175.5 0.8 copy.159
  176.3 1.6 reshape.593
  178.0 22.1 %all-to-all-start.1 = ((f32[64,1,576]{2,1,0:T(1,128)}), f32[64,1,576]{2,1,0:T(1,128)S(1)}, u32[]{:S(2)}, u32[]{:S(2)}) async-start(f32[64,1,576]{2,1,0:T(1,128)} %reshape.593), calls=%async_computation.1 | async-start | bytes 327680 | tf_op jit(solution)/shard_map/all_to_all | solution.py:169
  200.1 0.5 log_add_fusion
  200.6 12.5 %all-to-all-done.1 = f32[64,1,576]{2,1,0:T(1,128)S(1)} async-done(((f32[64,1,576]{2,1,0:T(1,128)}), f32[64,1,576]{2,1,0:T(1,128)S(1)}, u32[]{:S(2)}, u32[]{:S(2)}) %all-to-all-start.1) | async-done | bytes 147488 | tf_op jit(solution)/shard_map/all_to_all | solution.py:169
  213.1 1.0 reduce.8
  214.1 1.0 reshape.594
  215.2 0.3 bitcast_reduce_fusion.1
  215.5 0.6 slice_divide_fusion
  (45 shorter events, 0.9 us)
Async XLA Ops:
  0.6 50.6 %copy-start = (f32[16,23]{1,0:T(8,128)S(1)}, f32[16,23]{1,0:T(8,128)}, u32[]{:S(2)}) copy-start(f32[16,23]{1,0:T(8,128)} %param.8) | copy-start | bytes 4420
  2.3 52.2 %all-to-all-start = ((f32[64,1,768]{2,1,0:T(1,128)}), f32[64,1,768]{2,1,0:T(1,128)S(1)}, u32[]{:S(2)}, u32[]{:S(2)}) async-start(f32[64,1,768]{2,1,0:T(1,128)} %reshape.591), calls=%async_computation | async-start | bytes 393216 | tf_op jit(solution)/shard_map/all_to_all | solution.py:143
  51.2 0.6 copy-start.5
  56.3 10.1 %copy-start.3 = (bf16[1,32,2,64]{3,1,0,2:T(8,128)(2,1)S(1)}, bf16[1,32,2,64]{3,1,0,2:T(8,128)(2,1)}, u32[]{:S(2)}) copy-start(bf16[1,32,2,64]{3,1,0,2:T(8,128)(2,1)} %get-tuple-element.25) | copy-start | bytes 24580
  56.3 10.1 %copy-start.4 = (bf16[1,32,64]{2,1,0:T(8,128)(2,1)S(1)}, bf16[1,32,64]{2,1,0:T(8,128)(2,1)}, u32[]{:S(2)}) copy-start(bf16[1,32,64]{2,1,0:T(8,128)(2,1)} %cosine_convert_fusion.1) | copy-start | bytes 12292
  83.3 15.4 %copy-start.2 = (f32[64,12,8,8,64,1]{4,0,5,3,2,1:T(8,128)S(1)}, f32[64,12,8,8,64,1]{4,0,5,3,2,1:T(8,128)}, u32[]{:S(2)}) copy-start(f32[64,12,8,8,64,1]{4,0,5,3,2,1:T(8,128)} %get-tuple-element.36) | copy-start | bytes 37748740
  149.0 67.1 %copy-start.1 = (f32[16,23]{1,0:T(8,128)S(1)}, f32[16,23]{1,0:T(8,128)}, u32[]{:S(2)}) copy-start(f32[16,23]{1,0:T(8,128)} %param.8) | copy-start | bytes 4420
  178.0 35.1 %all-to-all-start.1 = ((f32[64,1,576]{2,1,0:T(1,128)}), f32[64,1,576]{2,1,0:T(1,128)S(1)}, u32[]{:S(2)}, u32[]{:S(2)}) async-start(f32[64,1,576]{2,1,0:T(1,128)} %reshape.593), calls=%async_computation.1 | async-start | bytes 327680 | tf_op jit(solution)/shard_map/all_to_all | solution.py:169

commit v3 on v2

--- a/solution.py
+++ b/solution.py
@@ -110,18 +110,18 @@
     total = jnp.sum(expo, axis=(2, 3, 4))
     uhalf = product("knyrx,xdb->knrydb", expo.astype(jnp.bfloat16), tab_e).astype(jnp.bfloat16)
     what = product("knrydb,ydca->knrcab", uhalf, tab_f).astype(jnp.bfloat16)
-    what = what.reshape(classes, count, ROT, 2, BAND * BAND).astype(jnp.float32)
+    what = what.astype(jnp.float32)
+    yval = output_value.reshape(count, ROT, 2, BAND, BAND)
     preal = jnp.sum(
-        output_value[None, :, :, 0] * what[:, :, :, 0]
-        - output_value[None, :, :, 1] * what[:, :, :, 1],
+        yval[None, :, :, 0] * what[:, :, :, 0] - yval[None, :, :, 1] * what[:, :, :, 1],
         axis=2,
     )
     pimag = jnp.sum(
-        output_value[None, :, :, 0] * what[:, :, :, 1]
-        + output_value[None, :, :, 1] * what[:, :, :, 0],
+        yval[None, :, :, 0] * what[:, :, :, 1] + yval[None, :, :, 1] * what[:, :, :, 0],
         axis=2,
     )
-    return (peak, total, jnp.stack([preal, pimag], axis=2))
+    proj = jnp.stack([preal, pimag], axis=2)
+    return (peak, total, proj.reshape(classes, count, 2, BAND * BAND))
 
 
 def shards(particles, group_ids, references, ctf_profile, noise_power):
@@ -135,7 +135,10 @@
     width = ROT * 2 * BAND * BAND
     label_row = jnp.broadcast_to(group_ids.astype(jnp.bfloat16)[:, None], (count, 128))
     payload = jnp.concatenate([own_bands.reshape(count, width), label_row], axis=1)
-    gathered = lax.all_gather(payload, "cls", axis=0, tiled=True)
+    peers = lax.psum(1, "cls")
+    gathered = lax.all_to_all(
+        jnp.broadcast_to(payload, (peers,) + payload.shape[1:]), "cls", 0, 0, tiled=True
+    )
     fourier_input = gathered[:, :width].reshape(-1, ROT, 2, BAND * BAND)
     block_labels = gathered[:, width].astype(jnp.int32)
     rows = lax.psum(1, "dom")
@@ -156,7 +159,10 @@
     peaks, totals, projs = class_step(abstract_value, output_value, rbands, offset.T, tabs)
     local_top = jnp.max(peaks, axis=0)
     local_mass = jnp.sum(jnp.exp(peaks - local_top[None, :]) * totals, axis=0)
-    summary = lax.all_gather(jnp.stack([local_top, local_mass]), "cls", axis=0)
+    own_summary = jnp.stack([local_top, local_mass])
+    summary = lax.all_to_all(
+        jnp.broadcast_to(own_summary[None], (peers,) + own_summary.shape), "cls", 0, 0, tiled=True
+    )
     top = jnp.max(summary[:, 0], axis=0)
     mass = jnp.sum(jnp.exp(summary[:, 0] - top[None, :]) * summary[:, 1], axis=0)
     log_evidence = top + jnp.log(mass)

time: 217 us -> 181 us (0.83)
  blocking collectives: 38.8 us -> 0 us
  other arithmetic: 34.9 us -> 44.3 us
  local copies, waits for them, and re-layouts: 36.4 us -> 27.4 us
  waiting for transfers between devices: 12.5 us -> 14.7 us
    all_gather x2 -> x0, blocking collectives: 38.8 us -> none  [the longest x1 24.3 us: shards(): gathered = lax.all_gather(payload, 'cls', axis=0, tiled=True)]
    convert_element_type x1, local copies, waits for them, and re-layouts: 19.9 us -> 0.68 us  [shards(): complete_input = fourier_input.astype(jnp.float32)]
    all_to_all x1, starting transfers between devices: 22.1 us -> 11.3 us  [shards(): owned = jnp.sum(lax.all_to_all(parts, 'dom', 0, 0, tiled=True), axis=0)]
    all_to_all x0 -> x2, starting transfers between devices: none -> 10.1 us  [the longest x1 5.14 us: shards(): lax.all_to_all(jnp.broadcast_to(own_summary[None], (peers,) + own_summary...]
    reduce_sum x1, other arithmetic: 5.18 us -> 11.2 us  [class_step(): jnp.sum(yval[None, :, :, 0] * what[:, :, :, 0] - yval[None, :, :, 1] * wh...]
    broadcast_in_dim x0 -> x1, other arithmetic: none -> 2.26 us  [shards(): jnp.broadcast_to(payload, (peers,) + payload.shape[1:])]
    all_to_all x1, waiting for transfers between devices: 0.01 us -> 2.25 us  [shards(): pieces = lax.all_to_all(spread, 'dom', 0, 0, tiled=True)]
    another operation x1 -> x2, other arithmetic: 6.34 us -> 7.67 us
  transfers between devices with their start and end apart: 2 -> 4, of which waited for: 1 -> 2; matrix products, arithmetic and copies ran while one was open for 5% -> 34% of each run, Pallas kernels for 0% -> 0%
where the time goes in v3:
time: 181 us; the launch traced here: 180 us
  matrix products  52.9 us (29%)
  other arithmetic  44.3 us (24%)
  starting transfers between devices  39 us (22%)
  local copies, waits for them, and re-layouts  27.4 us (15%)
  waiting for transfers between devices  14.7 us (8%)
    dot_general x3, matrix products, product(): return jnp.einsum(form, left, right, preferred_element_type=jnp.float32)  46.7 us
    all_to_all x1, starting transfers between devices, shards(): pieces = lax.all_to_all(spread, 'dom', 0, 0, tiled=True)  17.6 us
    all_to_all x1, waiting for transfers between devices, shards(): owned = jnp.sum(lax.all_to_all(parts, 'dom', 0, 0, tiled=True), axis=0)  12.5 us
    all_to_all x1, starting transfers between devices, shards(): owned = jnp.sum(lax.all_to_all(parts, 'dom', 0, 0, tiled=True), axis=0)  11.3 us
    reduce_sum x1, other arithmetic, class_step(): jnp.sum(yval[None, :, :, 0] * what[:, :, :, 0] - yval[None, :, :, 1] * wh...  11.2 us
    reduce_max x1, other arithmetic, shards(): local_top = jnp.max(peaks, axis=0)  11.1 us
    unnamed x26, local copies, waits for them, and re-layouts  10.9 us
    another operation x1, other arithmetic  7.66 us
  transfers between devices with their start and end apart: 4, of which 2 were waited for; matrix products, arithmetic and copies ran while one was open for 34% of the time, Pallas kernels for 0%

profile of v3, /device:TPU:1, one launch (start us, length us, event | category | flops | bytes accessed | tf_op | source)
XLA Modules:
  0.0 180.0 jit_solution(16734529071746660931)
XLA Ops:
  0.6 0.7 broadcast_in_dim.10
  1.4 0.9 reshape.603
  2.3 17.6 %all-to-all-start.1 = ((f32[64,1,768]{2,1,0:T(1,128)}), f32[64,1,768]{2,1,0:T(1,128)S(1)}, u32[]{:S(2)}, u32[]{:S(2)}) async-start(f32[64,1,768]{2,1,0:T(1,128)} %reshape.603), calls=%async_computation.1 | async-start | bytes 393216 | tf_op jit(solution)/shard_map/all_to_all | solution.py:146
  20.0 0.8 copy.90
  20.8 0.8 rev.22
  21.6 0.7 constant_dynamic-update-slice_fusion.7
  22.3 0.8 rev.23
  23.3 0.2 fusion.87
  23.4 0.2 sine_convert_fusion
  23.6 0.2 fusion.93
  24.6 0.4 fusion.24
  25.9 0.2 pad_reduce_fusion
  26.1 0.3 broadcast_in_dim.9
  26.4 0.5 broadcast.692
  26.9 2.3 %reduce.9 = bf16[8,16512]{1,0:T(8,128)(2,1)S(1)} reduce(bf16[8,1,16512]{2,1,0:T(2,128)(2,1)S(1)} %broadcast_in_dim.9, bf16[]{:T(256)} %broadcast.692), dimensions={1}, to_apply=%broadcast_in_dim.9.reduce_sub_computation | reduce | bytes 528386 | tf_op jit(solution)/shard_map/broadcast_in_dim | solution.py:140
  29.1 0.9 reshape.601
  30.2 0.8 fusion.31
  31.0 2.3 %all-to-all-done.1 = f32[64,1,768]{2,1,0:T(1,128)S(1)} async-done(((f32[64,1,768]{2,1,0:T(1,128)}), f32[64,1,768]{2,1,0:T(1,128)S(1)}, u32[]{:S(2)}, u32[]{:S(2)}) %all-to-all-start.1) | async-done | bytes 196640 | tf_op jit(solution)/shard_map/all_to_all | solution.py:146
  33.3 4.9 %all-to-all-start = ((bf16[8,2,8256]{2,1,0:T(2,128)(2,1)}), bf16[8,2,8256]{2,1,0:T(2,128)(2,1)S(1)}, u32[]{:S(2)}, u32[]{:S(2)}) async-start(bf16[8,2,8256]{2,1,0:T(2,128)(2,1)} %reshape.601), calls=%async_computation | async-start | bytes 532480 | tf_op jit(solution)/shard_map/all_to_all | solution.py:139
  38.2 0.6 broadcast.693
  38.8 1.1 reduce.10
  40.1 1.3 convolution_bitcast_fusion.1
  41.4 1.1 convolution_bitcast_fusion
  42.5 0.2 reshape.592
  42.7 0.8 mul.415
  43.4 0.8 mul.420
  44.2 0.7 fusion.38
  44.9 0.3 reshape.602
  45.5 0.7 reshape.565
  46.2 0.2 fusion.90
  46.3 0.2 broadcast_divide_fusion
  46.6 0.7 fusion.104
  47.3 0.2 copy.96
  47.5 0.3 mul.413
  47.8 1.1 copy.100
  48.9 1.3 mul.418
  50.3 1.0 convolution_multiply_fusion
  51.4 7.7 %add_convert_fusion = (bf16[12,8,8,1,32,32]{5,4,3,2,1,0:T(8,128)(2,1)}, bf16[12,8,8,1,32,32]{5,4,3,2,1,0:T(8,128)(2,1)}) fusion(f32[12,32,32]{2,1,0:T(8,128)} %mul.420, f32[8,8,32,32]{3,2,1,0:T(8,128)} %mul.418, f32[12,32,32]{2,1,0:T(8,128)} %mul.415, f32[8,8,32,32]{3,2,1,0:T(8,128)S(1)} %mul.413), kind=kLoop, calls=%fused_computation.27 | loop fusion | flops 6291456 | bytes 3768320 | tf_op jit(solution)/shard_map/convert.4
  59.0 16.8 %bitcast_reduce_fusion = (f32[12,8]{1,0:T(8,128)S(1)}, f32[64,12,8,8,64,1]{4,0,5,3,2,1:T(8,128)}) fusion(f32[12,8]{1,0:T(8,128)S(1)} %copy.102, bf16[12,8,8,1,32,32]{5,4,3,2,1,0:T(8,128)(2,1)} %get-tuple-element.7, bf16[12,8,8,1,32,32]{5,4,3,2,1,0:T(8,128)(2,1)} %get-tuple-element.6, bf16[1,32,2,64]{3,1,0,2:T(8,128)(2,1)S(1)} %get-tuple-element.21, ...), kind=kOutput, calls=%fused_computation.2 | convolution fusion | flops 821084032 | bytes 15753984 | tf_op jit(solution)/shard_map/knradx,day->knyrx/dot_general | solution.py:49
  75.9 11.1 %fusion.1 = f32[8]{0:T(128)S(1)} fusion(f32[64,12,8,8,64,1]{4,0,5,3,2,1:T(8,128)} %get-tuple-element.32, f32[12,8]{1,0:T(8,128)S(1)} %copy.102), kind=kLoop, calls=%fused_computation.7 | loop fusion | flops 6291448 | bytes 12583328 | tf_op jit(solution)/shard_map/reduce_max | solution.py:160
  87.0 4.3 %copy-done.2 = f32[64,12,8,8,64,1]{4,0,5,3,2,1:T(8,128)S(1)} copy-done((f32[64,12,8,8,64,1]{4,0,5,3,2,1:T(8,128)S(1)}, f32[64,12,8,8,64,1]{4,0,5,3,2,1:T(8,128)}, u32[]{:S(2)}) %copy-start.2) | copy-done | bytes 12582936
  91.3 6.0 %fusion.2 = f32[12,8]{1,0:T(8,128)S(1)} fusion(f32[64,12,8,8,64,1]{4,0,5,3,2,1:T(8,128)S(1)} %copy-done.2, f32[12,8]{1,0:T(8,128)S(1)} %get-tuple-element.31, f32[12,8]{1,0:T(8,128)S(1)} %copy.102), kind=kLoop, calls=%fused_computation.8 | loop fusion | flops 9437088 | bytes 12584064 | tf_op jit(solution)/shard_map/reduce_sum | solution.py:110
  97.3 0.6 broadcast_in_dim.11
  97.9 5.1 %all-to-all-start.2 = ((f32[8,2,8]{2,1,0:T(2,128)}), f32[8,2,8]{2,1,0:T(2,128)}, u32[]{:S(2)}, u32[]{:S(2)}) async-start(f32[8,2,8]{2,1,0:T(2,128)} %broadcast_in_dim.11), calls=%async_computation.2 | async-start | bytes 16384 | tf_op jit(solution)/shard_map/all_to_all | solution.py:163
  103.0 0.2 copy_multiply_fusion
  103.3 1.5 slice_bitcast_fusion.3
  104.8 29.4 %convert_bitcast_fusion = f32[12,8,8,2,32,32]{5,4,2,1,0,3:T(8,128)} fusion(f32[64,12,8,8,64,1]{4,0,5,3,2,1:T(8,128)} %get-tuple-element.32, f32[12,8]{1,0:T(8,128)S(1)} %get-tuple-element.31, f32[12,8]{1,0:T(8,128)S(1)} %copy.102, bf16[64,1,32]{0,2,1:T(8,128)(2,1)S(1)} %get-tuple-element.22, bf16[64,1,32]{0,2,1:T(8,128)(2,1)S(1)} %get-tuple-element.24, ...), kind=kOutput, calls=%fused_computation.6 | convolution fusion | flops 821059584 | bytes 18899712 | tf_op jit(solution)/shard_map/knrydb,ydca->knrcab/dot_general | solution.py:49
  134.3 11.2 %subtract_reduce_fusion = (f32[12,8,32,32]{3,2,1,0:T(8,128)S(1)}, f32[12,8,32,32]{3,2,1,0:T(8,128)S(1)}) fusion(f32[12,8,8,2,32,32]{5,4,2,1,0,3:T(8,128)} %convert_bitcast_fusion, f32[8,8,32,32]{3,2,1,0:T(8,128)} %get-tuple-element.9, f32[8,8,32,32]{3,2,1,0:T(8,128)} %get-tuple-element.8), kind=kLoop, calls=%fused_computation.22 | loop fusion | flops 6094848 | bytes 7602176 | tf_op jit(solution)/shard_map/reduce_sum | solution.py:115
  145.5 0.7 stack.144
  146.2 0.7 stack.145
  146.9 0.8 fusion.106
  147.8 1.0 fusion.50
  148.8 0.8 fusion.25
  149.6 0.3 concatenate.18
  149.9 0.2 concatenate.19
  150.2 0.8 copy.178
  151.0 1.6 reshape.605
  152.6 11.3 %all-to-all-start.3 = ((f32[64,1,576]{2,1,0:T(1,128)}), f32[64,1,576]{2,1,0:T(1,128)S(1)}, u32[]{:S(2)}, u32[]{:S(2)}) async-start(f32[64,1,576]{2,1,0:T(1,128)} %reshape.605), calls=%async_computation.3 | async-start | bytes 327680 | tf_op jit(solution)/shard_map/all_to_all | solution.py:175
  164.0 0.5 log_add_fusion
  164.5 12.5 %all-to-all-done.3 = f32[64,1,576]{2,1,0:T(1,128)S(1)} async-done(((f32[64,1,576]{2,1,0:T(1,128)}), f32[64,1,576]{2,1,0:T(1,128)S(1)}, u32[]{:S(2)}, u32[]{:S(2)}) %all-to-all-start.3) | async-done | bytes 147488 | tf_op jit(solution)/shard_map/all_to_all | solution.py:175
  177.0 1.1 reduce.11
  178.1 1.0 reshape.606
  179.1 0.3 bitcast_reduce_fusion.1
  179.4 0.6 slice_divide_fusion
  (53 shorter events, 2.1 us)
Async XLA Ops:
  0.6 45.5 %copy-start = (f32[16,23]{1,0:T(8,128)S(1)}, f32[16,23]{1,0:T(8,128)}, u32[]{:S(2)}) copy-start(f32[16,23]{1,0:T(8,128)} %param.8) | copy-start | bytes 4420
  2.3 31.0 %all-to-all-start.1 = ((f32[64,1,768]{2,1,0:T(1,128)}), f32[64,1,768]{2,1,0:T(1,128)S(1)}, u32[]{:S(2)}, u32[]{:S(2)}) async-start(f32[64,1,768]{2,1,0:T(1,128)} %reshape.603), calls=%async_computation.1 | async-start | bytes 393216 | tf_op jit(solution)/shard_map/all_to_all | solution.py:146
  33.3 11.6 %all-to-all-start = ((bf16[8,2,8256]{2,1,0:T(2,128)(2,1)}), bf16[8,2,8256]{2,1,0:T(2,128)(2,1)S(1)}, u32[]{:S(2)}, u32[]{:S(2)}) async-start(bf16[8,2,8256]{2,1,0:T(2,128)(2,1)} %reshape.601), calls=%async_computation | async-start | bytes 532480 | tf_op jit(solution)/shard_map/all_to_all | solution.py:139
  46.5 29.4 %copy-start.3 = (f32[8,1024]{1,0:T(8,128)}, f32[8,1024]{1,0:T(8,128)S(1)}, u32[]{:S(2)}) copy-start(f32[8,1024]{1,0:T(8,128)S(1)} %get-tuple-element.30) | copy-start | bytes 98308
  75.9 15.4 %copy-start.2 = (f32[64,12,8,8,64,1]{4,0,5,3,2,1:T(8,128)S(1)}, f32[64,12,8,8,64,1]{4,0,5,3,2,1:T(8,128)}, u32[]{:S(2)}) copy-start(f32[64,12,8,8,64,1]{4,0,5,3,2,1:T(8,128)} %get-tuple-element.32) | copy-start | bytes 37748740
  97.3 37.0 %copy-start.4 = (f32[12,8]{1,0:T(8,128)}, f32[12,8]{1,0:T(8,128)S(1)}, u32[]{:S(2)}) copy-start(f32[12,8]{1,0:T(8,128)S(1)} %fusion.2) | copy-start | bytes 1156
  97.9 49.0 %all-to-all-start.2 = ((f32[8,2,8]{2,1,0:T(2,128)}), f32[8,2,8]{2,1,0:T(2,128)}, u32[]{:S(2)}, u32[]{:S(2)}) async-start(f32[8,2,8]{2,1,0:T(2,128)} %broadcast_in_dim.11), calls=%async_computation.2 | async-start | bytes 16384 | tf_op jit(solution)/shard_map/all_to_all | solution.py:163
  134.3 45.8 %copy-start.1 = (f32[16,23]{1,0:T(8,128)S(1)}, f32[16,23]{1,0:T(8,128)}, u32[]{:S(2)}) copy-start(f32[16,23]{1,0:T(8,128)} %param.8) | copy-start | bytes 4420
  152.6 24.3 %all-to-all-start.3 = ((f32[64,1,576]{2,1,0:T(1,128)}), f32[64,1,576]{2,1,0:T(1,128)S(1)}, u32[]{:S(2)}, u32[]{:S(2)}) async-start(f32[64,1,576]{2,1,0:T(1,128)} %reshape.605), calls=%async_computation.3 | async-start | bytes 327680 | tf_op jit(solution)/shard_map/all_to_all | solution.py:175

commit v4 on v3

--- a/solution.py
+++ b/solution.py
@@ -101,26 +101,34 @@
     imag_ref = ref_bands[:, None, None, 1]
     breal = abstract_value[None, :, :, 0] * real_ref + abstract_value[None, :, :, 1] * imag_ref
     bimag = abstract_value[None, :, :, 1] * real_ref - abstract_value[None, :, :, 0] * imag_ref
-    bmat = jnp.stack([breal, bimag], axis=3).astype(jnp.bfloat16)
-    bmat = bmat.reshape(classes, count, ROT, 2, BAND, BAND)
-    edge = product("knrcab,cbdx->knradx", bmat, tab_c).astype(jnp.bfloat16)
-    score = product("knradx,day->knyrx", edge, tab_d) - offset[:, :, None, None, None]
-    peak = jnp.max(score, axis=(2, 3, 4))
-    expo = jnp.exp(score - peak[:, :, None, None, None])
-    total = jnp.sum(expo, axis=(2, 3, 4))
-    uhalf = product("knyrx,xdb->knrydb", expo.astype(jnp.bfloat16), tab_e).astype(jnp.bfloat16)
-    what = product("knrydb,ydca->knrcab", uhalf, tab_f).astype(jnp.bfloat16)
-    what = what.astype(jnp.float32)
-    yval = output_value.reshape(count, ROT, 2, BAND, BAND)
+    lead = (classes, count, ROT)
+    bmat = jnp.stack(
+        [breal.reshape(lead + (BAND, BAND)), bimag.reshape(lead + (BAND, BAND))], axis=4
+    ).astype(jnp.bfloat16)
+    edge = product("mk,kn->mn", bmat.reshape(-1, 2 * BAND), tab_c.reshape(2 * BAND, 2 * L))
+    edge = edge.astype(jnp.bfloat16).reshape(lead + (BAND, 2, L))
+    edge = jnp.transpose(edge, (0, 1, 2, 5, 4, 3)).reshape(-1, 2 * BAND)
+    score = product("mk,kn->mn", edge, tab_d.reshape(2 * BAND, L))
+    score = score.reshape(classes, count, ROT * L, L) - offset[:, :, None, None]
+    peak = jnp.max(score, axis=(2, 3))
+    expo = jnp.exp(score - peak[:, :, None, None])
+    total = jnp.sum(expo, axis=(2, 3))
+    expo_low = jnp.transpose(expo.astype(jnp.bfloat16).reshape(lead + (L, L)), (0, 1, 2, 4, 3))
+    uhalf = product("mk,kn->mn", expo_low.reshape(-1, L), tab_e.reshape(L, 2 * BAND))
+    uhalf = uhalf.astype(jnp.bfloat16).reshape(lead + (L, 2, BAND))
+    uhalf = jnp.transpose(uhalf, (0, 1, 2, 5, 3, 4)).reshape(-1, 2 * L)
+    what = product("mk,kn->mn", uhalf, tab_f.reshape(2 * L, 2 * BAND)).astype(jnp.bfloat16)
+    what = what.astype(jnp.float32).reshape(lead + (BAND, 2, BAND))
+    yval = jnp.transpose(output_value.reshape(count, ROT, 2, BAND, BAND), (0, 1, 4, 2, 3))
     preal = jnp.sum(
-        yval[None, :, :, 0] * what[:, :, :, 0] - yval[None, :, :, 1] * what[:, :, :, 1],
+        yval[None, :, :, :, 0] * what[:, :, :, :, 0] - yval[None, :, :, :, 1] * what[:, :, :, :, 1],
         axis=2,
     )
     pimag = jnp.sum(
-        yval[None, :, :, 0] * what[:, :, :, 1] + yval[None, :, :, 1] * what[:, :, :, 0],
+        yval[None, :, :, :, 0] * what[:, :, :, :, 1] + yval[None, :, :, :, 1] * what[:, :, :, :, 0],
         axis=2,
     )
-    proj = jnp.stack([preal, pimag], axis=2)
+    proj = jnp.transpose(jnp.stack([preal, pimag], axis=2), (0, 1, 2, 4, 3))
     return (peak, total, proj.reshape(classes, count, 2, BAND * BAND))
 
 

time: 181 us -> 379 us (2.09); the launches traced: 180 us -> 371 us
  local copies, waits for them, and re-layouts: 27.4 us -> 247 us
  matrix products: 52.9 us -> 28.8 us
  other arithmetic: 44.3 us -> 38.7 us
    reshape x0 -> x11, local copies, waits for them, and re-layouts: none -> 175 us  [the longest x2 58.2 us: class_step(): uhalf = uhalf.astype(jnp.bfloat16).reshape(lead + (L, 2, BAND))]
    dot_general x3 -> x5, matrix products: 46.7 us -> 23 us  [product(): return jnp.einsum(form, left, right, preferred_element_type=jnp.float32)]
    transpose x0 -> x2, local copies, waits for them, and re-layouts: none -> 17.6 us  [the longest x1 15.8 us: class_step(): edge = jnp.transpose(edge, (0, 1, 2, 5, 4, 3)).reshape(-1, 2 * BAND)]
    dot_general x0 -> x1, local copies, waits for them, and re-layouts: none -> 17.1 us  [product(): return jnp.einsum(form, left, right, preferred_element_type=jnp.float32)]
    convert_element_type x0 -> x1, local copies, waits for them, and re-layouts: none -> 14.9 us  [class_step(): bmat = jnp.stack([breal.reshape(lead + (BAND, BAND)), bimag.reshape(lead...]
    reduce_max x1, other arithmetic: 11.1 us -> 5.02 us  [shards(): local_top = jnp.max(peaks, axis=0)]
    unnamed x26 -> x24, local copies, waits for them, and re-layouts: 10.9 us -> 6.64 us
    another operation x1 -> x3, other arithmetic: 7.66 us -> 11.3 us  [the longest x1 6.14 us: class_step(): jnp.stack([breal.reshape(lead + (BAND, BAND)), bimag.reshape(lead + (BAND...]
  transfers between devices with their start and end apart: 4 -> 4, of which waited for: 2 -> 2; matrix products, arithmetic and copies ran while one was open for 34% -> 54% of each run, Pallas kernels for 0% -> 0%
where the time goes in v4:
time: 379 us; the launch traced here: 371 us
  local copies, waits for them, and re-layouts  247 us (65%)
  starting transfers between devices  40 us (11%)
  other arithmetic  38.7 us (10%)
  matrix products  28.8 us (8%)
  waiting for transfers between devices  14.4 us (4%)
    reshape x2, local copies, waits for them, and re-layouts, class_step(): uhalf = uhalf.astype(jnp.bfloat16).reshape(lead + (L, 2, BAND))  58.2 us
    reshape x2, local copies, waits for them, and re-layouts, class_step(): expo.astype(jnp.bfloat16).reshape(lead + (L, L))  36 us
    reshape x1, local copies, waits for them, and re-layouts, class_step(): uhalf = jnp.transpose(uhalf, (0, 1, 2, 5, 3, 4)).reshape(-1, 2 * L)  29.3 us
    dot_general x5, matrix products, product(): return jnp.einsum(form, left, right, preferred_element_type=jnp.float32)  23 us
    reshape x1, local copies, waits for them, and re-layouts, class_step(): edge = edge.astype(jnp.bfloat16).reshape(lead + (BAND, 2, L))  21.6 us
    all_to_all x1, starting transfers between devices, shards(): pieces = lax.all_to_all(spread, 'dom', 0, 0, tiled=True)  17.6 us
    dot_general x1, local copies, waits for them, and re-layouts, product(): return jnp.einsum(form, left, right, preferred_element_type=jnp.float32)  17.1 us
    transpose x1, local copies, waits for them, and re-layouts, class_step(): edge = jnp.transpose(edge, (0, 1, 2, 5, 4, 3)).reshape(-1, 2 * BAND)  15.8 us
  transfers between devices with their start and end apart: 4, of which 2 were waited for; matrix products, arithmetic and copies ran while one was open for 54% of the time, Pallas kernels for 0%

profile of v4, /device:TPU:1, one launch (start us, length us, event | category | flops | bytes accessed | tf_op | source)
XLA Modules:
  0.0 371.3 jit_solution(14261515307200187040)
XLA Ops:
  0.6 0.7 broadcast_in_dim.10
  1.4 0.9 reshape.668
  2.3 17.6 %all-to-all-start.1 = ((f32[64,1,768]{2,1,0:T(1,128)}), f32[64,1,768]{2,1,0:T(1,128)S(1)}, u32[]{:S(2)}, u32[]{:S(2)}) async-start(f32[64,1,768]{2,1,0:T(1,128)} %reshape.668), calls=%async_computation.1 | async-start | bytes 393216 | tf_op jit(solution)/shard_map/all_to_all | solution.py:154
  20.0 0.8 copy.210
  20.8 0.8 rev.22
  21.6 0.7 constant_dynamic-update-slice_fusion.7
  22.3 0.8 rev.23
  24.7 0.4 fusion.5
  26.4 0.5 broadcast.693
  26.9 2.3 reduce.12
  29.2 0.9 reshape.666
  30.6 0.8 fusion.10
  31.4 1.9 all-to-all-done.1
  33.3 5.1 %all-to-all-start = ((bf16[8,2,8256]{2,1,0:T(2,128)(2,1)}), bf16[8,2,8256]{2,1,0:T(2,128)(2,1)S(1)}, u32[]{:S(2)}, u32[]{:S(2)}) async-start(bf16[8,2,8256]{2,1,0:T(2,128)(2,1)} %reshape.666), calls=%async_computation | async-start | bytes 532480 | tf_op jit(solution)/shard_map/all_to_all | solution.py:147
  38.4 0.5 broadcast.694
  39.0 1.1 reduce.13
  40.2 1.3 convolution_bitcast_fusion.1
  41.4 1.1 convolution_bitcast_fusion
  43.1 0.8 copy.222
  44.0 0.7 fusion.17
  44.7 0.3 reshape.667
  45.2 0.4 reshape.636
  45.6 2.0 reshape.634
  48.2 1.4 slice_reduce_fusion.1
  49.6 0.3 mul.404
  49.9 0.9 copy.216
  50.8 0.3 mul.409
  51.2 0.9 copy.221
  52.1 5.2 %add_convert_fusion = (bf16[12,8,8,32,1,32]{3,2,1,0,5,4:T(8,128)(2,1)S(1)}, bf16[12,8,8,32,1,32]{3,2,1,0,5,4:T(8,128)(2,1)S(1)}) fusion(f32[12,32,32]{1,0,2:T(8,128)} %copy.222, f32[8,8,32,32]{2,1,0,3:T(8,128)S(1)} %copy.221, f32[12,32,32]{1,0,2:T(8,128)S(1)} %copy.220, f32[8,8,32,32]{2,1,0,3:T(8,128)S(1)} %copy.216), kind=kLoop, calls=%fused_computation.11 | loop fusion | flops 6291456 | bytes 3768320 | tf_op jit(solution)/shard_map/convert.4
  57.3 6.1 %pad_maximum_fusion = bf16[12,8,8,32,2,32]{3,2,1,0,5,4:T(8,128)(2,1)} fusion(bf16[12,8,8,32,1,32]{3,2,1,0,5,4:T(8,128)(2,1)S(1)} %get-tuple-element.18, bf16[12,8,8,32,1,32]{3,2,1,0,5,4:T(8,128)(2,1)S(1)} %get-tuple-element.17), kind=kLoop, calls=%fused_computation.6 | loop fusion | flops 1572864 | bytes 6291456 | tf_op jit(solution)/shard_map/stack | solution.py:105
  63.4 14.9 %convert_element_type.238 = bf16[24576,64]{0,1:T(8,128)(2,1)S(1)} reshape(bf16[12,8,8,32,2,32]{3,2,1,0,5,4:T(8,128)(2,1)} %pad_maximum_fusion) | data formatting | bytes 6291456 | tf_op jit(solution)/shard_map/convert_element_type | solution.py:107
  78.3 4.0 %convolution_convert_fusion.1 = bf16[24576,128]{1,0:T(8,128)(2,1)} fusion(bf16[24576,64]{0,1:T(8,128)(2,1)S(1)} %convert_element_type.238, bf16[64,128]{1,0:T(8,128)(2,1)S(1)} %reshape.622), kind=kOutput, calls=%fused_computation.1 | convolution fusion | flops 405798912 | bytes 9453568 | tf_op jit(solution)/shard_map/mk,kn->mn/dot_general | solution.py:49
  82.3 21.6 %reshape.623 = bf16[12,8,8,32,2,64]{5,4,3,2,1,0:T(2,128)(2,1)} reshape(bf16[24576,128]{1,0:T(8,128)(2,1)} %convolution_convert_fusion.1) | data formatting | bytes 12582912 | tf_op jit(solution)/shard_map/reshape | solution.py:109
  103.9 15.8 %copy.224 = bf16[12,8,8,64,2,32]{3,2,5,4,1,0:T(8,128)(2,1)} copy(bf16[12,8,8,64,2,32]{3,4,5,2,1,0:T(2,128)(2,1)} %bitcast.204) | data formatting | bytes 12582912 | tf_op jit(solution)/shard_map/transpose | solution.py:110
  119.7 17.1 %dot_general.55 = bf16[12,8,512,64]{2,3,1,0:T(8,128)(2,1)} reshape(bf16[12,8,8,64,2,32]{3,2,5,4,1,0:T(8,128)(2,1)} %copy.224) | data formatting | bytes 12582912 | tf_op jit(solution)/shard_map/mk,kn->mn/dot_general | solution.py:49
  137.1 4.9 %subtract_reduce_fusion.2 = (f32[12,8]{1,0:T(8,128)S(1)}, f32[12,8,512,64]{2,3,1,0:T(8,128)S(1)}) fusion(f32[12,8]{1,0:T(8,128)S(1)} %copy.226, bf16[12,8,512,64]{2,3,1,0:T(8,128)(2,1)} %dot_general.55, bf16[64,64,1,1]{1,0,3,2:T(8,128)(2,1)S(1)} %bitcast.217), kind=kOutput, calls=%fused_computation.15 | convolution fusion | flops 408944544 | bytes 18883328 | tf_op jit(solution)/shard_map/mk,kn->mn/dot_general | solution.py:49
  142.0 5.0 %subtract_reduce_fusion.1 = (f32[8]{0:T(128)S(1)}, f32[12,8]{1,0:T(8,128)S(1)}, bf16[12,8,512,64]{2,3,1,0:T(8,128)(2,1)}) fusion(f32[12,8,512,64]{2,3,1,0:T(8,128)S(1)} %get-tuple-element.42, f32[12,8]{1,0:T(8,128)S(1)} %copy.226, f32[12,8]{1,0:T(8,128)S(1)} %get-tuple-element.41), kind=kLoop, calls=%fused_computation.14 | loop fusion | flops 15728536 | bytes 18875552 | tf_op jit(solution)/shard_map/reduce_max | solution.py:168
  147.1 0.6 broadcast_in_dim.11
  147.7 5.6 %all-to-all-start.2 = ((f32[8,2,8]{2,1,0:T(2,128)}), f32[8,2,8]{2,1,0:T(2,128)S(1)}, u32[]{:S(2)}, u32[]{:S(2)}) async-start(f32[8,2,8]{2,1,0:T(2,128)} %broadcast_in_dim.11), calls=%async_computation.2 | async-start | bytes 16384 | tf_op jit(solution)/shard_map/all_to_all | solution.py:171
  153.3 16.2 %reshape.625 = bf16[12,8,8,64,64]{3,2,4,1,0:T(8,128)(2,1)} reshape(bf16[12,8,512,64]{2,3,1,0:T(8,128)(2,1)} %get-tuple-element.16) | data formatting | bytes 12582912 | tf_op jit(solution)/shard_map/reshape | solution.py:116
  169.5 19.8 %copy.227 = bf16[12,8,8,64,64]{4,2,1,0,3:T(8,128)(2,1)} copy(bf16[12,8,8,64,64]{3,2,4,1,0:T(8,128)(2,1)} %reshape.625) | data formatting | bytes 12582912 | tf_op jit(solution)/shard_map/reshape | solution.py:116
  189.3 13.6 %reshape.626 = bf16[49152,64]{0,1:T(8,128)(2,1)} reshape(bf16[12,8,8,64,64]{3,2,1,0,4:T(8,128)(2,1)} %bitcast.205) | data formatting | bytes 12582912 | tf_op jit(solution)/shard_map/reshape | solution.py:117
  202.9 7.2 %convolution_convert_fusion = bf16[49152,64]{0,1:T(8,128)(2,1)} fusion(bf16[64,64]{0,1:T(8,128)(2,1)S(1)} %bitcast.218, bf16[49152,64]{0,1:T(8,128)(2,1)} %reshape.626), kind=kOutput, calls=%fused_computation | convolution fusion | flops 405798912 | bytes 12591104 | tf_op jit(solution)/shard_map/mk,kn->mn/dot_general | solution.py:49
  210.1 14.8 %reshape.628 = bf16[12,8,8,64,2,32]{3,2,1,0,5,4:T(8,128)(2,1)} reshape(bf16[49152,64]{0,1:T(8,128)(2,1)} %convolution_convert_fusion) | data formatting | bytes 12582912 | tf_op jit(solution)/shard_map/reshape | solution.py:118
  224.9 43.4 %copy.228 = bf16[12,8,8,64,2,32]{5,2,1,0,4,3:T(8,128)(2,1)} copy(bf16[12,8,8,64,2,32]{3,2,1,0,5,4:T(8,128)(2,1)} %reshape.628) | data formatting | bytes 12582912 | tf_op jit(solution)/shard_map/reshape | solution.py:118
  268.3 29.3 %reshape.629 = bf16[24576,128]{0,1:T(8,128)(2,1)} reshape(bf16[12,8,8,32,64,2]{3,2,1,0,5,4:T(8,128)(2,1)} %bitcast.203) | data formatting | bytes 12582912 | tf_op jit(solution)/shard_map/reshape | solution.py:119
  297.6 6.5 %fusion = f32[24576,64]{0,1:T(8,128)} fusion(bf16[24576,128]{0,1:T(8,128)(2,1)} %reshape.629, bf16[128,64]{1,0:T(8,128)(2,1)S(1)} %reshape.630), kind=kOutput, calls=%fused_computation.3 | convolution fusion | flops 405798912 | bytes 12599296 | tf_op jit(solution)/shard_map/mk,kn->mn/dot_general | solution.py:49
  304.1 14.1 %reshape.638 = f32[12,8,8,32,2,32]{3,2,1,0,5,4:T(8,128)} reshape(f32[24576,64]{0,1:T(8,128)} %fusion) | data formatting | bytes 12582912 | tf_op jit(solution)/shard_map/reshape | solution.py:121
  318.7 0.6 copy.215
  319.3 0.6 copy.230
  320.0 13.8 %subtract_reduce_fusion = (f32[12,8,32,32]{2,1,0,3:T(8,128)S(1)}, f32[12,8,32,32]{2,1,0,3:T(8,128)S(1)}) fusion(f32[12,8,8,32,2,32]{3,2,1,0,5,4:T(8,128)} %reshape.638, f32[8,8,32,32]{2,1,0,3:T(8,128)S(1)} %copy.230, f32[8,8,32,32]{2,1,0,3:T(8,128)S(1)} %copy.215), kind=kLoop, calls=%fused_computation.8 | loop fusion | flops 6094848 | bytes 7602176 | tf_op jit(solution)/shard_map/reduce_sum | solution.py:123
  334.0 1.8 copy.231
  335.8 2.3 reshape.633
  338.4 1.9 fusion.57
  340.4 0.3 concatenate.15
  341.0 0.8 copy.291
  341.8 1.6 reshape.670
  343.4 11.7 %all-to-all-start.3 = ((f32[64,1,576]{2,1,0:T(1,128)}), f32[64,1,576]{2,1,0:T(1,128)S(1)}, u32[]{:S(2)}, u32[]{:S(2)}) async-start(f32[64,1,576]{2,1,0:T(1,128)} %reshape.670), calls=%async_computation.3 | async-start | bytes 327680 | tf_op jit(solution)/shard_map/all_to_all | solution.py:183
  355.2 0.5 log_add_fusion
  355.7 12.5 %all-to-all-done.3 = f32[64,1,576]{2,1,0:T(1,128)S(1)} async-done(((f32[64,1,576]{2,1,0:T(1,128)}), f32[64,1,576]{2,1,0:T(1,128)S(1)}, u32[]{:S(2)}, u32[]{:S(2)}) %all-to-all-start.3) | async-done | bytes 147488 | tf_op jit(solution)/shard_map/all_to_all | solution.py:183
  368.2 1.0 reduce.14
  369.2 1.0 reshape.671
  370.2 0.3 bitcast_reduce_fusion
  370.5 0.6 slice_divide_fusion
  (77 shorter events, 5.7 us)
Async XLA Ops:
  0.6 47.0 %copy-start = (f32[16,23]{1,0:T(8,128)S(1)}, f32[16,23]{1,0:T(8,128)}, u32[]{:S(2)}) copy-start(f32[16,23]{1,0:T(8,128)} %param.8) | copy-start | bytes 4420
  2.3 31.0 %all-to-all-start.1 = ((f32[64,1,768]{2,1,0:T(1,128)}), f32[64,1,768]{2,1,0:T(1,128)S(1)}, u32[]{:S(2)}, u32[]{:S(2)}) async-start(f32[64,1,768]{2,1,0:T(1,128)} %reshape.668), calls=%async_computation.1 | async-start | bytes 393216 | tf_op jit(solution)/shard_map/all_to_all | solution.py:154
  33.3 11.4 %all-to-all-start = ((bf16[8,2,8256]{2,1,0:T(2,128)(2,1)}), bf16[8,2,8256]{2,1,0:T(2,128)(2,1)S(1)}, u32[]{:S(2)}, u32[]{:S(2)}) async-start(bf16[8,2,8256]{2,1,0:T(2,128)(2,1)} %reshape.666), calls=%async_computation | async-start | bytes 532480 | tf_op jit(solution)/shard_map/all_to_all | solution.py:147
  119.7 17.2 %copy-start.3 = (f32[12,1,1024]{2,1,0:T(1,128)S(1)}, f32[12,1,1024]{2,1,0:T(1,128)}, u32[]{:S(2)}) copy-start(f32[12,1,1024]{2,1,0:T(1,128)} %fusion.17) | copy-start | bytes 147460
  147.7 190.4 %all-to-all-start.2 = ((f32[8,2,8]{2,1,0:T(2,128)}), f32[8,2,8]{2,1,0:T(2,128)S(1)}, u32[]{:S(2)}, u32[]{:S(2)}) async-start(f32[8,2,8]{2,1,0:T(2,128)} %broadcast_in_dim.11), calls=%async_computation.2 | async-start | bytes 16384 | tf_op jit(solution)/shard_map/all_to_all | solution.py:171
  304.1 14.1 %copy-start.2 = (f32[8,8,2,32,32]{4,3,2,1,0:T(8,128)S(1)}, f32[8,8,2,32,32]{4,3,2,1,0:T(8,128)}, u32[]{:S(2)}) copy-start(f32[8,8,2,32,32]{4,3,2,1,0:T(8,128)} %reshape.634) | copy-start | bytes 1572868
  338.4 32.7 %copy-start.1 = (f32[16,23]{1,0:T(8,128)S(1)}, f32[16,23]{1,0:T(8,128)}, u32[]{:S(2)}) copy-start(f32[16,23]{1,0:T(8,128)} %param.8) | copy-start | bytes 4420
  343.4 24.7 %all-to-all-start.3 = ((f32[64,1,576]{2,1,0:T(1,128)}), f32[64,1,576]{2,1,0:T(1,128)S(1)}, u32[]{:S(2)}, u32[]{:S(2)}) async-start(f32[64,1,576]{2,1,0:T(1,128)} %reshape.670), calls=%async_computation.3 | async-start | bytes 327680 | tf_op jit(solution)/shard_map/all_to_all | solution.py:183

commit v5 on v3

--- a/solution.py
+++ b/solution.py
@@ -157,6 +157,7 @@
         contrast_transfer * contrast_transfer / noise_deviation[None, :], power.T, precision=HIGHEST
     )
     peaks, totals, projs = class_step(abstract_value, output_value, rbands, offset.T, tabs)
+    peaks, totals = lax.optimization_barrier((peaks, totals))
     local_top = jnp.max(peaks, axis=0)
     local_mass = jnp.sum(jnp.exp(peaks - local_top[None, :]) * totals, axis=0)
     own_summary = jnp.stack([local_top, local_mass])

time: 181 us -> 171 us (0.945)
  other arithmetic: 44.3 us -> 38.5 us
  local copies, waits for them, and re-layouts: 27.4 us -> 23.1 us
    reduce_max x1, other arithmetic: 11.1 us -> 0.02 us  [shards(): local_top = jnp.max(peaks, axis=0)]
    reduce_sum x1, other arithmetic: 5.99 us -> 11.3 us  [class_step(): total = jnp.sum(expo, axis=(2, 3, 4))]
    unnamed x26 -> x20, local copies, waits for them, and re-layouts: 10.9 us -> 6.63 us
  transfers between devices with their start and end apart: 4 -> 4, of which waited for: 2 -> 2; matrix products, arithmetic and copies ran while one was open for 34% -> 36% of each run, Pallas kernels for 0% -> 0%
where the time goes in v5:
time: 171 us; the launch traced here: 170 us
  matrix products  53.2 us (31%)
  starting transfers between devices  39 us (23%)
  other arithmetic  38.5 us (23%)
  local copies, waits for them, and re-layouts  23.1 us (14%)
  waiting for transfers between devices  14.7 us (9%)
    dot_general x3, matrix products, product(): return jnp.einsum(form, left, right, preferred_element_type=jnp.float32)  46.7 us
    all_to_all x1, starting transfers between devices, shards(): pieces = lax.all_to_all(spread, 'dom', 0, 0, tiled=True)  17.6 us
    all_to_all x1, waiting for transfers between devices, shards(): owned = jnp.sum(lax.all_to_all(parts, 'dom', 0, 0, tiled=True), axis=0)  12.5 us
    all_to_all x1, starting transfers between devices, shards(): owned = jnp.sum(lax.all_to_all(parts, 'dom', 0, 0, tiled=True), axis=0)  11.3 us
    reduce_sum x1, other arithmetic, class_step(): total = jnp.sum(expo, axis=(2, 3, 4))  11.3 us
    reduce_sum x1, other arithmetic, class_step(): jnp.sum(yval[None, :, :, 0] * what[:, :, :, 0] - yval[None, :, :, 1] * wh...  11.2 us
    another operation x1, other arithmetic  7.66 us
    unnamed x20, local copies, waits for them, and re-layouts  6.63 us
  transfers between devices with their start and end apart: 4, of which 2 were waited for; matrix products, arithmetic and copies ran while one was open for 36% of the time, Pallas kernels for 0%

profile of v5, /device:TPU:1, one launch (start us, length us, event | category | flops | bytes accessed | tf_op | source)
XLA Modules:
  0.0 170.2 jit_solution(9180651578244253792)
XLA Ops:
  0.6 0.7 broadcast_in_dim.10
  1.4 0.9 reshape.603
  2.3 17.6 %all-to-all-start.1 = ((f32[64,1,768]{2,1,0:T(1,128)}), f32[64,1,768]{2,1,0:T(1,128)S(1)}, u32[]{:S(2)}, u32[]{:S(2)}) async-start(f32[64,1,768]{2,1,0:T(1,128)} %reshape.603), calls=%async_computation.1 | async-start | bytes 393216 | tf_op jit(solution)/shard_map/all_to_all | solution.py:146
  20.0 0.8 copy.90
  20.8 0.8 rev.22
  21.6 0.7 constant_dynamic-update-slice_fusion.7
  22.3 0.8 rev.23
  23.3 0.2 fusion.86
  23.4 0.2 sine_convert_fusion
  23.6 0.2 fusion.92
  23.8 0.1 cosine_convert_fusion.1
  23.9 0.1 fusion.81
  24.1 0.1 fusion.91
  24.6 0.4 fusion.23
  25.9 0.2 pad_reduce_fusion
  26.1 0.3 broadcast_in_dim.9
  26.4 0.5 broadcast.692
  26.9 2.3 %reduce.7 = bf16[8,16512]{1,0:T(8,128)(2,1)S(1)} reduce(bf16[8,1,16512]{2,1,0:T(2,128)(2,1)S(1)} %broadcast_in_dim.9, bf16[]{:T(256)} %broadcast.692), dimensions={1}, to_apply=%broadcast_in_dim.9.reduce_sub_computation | reduce | bytes 528386 | tf_op jit(solution)/shard_map/broadcast_in_dim | solution.py:140
  29.1 0.9 reshape.601
  30.2 0.8 fusion.30
  31.0 2.3 %all-to-all-done.1 = f32[64,1,768]{2,1,0:T(1,128)S(1)} async-done(((f32[64,1,768]{2,1,0:T(1,128)}), f32[64,1,768]{2,1,0:T(1,128)S(1)}, u32[]{:S(2)}, u32[]{:S(2)}) %all-to-all-start.1) | async-done | bytes 196640 | tf_op jit(solution)/shard_map/all_to_all | solution.py:146
  33.3 4.9 %all-to-all-start = ((bf16[8,2,8256]{2,1,0:T(2,128)(2,1)}), bf16[8,2,8256]{2,1,0:T(2,128)(2,1)S(1)}, u32[]{:S(2)}, u32[]{:S(2)}) async-start(bf16[8,2,8256]{2,1,0:T(2,128)(2,1)} %reshape.601), calls=%async_computation | async-start | bytes 532480 | tf_op jit(solution)/shard_map/all_to_all | solution.py:139
  38.2 0.6 broadcast.693
  38.8 1.1 reduce.8
  40.1 1.3 convolution_bitcast_fusion.1
  41.4 1.1 convolution_bitcast_fusion
  42.5 0.2 reshape.592
  42.7 0.8 mul.415
  43.4 0.8 mul.420
  44.2 0.7 fusion.37
  44.9 0.3 reshape.602
  45.5 0.7 reshape.565
  46.2 0.2 fusion.89
  46.3 0.2 broadcast_divide_fusion
  46.6 0.7 fusion.103
  47.3 0.2 copy.96
  47.4 0.3 mul.413
  47.8 1.1 copy.100
  48.9 1.3 mul.418
  50.3 1.0 convolution_multiply_fusion
  51.4 7.7 %add_convert_fusion = (bf16[12,8,8,1,32,32]{5,4,3,2,1,0:T(8,128)(2,1)}, bf16[12,8,8,1,32,32]{5,4,3,2,1,0:T(8,128)(2,1)}) fusion(f32[12,32,32]{2,1,0:T(8,128)} %mul.420, f32[8,8,32,32]{3,2,1,0:T(8,128)} %mul.418, f32[12,32,32]{2,1,0:T(8,128)} %mul.415, f32[8,8,32,32]{3,2,1,0:T(8,128)S(1)} %mul.413), kind=kLoop, calls=%fused_computation.26 | loop fusion | flops 6291456 | bytes 3768320 | tf_op jit(solution)/shard_map/convert.4
  59.0 16.8 %bitcast_reduce_fusion = (f32[12,8]{1,0:T(8,128)S(1)}, f32[64,12,8,8,64,1]{4,0,5,3,2,1:T(8,128)}) fusion(f32[12,8]{1,0:T(8,128)S(1)} %copy.102, bf16[12,8,8,1,32,32]{5,4,3,2,1,0:T(8,128)(2,1)} %get-tuple-element.11, bf16[12,8,8,1,32,32]{5,4,3,2,1,0:T(8,128)(2,1)} %get-tuple-element.10, bf16[1,32,2,64]{3,1,0,2:T(8,128)(2,1)S(1)} %get-tuple-element.25, ...), kind=kOutput, calls=%fused_computation.2 | convolution fusion | flops 821084032 | bytes 15753984 | tf_op jit(solution)/shard_map/knradx,day->knyrx/dot_general | solution.py:49
  75.9 11.3 %fusion.1 = f32[12,8]{1,0:T(8,128)S(1)} fusion(f32[64,12,8,8,64,1]{4,0,5,3,2,1:T(8,128)} %get-tuple-element.36, f32[12,8]{1,0:T(8,128)S(1)} %get-tuple-element.4, f32[12,8]{1,0:T(8,128)S(1)} %copy.102), kind=kLoop, calls=%fused_computation.7 | loop fusion | flops 9437088 | bytes 12584064 | tf_op jit(solution)/shard_map/reduce_sum | solution.py:110
  87.2 0.6 broadcast_in_dim.11
  87.8 5.1 %all-to-all-start.2 = ((f32[8,2,8]{2,1,0:T(2,128)}), f32[8,2,8]{2,1,0:T(2,128)S(1)}, u32[]{:S(2)}, u32[]{:S(2)}) async-start(f32[8,2,8]{2,1,0:T(2,128)} %broadcast_in_dim.11), calls=%async_computation.2 | async-start | bytes 16384 | tf_op jit(solution)/shard_map/all_to_all | solution.py:164
  93.0 0.2 copy_multiply_fusion
  93.2 1.5 slice_bitcast_fusion.3
  94.8 29.4 %convert_bitcast_fusion = f32[12,8,8,2,32,32]{5,4,2,1,0,3:T(8,128)} fusion(f32[64,12,8,8,64,1]{4,0,5,3,2,1:T(8,128)} %get-tuple-element.36, f32[12,8]{1,0:T(8,128)S(1)} %get-tuple-element.4, f32[12,8]{1,0:T(8,128)S(1)} %copy.102, bf16[64,1,32]{0,2,1:T(8,128)(2,1)S(1)} %get-tuple-element.26, bf16[64,1,32]{0,2,1:T(8,128)(2,1)S(1)} %get-tuple-element.28, ...), kind=kOutput, calls=%fused_computation.6 | convolution fusion | flops 821059584 | bytes 18899712 | tf_op jit(solution)/shard_map/knrydb,ydca->knrcab/dot_general | solution.py:49
  124.2 11.2 %subtract_reduce_fusion = (f32[12,8,32,32]{3,2,1,0:T(8,128)S(1)}, f32[12,8,32,32]{3,2,1,0:T(8,128)S(1)}) fusion(f32[12,8,8,2,32,32]{5,4,2,1,0,3:T(8,128)} %convert_bitcast_fusion, f32[8,8,32,32]{3,2,1,0:T(8,128)} %get-tuple-element.13, f32[8,8,32,32]{3,2,1,0:T(8,128)} %get-tuple-element.12), kind=kLoop, calls=%fused_computation.21 | loop fusion | flops 6094848 | bytes 7602176 | tf_op jit(solution)/shard_map/reduce_sum | solution.py:115
  135.4 1.5 stack.144
  136.9 0.7 stack.145
  137.7 0.2 fusion.49
  137.9 1.8 %fusion.24 = f32[12,1,2,1024]{3,1,2,0:T(1,128)S(1)} fusion(f32[12,8,1,1]{1,0,2,3:T(8,128)S(1)} %fusion.93, f32[12,8,1,1024]{3,1,0,2:T(8,128)S(1)} %stack.145, f32[12,8,1,1024]{3,1,0,2:T(8,128)} %stack.144), kind=kOutput, calls=%fused_computation.40 | convolution fusion | flops 2555904 | bytes 885120 | tf_op jit(solution)/shard_map/kp,kpcf->ckf/dot_general | solution.py:171
  139.7 0.3 concatenate.18
  140.0 0.2 concatenate.19
  140.3 0.8 copy.178
  141.1 1.6 reshape.605
  142.8 11.3 %all-to-all-start.3 = ((f32[64,1,576]{2,1,0:T(1,128)}), f32[64,1,576]{2,1,0:T(1,128)S(1)}, u32[]{:S(2)}, u32[]{:S(2)}) async-start(f32[64,1,576]{2,1,0:T(1,128)} %reshape.605), calls=%async_computation.3 | async-start | bytes 327680 | tf_op jit(solution)/shard_map/all_to_all | solution.py:176
  154.1 0.5 log_add_fusion
  154.6 12.5 %all-to-all-done.3 = f32[64,1,576]{2,1,0:T(1,128)S(1)} async-done(((f32[64,1,576]{2,1,0:T(1,128)}), f32[64,1,576]{2,1,0:T(1,128)S(1)}, u32[]{:S(2)}, u32[]{:S(2)}) %all-to-all-start.3) | async-done | bytes 147488 | tf_op jit(solution)/shard_map/all_to_all | solution.py:176
  167.1 1.1 reduce.9
  168.2 1.0 reshape.606
  169.3 0.3 bitcast_reduce_fusion.1
  169.6 0.6 slice_divide_fusion
  (47 shorter events, 1.7 us)
Async XLA Ops:
  0.6 45.5 %copy-start = (f32[16,23]{1,0:T(8,128)S(1)}, f32[16,23]{1,0:T(8,128)}, u32[]{:S(2)}) copy-start(f32[16,23]{1,0:T(8,128)} %param.8) | copy-start | bytes 4420
  2.3 31.0 %all-to-all-start.1 = ((f32[64,1,768]{2,1,0:T(1,128)}), f32[64,1,768]{2,1,0:T(1,128)S(1)}, u32[]{:S(2)}, u32[]{:S(2)}) async-start(f32[64,1,768]{2,1,0:T(1,128)} %reshape.603), calls=%async_computation.1 | async-start | bytes 393216 | tf_op jit(solution)/shard_map/all_to_all | solution.py:146
  33.3 11.6 %all-to-all-start = ((bf16[8,2,8256]{2,1,0:T(2,128)(2,1)}), bf16[8,2,8256]{2,1,0:T(2,128)(2,1)S(1)}, u32[]{:S(2)}, u32[]{:S(2)}) async-start(bf16[8,2,8256]{2,1,0:T(2,128)(2,1)} %reshape.601), calls=%async_computation | async-start | bytes 532480 | tf_op jit(solution)/shard_map/all_to_all | solution.py:139
  87.8 49.8 %all-to-all-start.2 = ((f32[8,2,8]{2,1,0:T(2,128)}), f32[8,2,8]{2,1,0:T(2,128)S(1)}, u32[]{:S(2)}, u32[]{:S(2)}) async-start(f32[8,2,8]{2,1,0:T(2,128)} %broadcast_in_dim.11), calls=%async_computation.2 | async-start | bytes 16384 | tf_op jit(solution)/shard_map/all_to_all | solution.py:164
  124.2 46.0 %copy-start.1 = (f32[16,23]{1,0:T(8,128)S(1)}, f32[16,23]{1,0:T(8,128)}, u32[]{:S(2)}) copy-start(f32[16,23]{1,0:T(8,128)} %param.8) | copy-start | bytes 4420
  142.8 24.3 %all-to-all-start.3 = ((f32[64,1,576]{2,1,0:T(1,128)}), f32[64,1,576]{2,1,0:T(1,128)S(1)}, u32[]{:S(2)}, u32[]{:S(2)}) async-start(f32[64,1,576]{2,1,0:T(1,128)} %reshape.605), calls=%async_computation.3 | async-start | bytes 327680 | tf_op jit(solution)/shard_map/all_to_all | solution.py:176

commit v6 on v5

--- a/solution.py
+++ b/solution.py
@@ -108,7 +108,8 @@
     peak = jnp.max(score, axis=(2, 3, 4))
     expo = jnp.exp(score - peak[:, :, None, None, None])
     total = jnp.sum(expo, axis=(2, 3, 4))
-    uhalf = product("knyrx,xdb->knrydb", expo.astype(jnp.bfloat16), tab_e).astype(jnp.bfloat16)
+    expo_low, total = lax.optimization_barrier((expo.astype(jnp.bfloat16), total))
+    uhalf = product("knyrx,xdb->knrydb", expo_low, tab_e).astype(jnp.bfloat16)
     what = product("knrydb,ydca->knrcab", uhalf, tab_f).astype(jnp.bfloat16)
     what = what.astype(jnp.float32)
     yval = output_value.reshape(count, ROT, 2, BAND, BAND)
@@ -135,16 +136,29 @@
     width = ROT * 2 * BAND * BAND
     label_row = jnp.broadcast_to(group_ids.astype(jnp.bfloat16)[:, None], (count, 128))
     payload = jnp.concatenate([own_bands.reshape(count, width), label_row], axis=1)
-    peers = lax.psum(1, "cls")
+    peers = lax.psum(1, CLS)
     gathered = lax.all_to_all(
-        jnp.broadcast_to(payload, (peers,) + payload.shape[1:]), "cls", 0, 0, tiled=True
+        jnp.broadcast_to(payload, (peers,) + payload.shape[1:]), CLS, 0, 0, tiled=True
     )
     fourier_input = gathered[:, :width].reshape(-1, ROT, 2, BAND * BAND)
     block_labels = gathered[:, width].astype(jnp.int32)
-    rows = lax.psum(1, "dom")
-    spread = jnp.broadcast_to(references[None], (rows,) + references.shape)
-    pieces = lax.all_to_all(spread, "dom", 0, 0, tiled=True)
-    maps = jnp.transpose(pieces, (1, 0, 2)).reshape(references.shape[0], -1)
+    rows = lax.psum(1, DOM)
+    width_y = lax.psum(1, "y")
+    width_z = lax.psum(1, "z_hi")
+    width_c = lax.psum(1, "core")
+    first = lax.all_to_all(
+        jnp.broadcast_to(references[None], (width_y,) + references.shape), "y", 0, 0, tiled=True
+    )
+    second = lax.all_to_all(
+        jnp.broadcast_to(first[None], (width_z * width_c,) + first.shape),
+        ("z_hi", "core"),
+        0,
+        0,
+        tiled=True,
+    )
+    pieces = second.reshape((width_z, width_c, width_y) + references.shape)
+    pieces = jnp.transpose(pieces, (3, 0, 2, 1, 4)).reshape(references.shape[0], -1)
+    maps = pieces
     complete_input = fourier_input.astype(jnp.float32)
     contrast_transfer, noise_deviation = spectra(ctf_profile, noise_power, block_labels)
     abstract_value = (
@@ -162,7 +176,7 @@
     local_mass = jnp.sum(jnp.exp(peaks - local_top[None, :]) * totals, axis=0)
     own_summary = jnp.stack([local_top, local_mass])
     summary = lax.all_to_all(
-        jnp.broadcast_to(own_summary[None], (peers,) + own_summary.shape), "cls", 0, 0, tiled=True
+        jnp.broadcast_to(own_summary[None], (peers,) + own_summary.shape), CLS, 0, 0, tiled=True
     )
     top = jnp.max(summary[:, 0], axis=0)
     mass = jnp.sum(jnp.exp(summary[:, 0] - top[None, :]) * summary[:, 1], axis=0)
@@ -172,13 +186,21 @@
     denom = jnp.dot(share * totals, contrast_transfer * contrast_transfer, precision=HIGHEST)
     stacked = jnp.concatenate([numer, denom[None]], axis=0)
     lanes = stacked.shape[2] // rows
-    parts = jnp.moveaxis(stacked.reshape(3, stacked.shape[1], rows, lanes), 2, 0)
-    owned = jnp.sum(lax.all_to_all(parts, "dom", 0, 0, tiled=True), axis=0)
+    split = stacked.reshape(3, stacked.shape[1], width_z, width_y, width_c, lanes)
+    step = jnp.sum(lax.all_to_all(jnp.moveaxis(split, 3, 0), "y", 0, 0, tiled=True), axis=0)
+    step = jnp.transpose(step, (2, 3, 0, 1, 4)).reshape(width_z * width_c, 3, -1, lanes)
+    owned = jnp.sum(lax.all_to_all(step, ("z_hi", "core"), 0, 0, tiled=True), axis=0)
     new_refs = owned[:2] / (owned[2] + 1.0)[None]
     return (new_refs, log_evidence)
 
 
+DOM = ("z_hi", "y", "core")
+CLS = ("z_lo", "x")
+
+
 def solution(mesh):
-    in_specs = (P(("dom", "cls"), None, None), P(("dom", "cls")), P("cls", "dom"), P(), P())
-    out_specs = (P(None, "cls", "dom"), P("dom"))
-    return jax.shard_map(shards, mesh=mesh, in_specs=in_specs, out_specs=out_specs, check_vma=False)
+    dom, cls = mesh.devices.shape
+    fine = jax.sharding.Mesh(mesh.devices.reshape(4, dom // 8, 2, 2, cls // 2), DOM + CLS)
+    in_specs = (P(DOM + CLS, None, None), P(DOM + CLS), P(CLS, DOM), P(), P())
+    out_specs = (P(None, CLS, DOM), P(DOM))
+    return jax.shard_map(shards, mesh=fine, in_specs=in_specs, out_specs=out_specs, check_vma=False)

time: 171 us -> 187 us (1.094)
  blocking collectives: 0 us -> 13 us
  other arithmetic: 38.5 us -> 45.3 us
  local copies, waits for them, and re-layouts: 23.1 us -> 26.4 us
  starting transfers between devices: 39 us -> 36 us
  waiting for transfers between devices: 14.7 us -> 12.2 us
  matrix products: 53.2 us -> 51.2 us
    all_to_all x0 -> x1, blocking collectives: none -> 13 us  [shards(): lax.all_to_all(jnp.moveaxis(split, 3, 0), 'y', 0, 0, tiled=True)]
    reduce_sum x1, other arithmetic: 11.3 us -> 16.9 us  [class_step(): total = jnp.sum(expo, axis=(2, 3, 4))]
    all_to_all x3 -> x4, starting transfers between devices: 33.9 us -> 30.9 us  [the longest x1 12.4 us: shards(): lax.all_to_all(jnp.broadcast_to(first[None], (width_z * width_c,) + first...]
    unnamed x20 -> x29, local copies, waits for them, and re-layouts: 6.63 us -> 9.36 us
    all_to_all x3 -> x4, waiting for transfers between devices: 14.7 us -> 12.2 us  [the longest x1 6.62 us: shards(): lax.all_to_all(step, ('z_hi', 'core'), 0, 0, tiled=True)]
  transfers between devices with their start and end apart: 4 -> 5, of which waited for: 2 -> 3; matrix products, arithmetic and copies ran while one was open for 36% -> 32% of each run, Pallas kernels for 0% -> 0%
where the time goes in v6:
time: 187 us; the launch traced here: 186 us
  matrix products  51.2 us (27%)
  other arithmetic  45.3 us (24%)
  starting transfers between devices  36 us (19%)
  local copies, waits for them, and re-layouts  26.4 us (14%)
  blocking collectives  13 us (7%)
  waiting for transfers between devices  12.2 us (7%)
    dot_general x3, matrix products, product(): return jnp.einsum(form, left, right, preferred_element_type=jnp.float32)  45 us
    reduce_sum x1, other arithmetic, class_step(): total = jnp.sum(expo, axis=(2, 3, 4))  16.9 us
    all_to_all x1, blocking collectives, shards(): lax.all_to_all(jnp.moveaxis(split, 3, 0), 'y', 0, 0, tiled=True)  13 us
    all_to_all x1, starting transfers between devices, shards(): lax.all_to_all(jnp.broadcast_to(first[None], (width_z * width_c,) + first...  12.4 us
    reduce_sum x1, other arithmetic, class_step(): jnp.sum(yval[None, :, :, 0] * what[:, :, :, 0] - yval[None, :, :, 1] * wh...  11.2 us
    unnamed x29, local copies, waits for them, and re-layouts  9.36 us
    another operation x1, other arithmetic  7.66 us
    all_to_all x1, starting transfers between devices, shards(): lax.all_to_all(jnp.broadcast_to(references[None], (width_y,) + references...  7.64 us
  transfers between devices with their start and end apart: 5, of which 3 were waited for; matrix products, arithmetic and copies ran while one was open for 32% of the time, Pallas kernels for 0%

profile of v6, /device:TPU:1, one launch (start us, length us, event | category | flops | bytes accessed | tf_op | source)
XLA Modules:
  0.0 185.8 jit_solution(1608498007758689434)
XLA Ops:
  0.6 0.7 broadcast_in_dim.12
  1.4 0.7 reshape.612
  2.0 7.6 %all-to-all-start.1 = ((f32[8,1,768]{2,1,0:T(1,128)}), f32[8,1,768]{2,1,0:T(1,128)S(1)}, u32[]{:S(2)}, u32[]{:S(2)}) async-start(f32[8,1,768]{2,1,0:T(1,128)} %reshape.612), calls=%async_computation.1 | async-start | bytes 49152 | tf_op jit(solution)/shard_map/all_to_all | solution.py:149
  9.7 0.8 copy.109
  10.5 0.8 rev.22
  11.3 0.7 constant_dynamic-update-slice_fusion.7
  12.0 0.8 rev.23
  14.3 0.4 fusion.20
  15.6 0.7 all-to-all-done.1
  16.4 0.5 broadcast.694
  16.9 0.6 reduce.8
  17.6 0.9 reshape.614
  18.5 12.4 %all-to-all-start.2 = ((f32[8,1,6144]{2,1,0:T(1,128)}), f32[8,1,6144]{2,1,0:T(1,128)S(1)}, u32[]{:S(2)}, u32[]{:S(2)}) async-start(f32[8,1,6144]{2,1,0:T(1,128)} %reshape.614), calls=%async_computation.2 | async-start | bytes 393216 | tf_op jit(solution)/shard_map/all_to_all | solution.py:152
  30.9 0.2 pad_reduce_fusion
  31.1 0.3 broadcast_in_dim.11
  31.4 0.5 broadcast.693
  31.9 2.3 %reduce.7 = bf16[8,16512]{1,0:T(8,128)(2,1)S(1)} reduce(bf16[8,1,16512]{2,1,0:T(2,128)(2,1)S(1)} %broadcast_in_dim.11, bf16[]{:T(256)} %broadcast.693), dimensions={1}, to_apply=%broadcast_in_dim.11.reduce_sub_computation | reduce | bytes 528386 | tf_op jit(solution)/shard_map/broadcast_in_dim | solution.py:141
  34.2 0.9 reshape.610
  35.3 0.8 fusion.25
  36.1 4.8 %all-to-all-done.2 = f32[8,1,6144]{2,1,0:T(1,128)S(1)} async-done(((f32[8,1,6144]{2,1,0:T(1,128)}), f32[8,1,6144]{2,1,0:T(1,128)S(1)}, u32[]{:S(2)}, u32[]{:S(2)}) %all-to-all-start.2) | async-done | bytes 196640 | tf_op jit(solution)/shard_map/all_to_all | solution.py:152
  40.9 4.5 %all-to-all-start = ((bf16[8,2,8256]{2,1,0:T(2,128)(2,1)}), bf16[8,2,8256]{2,1,0:T(2,128)(2,1)S(1)}, u32[]{:S(2)}, u32[]{:S(2)}) async-start(bf16[8,2,8256]{2,1,0:T(2,128)(2,1)} %reshape.610), calls=%async_computation | async-start | bytes 532480 | tf_op jit(solution)/shard_map/all_to_all | solution.py:140
  45.4 1.0 reduce.9
  46.6 0.3 copy.117
  46.9 1.2 convolution_bitcast_fusion.1
  48.1 1.1 convolution_bitcast_fusion
  49.4 0.8 mul.415
  50.2 0.8 mul.420
  51.0 0.7 fusion.32
  51.7 0.3 reshape.611
  52.2 0.7 reshape.574
  52.9 0.2 fusion.85
  53.3 0.7 fusion.99
  54.2 0.3 mul.413
  54.6 1.1 copy.120
  55.7 1.3 mul.418
  57.1 1.0 convolution_multiply_fusion
  58.1 7.7 %add_convert_fusion = (bf16[12,8,8,1,32,32]{5,4,3,2,1,0:T(8,128)(2,1)}, bf16[12,8,8,1,32,32]{5,4,3,2,1,0:T(8,128)(2,1)}) fusion(f32[12,32,32]{2,1,0:T(8,128)} %mul.420, f32[8,8,32,32]{3,2,1,0:T(8,128)} %mul.418, f32[12,32,32]{2,1,0:T(8,128)} %mul.415, f32[8,8,32,32]{3,2,1,0:T(8,128)S(1)} %mul.413), kind=kLoop, calls=%fused_computation.24 | loop fusion | flops 6291456 | bytes 3768320 | tf_op jit(solution)/shard_map/convert.4
  65.8 16.8 %bitcast_reduce_fusion = (f32[12,8]{1,0:T(8,128)S(1)}, f32[64,12,8,8,64,1]{4,0,5,3,2,1:T(8,128)}) fusion(f32[12,8]{1,0:T(8,128)S(1)} %copy.122, bf16[12,8,8,1,32,32]{5,4,3,2,1,0:T(8,128)(2,1)} %get-tuple-element.27, bf16[12,8,8,1,32,32]{5,4,3,2,1,0:T(8,128)(2,1)} %get-tuple-element.26, bf16[1,32,2,64]{3,1,0,2:T(8,128)(2,1)S(1)} %get-tuple-element.41, ...), kind=kOutput, calls=%fused_computation.2 | convolution fusion | flops 821084032 | bytes 15753984 | tf_op jit(solution)/shard_map/knradx,day->knyrx/dot_general | solution.py:49
  82.6 16.9 %fusion.1 = (f32[12,8]{1,0:T(8,128)S(1)}, bf16[12,8,64,8,64]{4,2,3,1,0:T(8,128)(2,1)}) fusion(f32[64,12,8,8,64,1]{4,0,5,3,2,1:T(8,128)} %get-tuple-element.52, f32[12,8]{1,0:T(8,128)S(1)} %get-tuple-element.8, f32[12,8]{1,0:T(8,128)S(1)} %copy.122), kind=kLoop, calls=%fused_computation.7 | loop fusion | flops 12582816 | bytes 18875520 | tf_op jit(solution)/shard_map/reduce_sum | solution.py:110
  99.6 0.6 broadcast_in_dim.14
  100.2 5.1 %all-to-all-start.3 = ((f32[8,2,8]{2,1,0:T(2,128)}), f32[8,2,8]{2,1,0:T(2,128)}, u32[]{:S(2)}, u32[]{:S(2)}) async-start(f32[8,2,8]{2,1,0:T(2,128)} %broadcast_in_dim.14), calls=%async_computation.3 | async-start | bytes 16384 | tf_op jit(solution)/shard_map/all_to_all | solution.py:178
  105.4 0.2 copy_multiply_fusion
  105.6 1.5 slice_bitcast_fusion.3
  107.2 27.7 %convert_bitcast_fusion = f32[12,8,8,2,32,32]{5,4,2,1,0,3:T(8,128)} fusion(bf16[12,8,64,8,64]{4,2,3,1,0:T(8,128)(2,1)} %get-tuple-element.6, bf16[64,1,32]{0,2,1:T(8,128)(2,1)S(1)} %get-tuple-element.42, bf16[64,1,32]{0,2,1:T(8,128)(2,1)S(1)} %get-tuple-element.44, bf16[64,1,2,32]{0,3,2,1:T(8,128)(2,1)S(1)} %get-tuple-element.37, ...), kind=kOutput, calls=%fused_computation.6 | convolution fusion | flops 811622400 | bytes 12607488 | tf_op jit(solution)/shard_map/knrydb,ydca->knrcab/dot_general | solution.py:49
  134.9 11.2 %subtract_reduce_fusion = (f32[12,8,32,32]{3,2,1,0:T(8,128)S(1)}, f32[12,8,32,32]{3,2,1,0:T(8,128)S(1)}) fusion(f32[12,8,8,2,32,32]{5,4,2,1,0,3:T(8,128)} %convert_bitcast_fusion, f32[8,8,32,32]{3,2,1,0:T(8,128)} %get-tuple-element.29, f32[8,8,32,32]{3,2,1,0:T(8,128)} %get-tuple-element.28), kind=kLoop, calls=%fused_computation.21 | loop fusion | flops 6094848 | bytes 7602176 | tf_op jit(solution)/shard_map/reduce_sum | solution.py:116
  146.1 0.7 stack.144
  146.8 0.7 stack.145
  147.5 0.8 fusion.101
  148.4 1.0 fusion.44
  149.3 0.8 fusion.21
  150.2 1.0 concatenate.18
  151.2 0.6 concatenate.19
  151.8 0.6 copy_bitcast_fusion.2
  152.4 1.6 reshape.616
  154.1 13.0 %all_to_all.34 = f32[8,1,4608]{2,1,0:T(1,128)S(1)} all-to-all(f32[8,1,4608]{2,1,0:T(1,128)S(1)} %reshape.616), channel_id=1, replica_groups=mesh['z_hi'=4,'y'=8,'core'=2,'z_lo'=2,'x'=4] {'y'}, dimensions={0} | all-to-all | bytes 294912 | tf_op jit(solution)/shard_map/all_to_all | solution.py:190
  167.1 0.9 reduce.10
  168.0 1.6 reshape.617
  169.6 0.6 bitcast_reduce_fusion.1
  170.2 0.7 reshape.618
  170.9 6.4 %all-to-all-start.5 = ((f32[8,1,576]{2,1,0:T(1,128)}), f32[8,1,576]{2,1,0:T(1,128)S(1)}, u32[]{:S(2)}, u32[]{:S(2)}) async-start(f32[8,1,576]{2,1,0:T(1,128)} %reshape.618), calls=%async_computation.5 | async-start | bytes 40960 | tf_op jit(solution)/shard_map/all_to_all | solution.py:192
  177.3 0.5 log_add_fusion
  177.8 6.6 %all-to-all-done.5 = f32[8,1,576]{2,1,0:T(1,128)S(1)} async-done(((f32[8,1,576]{2,1,0:T(1,128)}), f32[8,1,576]{2,1,0:T(1,128)S(1)}, u32[]{:S(2)}, u32[]{:S(2)}) %all-to-all-start.5) | async-done | bytes 18464 | tf_op jit(solution)/shard_map/all_to_all | solution.py:192
  184.4 0.6 reduce.11
  185.2 0.6 copy.129
  (64 shorter events, 3.3 us)
Async XLA Ops:
  0.6 52.3 %copy-start = (f32[16,23]{1,0:T(8,128)S(1)}, f32[16,23]{1,0:T(8,128)}, u32[]{:S(2)}) copy-start(f32[16,23]{1,0:T(8,128)} %param.8) | copy-start | bytes 4420
  2.0 14.3 %all-to-all-start.1 = ((f32[8,1,768]{2,1,0:T(1,128)}), f32[8,1,768]{2,1,0:T(1,128)S(1)}, u32[]{:S(2)}, u32[]{:S(2)}) async-start(f32[8,1,768]{2,1,0:T(1,128)} %reshape.612), calls=%async_computation.1 | async-start | bytes 49152 | tf_op jit(solution)/shard_map/all_to_all | solution.py:149
  18.5 22.4 %all-to-all-start.2 = ((f32[8,1,6144]{2,1,0:T(1,128)}), f32[8,1,6144]{2,1,0:T(1,128)S(1)}, u32[]{:S(2)}, u32[]{:S(2)}) async-start(f32[8,1,6144]{2,1,0:T(1,128)} %reshape.614), calls=%async_computation.2 | async-start | bytes 393216 | tf_op jit(solution)/shard_map/all_to_all | solution.py:152
  40.9 10.8 %all-to-all-start = ((bf16[8,2,8256]{2,1,0:T(2,128)(2,1)}), bf16[8,2,8256]{2,1,0:T(2,128)(2,1)S(1)}, u32[]{:S(2)}, u32[]{:S(2)}) async-start(bf16[8,2,8256]{2,1,0:T(2,128)(2,1)} %reshape.610), calls=%async_computation | async-start | bytes 532480 | tf_op jit(solution)/shard_map/all_to_all | solution.py:140
  53.3 29.4 %copy-start.2 = (f32[8,1024]{1,0:T(8,128)}, f32[8,1024]{1,0:T(8,128)S(1)}, u32[]{:S(2)}) copy-start(f32[8,1024]{1,0:T(8,128)S(1)} %get-tuple-element.50) | copy-start | bytes 98308
  99.6 35.3 %copy-start.3 = (f32[12,8]{1,0:T(8,128)}, f32[12,8]{1,0:T(8,128)S(1)}, u32[]{:S(2)}) copy-start(f32[12,8]{1,0:T(8,128)S(1)} %get-tuple-element.9) | copy-start | bytes 1156
  100.2 47.3 %all-to-all-start.3 = ((f32[8,2,8]{2,1,0:T(2,128)}), f32[8,2,8]{2,1,0:T(2,128)}, u32[]{:S(2)}, u32[]{:S(2)}) async-start(f32[8,2,8]{2,1,0:T(2,128)} %broadcast_in_dim.14), calls=%async_computation.3 | async-start | bytes 16384 | tf_op jit(solution)/shard_map/all_to_all | solution.py:178
  134.9 51.0 %copy-start.1 = (f32[16,23]{1,0:T(8,128)S(1)}, f32[16,23]{1,0:T(8,128)}, u32[]{:S(2)}) copy-start(f32[16,23]{1,0:T(8,128)} %param.8) | copy-start | bytes 4420
  170.9 13.5 %all-to-all-start.5 = ((f32[8,1,576]{2,1,0:T(1,128)}), f32[8,1,576]{2,1,0:T(1,128)S(1)}, u32[]{:S(2)}, u32[]{:S(2)}) async-start(f32[8,1,576]{2,1,0:T(1,128)} %reshape.618), calls=%async_computation.5 | async-start | bytes 40960 | tf_op jit(solution)/shard_map/all_to_all | solution.py:192

commit v7 on v5

--- a/solution.py
+++ b/solution.py
@@ -93,6 +93,15 @@
     return (contrast_transfer, noise_deviation)
 
 
+def merge_scaled(left, right):
+    left_top, left_sum = left
+    right_top, right_sum = right
+    top = jnp.maximum(left_top, right_top)
+    left_scale = jnp.where(left_top == top, 1.0, jnp.exp(left_top - top))
+    right_scale = jnp.where(right_top == top, 1.0, jnp.exp(right_top - top))
+    return (top, left_sum * left_scale + right_sum * right_scale)
+
+
 def class_step(abstract_value, output_value, ref_bands, offset, tabs):
     tab_c, tab_d, tab_e, tab_f = tabs
     classes = ref_bands.shape[0]
@@ -105,9 +114,13 @@
     bmat = bmat.reshape(classes, count, ROT, 2, BAND, BAND)
     edge = product("knrcab,cbdx->knradx", bmat, tab_c).astype(jnp.bfloat16)
     score = product("knradx,day->knyrx", edge, tab_d) - offset[:, :, None, None, None]
-    peak = jnp.max(score, axis=(2, 3, 4))
+    peak, total = lax.reduce(
+        (score, jnp.ones_like(score)),
+        (jnp.array(-jnp.inf, score.dtype), jnp.array(0.0, score.dtype)),
+        merge_scaled,
+        (2, 3, 4),
+    )
     expo = jnp.exp(score - peak[:, :, None, None, None])
-    total = jnp.sum(expo, axis=(2, 3, 4))
     uhalf = product("knyrx,xdb->knrydb", expo.astype(jnp.bfloat16), tab_e).astype(jnp.bfloat16)
     what = product("knrydb,ydca->knrcab", uhalf, tab_f).astype(jnp.bfloat16)
     what = what.astype(jnp.float32)

time: 171 us -> 179 us (1.047)
  other arithmetic: 38.5 us -> 48.6 us
  matrix products: 53.2 us -> 50.8 us
    another operation x1 -> x2, other arithmetic: 7.66 us -> 28.8 us  [the longest x1 21.2 us: class_step(): lax.reduce((score, jnp.ones_like(score)), (jnp.array(-jnp.inf, score.dtyp...]
    reduce_sum x1 -> x0, other arithmetic: 11.3 us -> none  [class_step(): total = jnp.sum(expo, axis=(2, 3, 4))]
    dot_general x3, matrix products: 46.7 us -> 44.5 us  [product(): return jnp.einsum(form, left, right, preferred_element_type=jnp.float32)]
    unnamed x20 -> x24, local copies, waits for them, and re-layouts: 6.63 us -> 6.64 us
  transfers between devices with their start and end apart: 4 -> 4, of which waited for: 2 -> 2; matrix products, arithmetic and copies ran while one was open for 36% -> 34% of each run, Pallas kernels for 0% -> 0%
where the time goes in v7:
time: 179 us; the launch traced here: 178 us
  matrix products  50.8 us (28%)
  other arithmetic  48.6 us (27%)
  starting transfers between devices  39 us (22%)
  local copies, waits for them, and re-layouts  23.3 us (13%)
  waiting for transfers between devices  14.7 us (8%)
    dot_general x3, matrix products, product(): return jnp.einsum(form, left, right, preferred_element_type=jnp.float32)  44.5 us
    another operation x1, other arithmetic, class_step(): lax.reduce((score, jnp.ones_like(score)), (jnp.array(-jnp.inf, score.dtyp...  21.2 us
    all_to_all x1, starting transfers between devices, shards(): pieces = lax.all_to_all(spread, 'dom', 0, 0, tiled=True)  17.6 us
    all_to_all x1, waiting for transfers between devices, shards(): owned = jnp.sum(lax.all_to_all(parts, 'dom', 0, 0, tiled=True), axis=0)  12.5 us
    all_to_all x1, starting transfers between devices, shards(): owned = jnp.sum(lax.all_to_all(parts, 'dom', 0, 0, tiled=True), axis=0)  11.3 us
    reduce_sum x1, other arithmetic, class_step(): jnp.sum(yval[None, :, :, 0] * what[:, :, :, 0] - yval[None, :, :, 1] * wh...  11.2 us
    another operation x1, other arithmetic  7.66 us
    unnamed x24, local copies, waits for them, and re-layouts  6.64 us
  transfers between devices with their start and end apart: 4, of which 2 were waited for; matrix products, arithmetic and copies ran while one was open for 34% of the time, Pallas kernels for 0%

profile of v7, /device:TPU:1, one launch (start us, length us, event | category | flops | bytes accessed | tf_op | source)
XLA Modules:
  0.0 178.0 jit_solution(13684366622504954780)
XLA Ops:
  0.6 0.7 broadcast_in_dim.12
  1.4 0.9 reshape.603
  2.3 17.6 %all-to-all-start.1 = ((f32[64,1,768]{2,1,0:T(1,128)}), f32[64,1,768]{2,1,0:T(1,128)S(1)}, u32[]{:S(2)}, u32[]{:S(2)}) async-start(f32[64,1,768]{2,1,0:T(1,128)} %reshape.603), calls=%async_computation.1 | async-start | bytes 393216 | tf_op jit(solution)/shard_map/all_to_all | solution.py:159
  20.0 0.8 copy.90
  20.8 0.8 rev.22
  21.6 0.7 constant_dynamic-update-slice_fusion.7
  22.3 0.8 rev.23
  23.3 0.2 fusion.85
  23.4 0.2 sine_convert_fusion
  23.6 0.2 fusion.91
  23.9 0.1 fusion.80
  24.6 0.4 fusion.22
  25.9 0.2 pad_reduce_fusion
  26.1 0.3 broadcast_in_dim.11
  26.4 0.5 broadcast.692
  26.9 2.3 %reduce.24 = bf16[8,16512]{1,0:T(8,128)(2,1)S(1)} reduce(bf16[8,1,16512]{2,1,0:T(2,128)(2,1)S(1)} %broadcast_in_dim.11, bf16[]{:T(256)} %broadcast.692), dimensions={1}, to_apply=%broadcast_in_dim.11.reduce_sub_computation | reduce | bytes 528386 | tf_op jit(solution)/shard_map/broadcast_in_dim | solution.py:153
  29.1 0.9 reshape.601
  30.2 0.8 fusion.29
  31.0 2.3 %all-to-all-done.1 = f32[64,1,768]{2,1,0:T(1,128)S(1)} async-done(((f32[64,1,768]{2,1,0:T(1,128)}), f32[64,1,768]{2,1,0:T(1,128)S(1)}, u32[]{:S(2)}, u32[]{:S(2)}) %all-to-all-start.1) | async-done | bytes 196640 | tf_op jit(solution)/shard_map/all_to_all | solution.py:159
  33.3 4.9 %all-to-all-start = ((bf16[8,2,8256]{2,1,0:T(2,128)(2,1)}), bf16[8,2,8256]{2,1,0:T(2,128)(2,1)S(1)}, u32[]{:S(2)}, u32[]{:S(2)}) async-start(bf16[8,2,8256]{2,1,0:T(2,128)(2,1)} %reshape.601), calls=%async_computation | async-start | bytes 532480 | tf_op jit(solution)/shard_map/all_to_all | solution.py:152
  38.2 0.6 broadcast.693
  38.8 1.1 reduce.25
  40.1 1.3 convolution_bitcast_fusion.1
  41.4 1.1 convolution_bitcast_fusion
  42.5 0.2 reshape.592
  42.7 0.8 mul.419
  43.4 0.8 mul.424
  44.2 0.7 fusion.36
  44.9 0.3 reshape.602
  45.5 0.7 reshape.565
  46.2 0.2 fusion.88
  46.3 0.2 broadcast_divide_fusion
  46.6 0.7 fusion.102
  47.3 0.2 copy.96
  47.5 0.3 mul.417
  47.8 1.1 copy.100
  48.9 1.3 mul.422
  50.3 1.0 convolution_multiply_fusion
  51.4 7.7 %add_convert_fusion = (bf16[12,8,8,1,32,32]{5,4,3,2,1,0:T(8,128)(2,1)}, bf16[12,8,8,1,32,32]{5,4,3,2,1,0:T(8,128)(2,1)}) fusion(f32[12,32,32]{2,1,0:T(8,128)} %mul.424, f32[8,8,32,32]{3,2,1,0:T(8,128)} %mul.422, f32[12,32,32]{2,1,0:T(8,128)} %mul.419, f32[8,8,32,32]{3,2,1,0:T(8,128)S(1)} %mul.417), kind=kLoop, calls=%fused_computation.25 | loop fusion | flops 6291456 | bytes 3768320 | tf_op jit(solution)/shard_map/convert.4
  59.0 14.7 %fusion.2 = f32[64,12,8,8,64,1]{4,0,5,3,2,1:T(8,128)} fusion(bf16[12,8,8,1,32,32]{5,4,3,2,1,0:T(8,128)(2,1)} %get-tuple-element.13, bf16[12,8,8,1,32,32]{5,4,3,2,1,0:T(8,128)(2,1)} %get-tuple-element.12, bf16[1,32,2,64]{3,1,0,2:T(8,128)(2,1)S(1)} %get-tuple-element.27, bf16[1,32,2,64]{3,1,0,2:T(8,128)(2,1)S(1)} %get-tuple-element.26, ...), kind=kOutput, calls=%fused_computation.8 | convolution fusion | flops 814792704 | bytes 15753216 | tf_op jit(solution)/shard_map/knradx,day->knyrx/dot_general | solution.py:49
  73.7 21.2 %bitcast_reduce_fusion = (f32[12,8]{1,0:T(8,128)S(1)}, f32[12,8]{1,0:T(8,128)S(1)}) fusion(f32[64,12,8,8,64,1]{4,0,5,3,2,1:T(8,128)} %fusion.2, f32[12,8]{1,0:T(8,128)S(1)} %copy.102), kind=kLoop, calls=%fused_computation.2 | loop fusion | flops 34602048 | bytes 12584064 | tf_op jit(solution)/shard_map/reduce | solution.py:117
  95.1 0.2 multiply_reduce_fusion.1
  95.3 0.6 broadcast_in_dim.14
  95.9 5.1 %all-to-all-start.2 = ((f32[8,2,8]{2,1,0:T(2,128)}), f32[8,2,8]{2,1,0:T(2,128)}, u32[]{:S(2)}, u32[]{:S(2)}) async-start(f32[8,2,8]{2,1,0:T(2,128)} %broadcast_in_dim.14), calls=%async_computation.2 | async-start | bytes 16384 | tf_op jit(solution)/shard_map/all_to_all | solution.py:177
  101.1 0.2 copy_multiply_fusion
  101.3 1.5 slice_bitcast_fusion.3
  102.8 29.4 %convert_bitcast_fusion = f32[12,8,8,2,32,32]{5,4,2,1,0,3:T(8,128)} fusion(f32[64,12,8,8,64,1]{4,0,5,3,2,1:T(8,128)} %fusion.2, f32[12,8]{1,0:T(8,128)S(1)} %get-tuple-element.5, f32[12,8]{1,0:T(8,128)S(1)} %copy.102, bf16[64,1,32]{0,2,1:T(8,128)(2,1)S(1)} %get-tuple-element.28, bf16[64,1,32]{0,2,1:T(8,128)(2,1)S(1)} %get-tuple-element.30, ...), kind=kOutput, calls=%fused_computation.7 | convolution fusion | flops 821059584 | bytes 18899712 | tf_op jit(solution)/shard_map/knrydb,ydca->knrcab/dot_general | solution.py:49
  132.3 11.2 %subtract_reduce_fusion = (f32[12,8,32,32]{3,2,1,0:T(8,128)S(1)}, f32[12,8,32,32]{3,2,1,0:T(8,128)S(1)}) fusion(f32[12,8,8,2,32,32]{5,4,2,1,0,3:T(8,128)} %convert_bitcast_fusion, f32[8,8,32,32]{3,2,1,0:T(8,128)} %get-tuple-element.15, f32[8,8,32,32]{3,2,1,0:T(8,128)} %get-tuple-element.14), kind=kLoop, calls=%fused_computation.20 | loop fusion | flops 6094848 | bytes 7602176 | tf_op jit(solution)/shard_map/reduce_sum | solution.py:128
  143.5 0.7 stack.144
  144.2 0.7 stack.145
  144.9 0.8 fusion.104
  145.8 1.0 fusion.48
  146.8 0.8 fusion.23
  147.6 0.3 concatenate.18
  147.9 0.2 concatenate.19
  148.2 0.8 copy.180
  149.0 1.6 reshape.605
  150.7 11.3 %all-to-all-start.3 = ((f32[64,1,576]{2,1,0:T(1,128)}), f32[64,1,576]{2,1,0:T(1,128)S(1)}, u32[]{:S(2)}, u32[]{:S(2)}) async-start(f32[64,1,576]{2,1,0:T(1,128)} %reshape.605), calls=%async_computation.3 | async-start | bytes 327680 | tf_op jit(solution)/shard_map/all_to_all | solution.py:189
  162.0 0.5 log_add_fusion
  162.5 12.5 %all-to-all-done.3 = f32[64,1,576]{2,1,0:T(1,128)S(1)} async-done(((f32[64,1,576]{2,1,0:T(1,128)}), f32[64,1,576]{2,1,0:T(1,128)S(1)}, u32[]{:S(2)}, u32[]{:S(2)}) %all-to-all-start.3) | async-done | bytes 147488 | tf_op jit(solution)/shard_map/all_to_all | solution.py:189
  175.0 1.1 reduce.26
  176.1 1.0 reshape.606
  177.1 0.3 bitcast_reduce_fusion.1
  177.4 0.6 slice_divide_fusion
  (53 shorter events, 2.1 us)
Async XLA Ops:
  0.6 45.5 %copy-start = (f32[16,23]{1,0:T(8,128)S(1)}, f32[16,23]{1,0:T(8,128)}, u32[]{:S(2)}) copy-start(f32[16,23]{1,0:T(8,128)} %param.8) | copy-start | bytes 4420
  2.3 31.0 %all-to-all-start.1 = ((f32[64,1,768]{2,1,0:T(1,128)}), f32[64,1,768]{2,1,0:T(1,128)S(1)}, u32[]{:S(2)}, u32[]{:S(2)}) async-start(f32[64,1,768]{2,1,0:T(1,128)} %reshape.603), calls=%async_computation.1 | async-start | bytes 393216 | tf_op jit(solution)/shard_map/all_to_all | solution.py:159
  33.3 11.6 %all-to-all-start = ((bf16[8,2,8256]{2,1,0:T(2,128)(2,1)}), bf16[8,2,8256]{2,1,0:T(2,128)(2,1)S(1)}, u32[]{:S(2)}, u32[]{:S(2)}) async-start(bf16[8,2,8256]{2,1,0:T(2,128)(2,1)} %reshape.601), calls=%async_computation | async-start | bytes 532480 | tf_op jit(solution)/shard_map/all_to_all | solution.py:152
  46.5 27.2 %copy-start.2 = (f32[8,1024]{1,0:T(8,128)}, f32[8,1024]{1,0:T(8,128)S(1)}, u32[]{:S(2)}) copy-start(f32[8,1024]{1,0:T(8,128)S(1)} %get-tuple-element.36) | copy-start | bytes 98308
  94.9 37.4 %copy-start.3 = (f32[12,8]{1,0:T(8,128)}, f32[12,8]{1,0:T(8,128)S(1)}, u32[]{:S(2)}) copy-start(f32[12,8]{1,0:T(8,128)S(1)} %get-tuple-element.7) | copy-start | bytes 1156
  95.9 49.0 %all-to-all-start.2 = ((f32[8,2,8]{2,1,0:T(2,128)}), f32[8,2,8]{2,1,0:T(2,128)}, u32[]{:S(2)}, u32[]{:S(2)}) async-start(f32[8,2,8]{2,1,0:T(2,128)} %broadcast_in_dim.14), calls=%async_computation.2 | async-start | bytes 16384 | tf_op jit(solution)/shard_map/all_to_all | solution.py:177
  132.3 45.8 %copy-start.1 = (f32[16,23]{1,0:T(8,128)S(1)}, f32[16,23]{1,0:T(8,128)}, u32[]{:S(2)}) copy-start(f32[16,23]{1,0:T(8,128)} %param.8) | copy-start | bytes 4420
  150.7 24.3 %all-to-all-start.3 = ((f32[64,1,576]{2,1,0:T(1,128)}), f32[64,1,576]{2,1,0:T(1,128)S(1)}, u32[]{:S(2)}, u32[]{:S(2)}) async-start(f32[64,1,576]{2,1,0:T(1,128)} %reshape.605), calls=%async_computation.3 | async-start | bytes 327680 | tf_op jit(solution)/shard_map/all_to_all | solution.py:189

commit v8 on v5

--- a/solution.py
+++ b/solution.py
@@ -130,16 +130,16 @@
     tabs = inverse_tables(cosine, sine)
     first_low = first_table_part.astype(jnp.bfloat16)
     second_low = second_table_part.astype(jnp.bfloat16)
-    own_bands = particle_band_rows(particles, first_low, second_low)
-    count = own_bands.shape[0]
-    width = ROT * 2 * BAND * BAND
+    count = particles.shape[0]
+    width = L * L
     label_row = jnp.broadcast_to(group_ids.astype(jnp.bfloat16)[:, None], (count, 128))
-    payload = jnp.concatenate([own_bands.reshape(count, width), label_row], axis=1)
+    payload = jnp.concatenate([particles.reshape(count, width), label_row], axis=1)
     peers = lax.psum(1, "cls")
     gathered = lax.all_to_all(
         jnp.broadcast_to(payload, (peers,) + payload.shape[1:]), "cls", 0, 0, tiled=True
     )
-    fourier_input = gathered[:, :width].reshape(-1, ROT, 2, BAND * BAND)
+    images = gathered[:, :width].reshape(-1, L, L)
+    fourier_input = particle_band_rows(images, first_low, second_low)
     block_labels = gathered[:, width].astype(jnp.int32)
     rows = lax.psum(1, "dom")
     spread = jnp.broadcast_to(references[None], (rows,) + references.shape)

time: 171 us -> 170 us (level)
  local copies, waits for them, and re-layouts: 23.1 us -> 18.8 us
  matrix products: 53.2 us -> 56.4 us
  starting transfers between devices: 39 us -> 40.9 us
  waiting for transfers between devices: 14.7 us -> 12.8 us
    dot_general x3, matrix products: 46.7 us -> 50.4 us  [product(): return jnp.einsum(form, left, right, preferred_element_type=jnp.float32)]
    all_to_all x1, waiting for transfers between devices: 2.25 us -> 0.35 us  [shards(): pieces = lax.all_to_all(spread, 'dom', 0, 0, tiled=True)]
    all_to_all x1, starting transfers between devices: 4.93 us -> 6.65 us  [shards(): lax.all_to_all(jnp.broadcast_to(payload, (peers,) + payload.shape[1:]), '...]
    unnamed x20 -> x53, local copies, waits for them, and re-layouts: 6.63 us -> 5.12 us
where the time goes in v8:
time: 170 us; the launch traced here: 169 us
  matrix products  56.4 us (33%)
  starting transfers between devices  40.9 us (24%)
  other arithmetic  38.5 us (23%)
  local copies, waits for them, and re-layouts  18.8 us (11%)
  waiting for transfers between devices  12.8 us (8%)
  between operations  1.85 us (1%)
    dot_general x3, matrix products, product(): return jnp.einsum(form, left, right, preferred_element_type=jnp.float32)  50.4 us
    all_to_all x1, starting transfers between devices, shards(): pieces = lax.all_to_all(spread, 'dom', 0, 0, tiled=True)  16.4 us
    all_to_all x1, starting transfers between devices, shards(): owned = jnp.sum(lax.all_to_all(parts, 'dom', 0, 0, tiled=True), axis=0)  12.7 us
    all_to_all x1, waiting for transfers between devices, shards(): owned = jnp.sum(lax.all_to_all(parts, 'dom', 0, 0, tiled=True), axis=0)  12.5 us
    reduce_sum x1, other arithmetic, class_step(): total = jnp.sum(expo, axis=(2, 3, 4))  11.5 us
    reduce_sum x1, other arithmetic, class_step(): jnp.sum(yval[None, :, :, 0] * what[:, :, :, 0] - yval[None, :, :, 1] * wh...  11.2 us
    all_to_all x1, starting transfers between devices, shards(): lax.all_to_all(jnp.broadcast_to(payload, (peers,) + payload.shape[1:]), '...  6.65 us
    another operation x1, other arithmetic  6.34 us
  transfers between devices with their start and end apart: 4, of which 2 were waited for; matrix products, arithmetic and copies ran while one was open for 36% of the time, Pallas kernels for 0%

profile of v8, /device:TPU:1, one launch (start us, length us, event | category | flops | bytes accessed | tf_op | source)
XLA Modules:
  0.0 169.4 jit_solution(2778855534570993818)
XLA Ops:
  1.3 0.8 reshape.558
  2.3 0.5 broadcast.692
  2.8 1.0 reduce.7
  3.8 0.7 reshape.596
  4.5 6.6 %all-to-all-start = ((bf16[8,2,2112]{2,1,0:T(2,128)(2,1)}), bf16[8,2,2112]{2,1,0:T(2,128)(2,1)S(1)}, u32[]{:S(2)}, u32[]{:S(2)}) async-start(bf16[8,2,2112]{2,1,0:T(2,128)(2,1)} %reshape.596), calls=%async_computation | async-start | bytes 139264 | tf_op jit(solution)/shard_map/all_to_all | solution.py:138
  11.2 0.7 fusion.80
  12.0 0.7 cosine_convert_fusion.1
  12.7 0.1 fusion.91
  12.8 0.1 fusion.90
  13.0 0.2 sine_convert_fusion
  13.2 0.2 fusion.85
  13.6 0.8 fusion.29
  14.4 0.6 maximum_bitcast_fusion.15
  15.1 0.6 fusion.79
  15.7 0.7 broadcast_in_dim.10
  16.4 0.9 reshape.598
  17.4 16.4 %all-to-all-start.1 = ((f32[64,1,768]{2,1,0:T(1,128)}), f32[64,1,768]{2,1,0:T(1,128)S(1)}, u32[]{:S(2)}, u32[]{:S(2)}) async-start(f32[64,1,768]{2,1,0:T(1,128)} %reshape.598), calls=%async_computation.1 | async-start | bytes 393216 | tf_op jit(solution)/shard_map/all_to_all | solution.py:146
  34.0 0.2 reshape.559
  34.2 0.2 stack.123
  34.4 0.1 rev.22
  34.6 0.1 rev.25
  34.7 0.1 rev.23
  34.8 0.1 copy.88
  35.0 0.1 copy.90
  35.1 0.1 copy.91
  35.4 0.2 fusion.88
  35.6 0.8 broadcast_divide_fusion
  36.7 0.3 copy-done.6
  37.0 4.1 %broadcast_multiply_fusion = (f32[8,8,2,32,32]{4,3,1,0,2:T(8,128)}, f32[8,8,2,32,32]{4,3,1,0,2:T(8,128)S(1)}) fusion(f32[8,32,32]{2,1,0:T(8,128)S(1)} %mul.401, bf16[8,8,64,64]{3,2,1,0:T(8,128)(2,1)S(1)} %bitcast_dynamic-update-slice_fusion.2, f32[64,1,32]{0,2,1:T(8,128)} %copy-done.2, f32[64,1,32]{0,2,1:T(8,128)} %copy-done.4, ...), kind=kOutput, calls=%fused_computation.38 | convolution fusion | flops 67788800 | bytes 1654784 | tf_op jit(solution)/shard_map/nrydb,ydca->nrcab/dot_general | solution.py:49
  41.1 1.0 reshape.562
  42.0 0.8 broadcast_multiply_fusion.1
  42.9 0.3 mul.413
  43.3 0.3 mul.418
  43.6 3.1 %slice_bitcast_fusion.3 = (f32[8,8,32,32]{3,2,1,0:T(8,128)}, f32[8,8,32,32]{3,2,1,0:T(8,128)}) fusion(f32[8,8,2,32,32]{4,3,1,0,2:T(8,128)} %get-tuple-element.37), kind=kLoop, calls=%fused_computation.36 | loop fusion | bytes 1048576 | tf_op jit(solution)/shard_map/mul | solution.py:116
  46.7 0.3 all-to-all-done.1
  47.1 0.6 broadcast.693
  47.7 1.2 reduce.8
  49.0 1.3 convolution_bitcast_fusion.1
  50.2 1.1 convolution_bitcast_fusion
  51.3 0.2 reshape.587
  51.8 0.2 convolution_multiply_fusion
  52.1 6.3 %add_convert_fusion = (bf16[12,8,8,1,32,32]{5,4,3,2,1,0:T(8,128)(2,1)}, bf16[12,8,8,1,32,32]{5,4,3,2,1,0:T(8,128)(2,1)}) fusion(f32[12,32,32]{2,1,0:T(8,128)S(1)} %mul.420, f32[8,8,32,32]{3,2,1,0:T(8,128)S(1)} %mul.418, f32[12,32,32]{2,1,0:T(8,128)S(1)} %mul.415, f32[8,8,32,32]{3,2,1,0:T(8,128)S(1)} %mul.413), kind=kLoop, calls=%fused_computation.26 | loop fusion | flops 6291456 | bytes 3768320 | tf_op jit(solution)/shard_map/convert.5
  58.4 16.9 %bitcast_reduce_fusion = (f32[12,8]{1,0:T(8,128)S(1)}, f32[64,12,8,8,64,1]{4,0,5,3,2,1:T(8,128)}) fusion(f32[12,8]{1,0:T(8,128)S(1)} %copy.99, bf16[12,8,8,1,32,32]{5,4,3,2,1,0:T(8,128)(2,1)} %get-tuple-element.11, bf16[12,8,8,1,32,32]{5,4,3,2,1,0:T(8,128)(2,1)} %get-tuple-element.10, bf16[1,32,2,64]{3,1,0,2:T(8,128)(2,1)S(1)} %copy-done.14, ...), kind=kOutput, calls=%fused_computation.2 | convolution fusion | flops 821084032 | bytes 15753984 | tf_op jit(solution)/shard_map/knradx,day->knyrx/dot_general | solution.py:49
  75.3 11.5 %fusion.1 = f32[12,8]{1,0:T(8,128)S(1)} fusion(f32[64,12,8,8,64,1]{4,0,5,3,2,1:T(8,128)} %get-tuple-element.36, f32[12,8]{1,0:T(8,128)S(1)} %get-tuple-element.4, f32[12,8]{1,0:T(8,128)S(1)} %copy.99), kind=kLoop, calls=%fused_computation.7 | loop fusion | flops 9437088 | bytes 12584064 | tf_op jit(solution)/shard_map/reduce_sum | solution.py:110
  86.9 0.6 broadcast_in_dim.11
  87.5 5.2 %all-to-all-start.2 = ((f32[8,2,8]{2,1,0:T(2,128)}), f32[8,2,8]{2,1,0:T(2,128)}, u32[]{:S(2)}, u32[]{:S(2)}) async-start(f32[8,2,8]{2,1,0:T(2,128)} %broadcast_in_dim.11), calls=%async_computation.2 | async-start | bytes 16384 | tf_op jit(solution)/shard_map/all_to_all | solution.py:164
  92.8 29.4 %convert_bitcast_fusion = f32[12,8,8,2,32,32]{5,4,2,1,0,3:T(8,128)} fusion(f32[64,12,8,8,64,1]{4,0,5,3,2,1:T(8,128)} %get-tuple-element.36, f32[12,8]{1,0:T(8,128)S(1)} %get-tuple-element.4, f32[12,8]{1,0:T(8,128)S(1)} %copy.99, bf16[64,1,32]{0,2,1:T(8,128)(2,1)S(1)} %get-tuple-element.26, bf16[64,1,32]{0,2,1:T(8,128)(2,1)S(1)} %copy-done.10, ...), kind=kOutput, calls=%fused_computation.6 | convolution fusion | flops 821059584 | bytes 18899712 | tf_op jit(solution)/shard_map/knrydb,ydca->knrcab/dot_general | solution.py:49
  122.2 11.2 %subtract_reduce_fusion = (f32[12,8,32,32]{3,2,1,0:T(8,128)S(1)}, f32[12,8,32,32]{3,2,1,0:T(8,128)S(1)}) fusion(f32[12,8,8,2,32,32]{5,4,2,1,0,3:T(8,128)} %convert_bitcast_fusion, f32[8,8,32,32]{3,2,1,0:T(8,128)} %get-tuple-element.13, f32[8,8,32,32]{3,2,1,0:T(8,128)} %get-tuple-element.12), kind=kLoop, calls=%fused_computation.21 | loop fusion | flops 6094848 | bytes 7602176 | tf_op jit(solution)/shard_map/reduce_sum | solution.py:115
  133.4 0.7 stack.144
  134.2 0.7 stack.145
  134.9 0.8 fusion.104
  135.7 1.0 fusion.48
  136.7 0.2 concatenate.19
  136.9 0.8 fusion.25
  137.7 0.3 concatenate.18
  138.1 0.8 copy.177
  139.0 1.6 reshape.600
  140.6 12.7 %all-to-all-start.3 = ((f32[64,1,576]{2,1,0:T(1,128)}), f32[64,1,576]{2,1,0:T(1,128)S(1)}, u32[]{:S(2)}, u32[]{:S(2)}) async-start(f32[64,1,576]{2,1,0:T(1,128)} %reshape.600), calls=%async_computation.3 | async-start | bytes 327680 | tf_op jit(solution)/shard_map/all_to_all | solution.py:176
  153.3 0.5 log_add_fusion
  153.8 12.5 %all-to-all-done.3 = f32[64,1,576]{2,1,0:T(1,128)S(1)} async-done(((f32[64,1,576]{2,1,0:T(1,128)}), f32[64,1,576]{2,1,0:T(1,128)S(1)}, u32[]{:S(2)}, u32[]{:S(2)}) %all-to-all-start.3) | async-done | bytes 147488 | tf_op jit(solution)/shard_map/all_to_all | solution.py:176
  166.3 1.1 reduce.9
  167.4 1.0 reshape.601
  168.4 0.3 bitcast_reduce_fusion.1
  168.7 0.6 slice_divide_fusion
  (80 shorter events, 2.0 us)
Async XLA Ops:
  0.6 34.8 %copy-start = (f32[16,23]{1,0:T(8,128)S(1)}, f32[16,23]{1,0:T(8,128)}, u32[]{:S(2)}) copy-start(f32[16,23]{1,0:T(8,128)} %param.8) | copy-start | bytes 4420
  4.5 12.8 %all-to-all-start = ((bf16[8,2,2112]{2,1,0:T(2,128)(2,1)}), bf16[8,2,2112]{2,1,0:T(2,128)(2,1)S(1)}, u32[]{:S(2)}, u32[]{:S(2)}) async-start(bf16[8,2,2112]{2,1,0:T(2,128)(2,1)} %reshape.596), calls=%async_computation | async-start | bytes 139264 | tf_op jit(solution)/shard_map/all_to_all | solution.py:138
  13.3 23.0 %copy-start.2 = (f32[64,1,32]{0,2,1:T(8,128)}, f32[64,1,32]{0,2,1:T(8,128)S(1)}, u32[]{:S(2)}) copy-start(f32[64,1,32]{0,2,1:T(8,128)S(1)} %get-tuple-element.27) | copy-start | bytes 24580
  13.3 23.0 %copy-start.4 = (f32[64,1,32]{0,2,1:T(8,128)}, f32[64,1,32]{0,2,1:T(8,128)S(1)}, u32[]{:S(2)}) copy-start(f32[64,1,32]{0,2,1:T(8,128)S(1)} %get-tuple-element.30) | copy-start | bytes 24580
  13.3 23.0 %copy-start.9 = (bf16[64,1,32]{0,2,1:T(8,128)(2,1)}, bf16[64,1,32]{0,2,1:T(8,128)(2,1)S(1)}, u32[]{:S(2)}) copy-start(bf16[64,1,32]{0,2,1:T(8,128)(2,1)S(1)} %get-tuple-element.28) | copy-start | bytes 12292
  14.4 21.9 %copy-start.17 = (f32[1,1024]{1,0:T(1,128)}, f32[1,1024]{1,0:T(1,128)S(1)}, u32[]{:S(2)}) copy-start(f32[1,1024]{1,0:T(1,128)S(1)} %fusion.29) | copy-start | bytes 12292
  17.4 29.7 %all-to-all-start.1 = ((f32[64,1,768]{2,1,0:T(1,128)}), f32[64,1,768]{2,1,0:T(1,128)S(1)}, u32[]{:S(2)}, u32[]{:S(2)}) async-start(f32[64,1,768]{2,1,0:T(1,128)} %reshape.598), calls=%async_computation.1 | async-start | bytes 393216 | tf_op jit(solution)/shard_map/all_to_all | solution.py:146
  36.4 0.6 copy-start.6
  36.4 15.5 %copy-start.18 = (f32[1,1024]{1,0:T(1,128)S(1)}, f32[1,1024]{1,0:T(1,128)}, u32[]{:S(2)}) copy-start(f32[1,1024]{1,0:T(1,128)} %copy-done.17) | copy-start | bytes 12292
  41.1 7.9 %copy-start.3 = (f32[64,1,32]{0,2,1:T(8,128)S(1)}, f32[64,1,32]{0,2,1:T(8,128)}, u32[]{:S(2)}) copy-start(f32[64,1,32]{0,2,1:T(8,128)} %copy-done.2) | copy-start | bytes 24580
  41.1 7.9 %copy-start.5 = (f32[64,1,32]{0,2,1:T(8,128)S(1)}, f32[64,1,32]{0,2,1:T(8,128)}, u32[]{:S(2)}) copy-start(f32[64,1,32]{0,2,1:T(8,128)} %copy-done.4) | copy-start | bytes 24580
  41.1 10.8 %copy-start.7 = (f32[8,1024]{1,0:T(8,128)S(1)}, f32[8,1024]{1,0:T(8,128)}, u32[]{:S(2)}) copy-start(f32[8,1024]{1,0:T(8,128)} %copy-done.6) | copy-start | bytes 98308
  43.2 15.2 %copy-start.13 = (bf16[1,32,2,64]{3,1,0,2:T(8,128)(2,1)S(1)}, bf16[1,32,2,64]{3,1,0,2:T(8,128)(2,1)}, u32[]{:S(2)}) copy-start(bf16[1,32,2,64]{3,1,0,2:T(8,128)(2,1)} %get-tuple-element.24) | copy-start | bytes 24580
  43.3 15.2 %copy-start.14 = (bf16[1,32,2,64]{3,1,0,2:T(8,128)(2,1)S(1)}, bf16[1,32,2,64]{3,1,0,2:T(8,128)(2,1)}, u32[]{:S(2)}) copy-start(bf16[1,32,2,64]{3,1,0,2:T(8,128)(2,1)} %get-tuple-element.25) | copy-start | bytes 24580
  43.3 15.2 %copy-start.15 = (bf16[1,32,64]{2,1,0:T(8,128)(2,1)S(1)}, bf16[1,32,64]{2,1,0:T(8,128)(2,1)}, u32[]{:S(2)}) copy-start(bf16[1,32,64]{2,1,0:T(8,128)(2,1)} %fusion.80) | copy-start | bytes 12292
  43.3 15.2 %copy-start.16 = (bf16[1,32,64]{2,1,0:T(8,128)(2,1)S(1)}, bf16[1,32,64]{2,1,0:T(8,128)(2,1)}, u32[]{:S(2)}) copy-start(bf16[1,32,64]{2,1,0:T(8,128)(2,1)} %cosine_convert_fusion.1) | copy-start | bytes 12292
  75.3 17.5 %copy-start.10 = (bf16[64,1,32]{0,2,1:T(8,128)(2,1)S(1)}, bf16[64,1,32]{0,2,1:T(8,128)(2,1)}, u32[]{:S(2)}) copy-start(bf16[64,1,32]{0,2,1:T(8,128)(2,1)} %copy-done.9) | copy-start | bytes 12292
  75.3 17.5 %copy-start.11 = (bf16[64,1,2,32]{0,3,2,1:T(8,128)(2,1)S(1)}, bf16[64,1,2,32]{0,3,2,1:T(8,128)(2,1)}, u32[]{:S(2)}) copy-start(bf16[64,1,2,32]{0,3,2,1:T(8,128)(2,1)} %get-tuple-element.20) | copy-start | bytes 24580
  75.3 17.5 %copy-start.12 = (bf16[64,1,2,32]{0,3,2,1:T(8,128)(2,1)S(1)}, bf16[64,1,2,32]{0,3,2,1:T(8,128)(2,1)}, u32[]{:S(2)}) copy-start(bf16[64,1,2,32]{0,3,2,1:T(8,128)(2,1)} %get-tuple-element.21) | copy-start | bytes 24580
  86.8 35.4 %copy-start.8 = (f32[12,8]{1,0:T(8,128)}, f32[12,8]{1,0:T(8,128)S(1)}, u32[]{:S(2)}) copy-start(f32[12,8]{1,0:T(8,128)S(1)} %fusion.1) | copy-start | bytes 1156
  87.5 47.4 %all-to-all-start.2 = ((f32[8,2,8]{2,1,0:T(2,128)}), f32[8,2,8]{2,1,0:T(2,128)}, u32[]{:S(2)}, u32[]{:S(2)}) async-start(f32[8,2,8]{2,1,0:T(2,128)} %broadcast_in_dim.11), calls=%async_computation.2 | async-start | bytes 16384 | tf_op jit(solution)/shard_map/all_to_all | solution.py:164
  122.2 47.1 %copy-start.1 = (f32[16,23]{1,0:T(8,128)S(1)}, f32[16,23]{1,0:T(8,128)}, u32[]{:S(2)}) copy-start(f32[16,23]{1,0:T(8,128)} %param.8) | copy-start | bytes 4420
  140.6 25.7 %all-to-all-start.3 = ((f32[64,1,576]{2,1,0:T(1,128)}), f32[64,1,576]{2,1,0:T(1,128)S(1)}, u32[]{:S(2)}, u32[]{:S(2)}) async-start(f32[64,1,576]{2,1,0:T(1,128)} %reshape.600), calls=%async_computation.3 | async-start | bytes 327680 | tf_op jit(solution)/shard_map/all_to_all | solution.py:176

commit v9 on v8

--- a/solution.py
+++ b/solution.py
@@ -145,7 +145,7 @@
     spread = jnp.broadcast_to(references[None], (rows,) + references.shape)
     pieces = lax.all_to_all(spread, "dom", 0, 0, tiled=True)
     maps = jnp.transpose(pieces, (1, 0, 2)).reshape(references.shape[0], -1)
-    complete_input = fourier_input.astype(jnp.float32)
+    complete_input = lax.reduce_precision(fourier_input.astype(jnp.float32), 8, 7)
     contrast_transfer, noise_deviation = spectra(ctf_profile, noise_power, block_labels)
     abstract_value = (
         complete_input * (contrast_transfer / noise_deviation[None, :])[:, None, None, :]

time: 170 us -> 170 us (level)
  no operation moved by 1% of the time
where the time goes in v9:
time: 170 us; the launch traced here: 169 us
  matrix products  56.4 us (33%)
  starting transfers between devices  40.9 us (24%)
  other arithmetic  38.5 us (23%)
  local copies, waits for them, and re-layouts  18.8 us (11%)
  waiting for transfers between devices  12.9 us (8%)
  between operations  1.85 us (1%)
    dot_general x3, matrix products, product(): return jnp.einsum(form, left, right, preferred_element_type=jnp.float32)  50.4 us
    all_to_all x1, starting transfers between devices, shards(): pieces = lax.all_to_all(spread, 'dom', 0, 0, tiled=True)  16.4 us
    all_to_all x1, starting transfers between devices, shards(): owned = jnp.sum(lax.all_to_all(parts, 'dom', 0, 0, tiled=True), axis=0)  12.7 us
    all_to_all x1, waiting for transfers between devices, shards(): owned = jnp.sum(lax.all_to_all(parts, 'dom', 0, 0, tiled=True), axis=0)  12.5 us
    reduce_sum x1, other arithmetic, class_step(): total = jnp.sum(expo, axis=(2, 3, 4))  11.5 us
    reduce_sum x1, other arithmetic, class_step(): jnp.sum(yval[None, :, :, 0] * what[:, :, :, 0] - yval[None, :, :, 1] * wh...  11.2 us
    all_to_all x1, starting transfers between devices, shards(): lax.all_to_all(jnp.broadcast_to(payload, (peers,) + payload.shape[1:]), '...  6.65 us
    another operation x1, other arithmetic  6.34 us
  transfers between devices with their start and end apart: 4, of which 2 were waited for; matrix products, arithmetic and copies ran while one was open for 36% of the time, Pallas kernels for 0%

profile of v9, /device:TPU:1, one launch (start us, length us, event | category | flops | bytes accessed | tf_op | source)
XLA Modules:
  0.0 169.3 jit_solution(15063348308462017882)
XLA Ops:
  1.3 0.8 reshape.558
  2.3 0.5 broadcast.692
  2.8 1.0 reduce.7
  3.8 0.7 reshape.595
  4.5 6.6 %all-to-all-start = ((bf16[8,2,2112]{2,1,0:T(2,128)(2,1)}), bf16[8,2,2112]{2,1,0:T(2,128)(2,1)S(1)}, u32[]{:S(2)}, u32[]{:S(2)}) async-start(bf16[8,2,2112]{2,1,0:T(2,128)(2,1)} %reshape.595), calls=%async_computation | async-start | bytes 139264 | tf_op jit(solution)/shard_map/all_to_all | solution.py:138
  11.2 0.7 fusion.80
  12.0 0.7 cosine_convert_fusion.1
  12.7 0.1 fusion.91
  12.8 0.1 fusion.90
  13.0 0.2 sine_convert_fusion
  13.2 0.2 fusion.85
  13.6 0.8 fusion.29
  14.4 0.6 maximum_bitcast_fusion.15
  15.1 0.6 fusion.79
  15.7 0.7 broadcast_in_dim.10
  16.4 0.9 reshape.597
  17.4 16.4 %all-to-all-start.1 = ((f32[64,1,768]{2,1,0:T(1,128)}), f32[64,1,768]{2,1,0:T(1,128)S(1)}, u32[]{:S(2)}, u32[]{:S(2)}) async-start(f32[64,1,768]{2,1,0:T(1,128)} %reshape.597), calls=%async_computation.1 | async-start | bytes 393216 | tf_op jit(solution)/shard_map/all_to_all | solution.py:146
  34.0 0.2 reshape.559
  34.2 0.2 stack.123
  34.4 0.1 rev.22
  34.6 0.1 rev.25
  34.7 0.1 rev.23
  34.8 0.1 copy.88
  35.0 0.1 copy.90
  35.1 0.1 copy.91
  35.4 0.2 fusion.88
  35.6 0.8 broadcast_divide_fusion
  36.7 0.3 copy-done.6
  37.0 4.1 %broadcast_multiply_fusion = (f32[8,8,2,32,32]{4,3,1,0,2:T(8,128)}, f32[8,8,2,32,32]{4,3,1,0,2:T(8,128)S(1)}) fusion(f32[8,32,32]{2,1,0:T(8,128)S(1)} %mul.401, bf16[8,8,64,64]{3,2,1,0:T(8,128)(2,1)S(1)} %bitcast_dynamic-update-slice_fusion.2, f32[64,1,32]{0,2,1:T(8,128)} %copy-done.2, f32[64,1,32]{0,2,1:T(8,128)} %copy-done.4, ...), kind=kOutput, calls=%fused_computation.38 | convolution fusion | flops 67919872 | bytes 1654784 | tf_op jit(solution)/shard_map/nrydb,ydca->nrcab/dot_general | solution.py:49
  41.0 1.0 reduce_precision.13
  42.0 0.8 broadcast_multiply_fusion.1
  42.9 0.3 mul.413
  43.3 0.3 mul.418
  43.6 3.1 %slice_bitcast_fusion.3 = (f32[8,8,32,32]{3,2,1,0:T(8,128)}, f32[8,8,32,32]{3,2,1,0:T(8,128)}) fusion(f32[8,8,2,32,32]{4,3,1,0,2:T(8,128)} %get-tuple-element.37), kind=kLoop, calls=%fused_computation.36 | loop fusion | bytes 1048576 | tf_op jit(solution)/shard_map/mul | solution.py:116
  46.7 0.4 all-to-all-done.1
  47.1 0.6 broadcast.693
  47.7 1.2 reduce.8
  49.0 1.3 convolution_bitcast_fusion.1
  50.2 1.1 convolution_bitcast_fusion
  51.3 0.2 reshape.586
  51.8 0.2 convolution_multiply_fusion
  52.1 6.3 %add_convert_fusion = (bf16[12,8,8,1,32,32]{5,4,3,2,1,0:T(8,128)(2,1)}, bf16[12,8,8,1,32,32]{5,4,3,2,1,0:T(8,128)(2,1)}) fusion(f32[12,32,32]{2,1,0:T(8,128)S(1)} %mul.420, f32[8,8,32,32]{3,2,1,0:T(8,128)S(1)} %mul.418, f32[12,32,32]{2,1,0:T(8,128)S(1)} %mul.415, f32[8,8,32,32]{3,2,1,0:T(8,128)S(1)} %mul.413), kind=kLoop, calls=%fused_computation.26 | loop fusion | flops 6291456 | bytes 3768320 | tf_op jit(solution)/shard_map/convert.2
  58.4 16.9 %bitcast_reduce_fusion = (f32[12,8]{1,0:T(8,128)S(1)}, f32[64,12,8,8,64,1]{4,0,5,3,2,1:T(8,128)}) fusion(f32[12,8]{1,0:T(8,128)S(1)} %copy.99, bf16[12,8,8,1,32,32]{5,4,3,2,1,0:T(8,128)(2,1)} %get-tuple-element.11, bf16[12,8,8,1,32,32]{5,4,3,2,1,0:T(8,128)(2,1)} %get-tuple-element.10, bf16[1,32,2,64]{3,1,0,2:T(8,128)(2,1)S(1)} %copy-done.14, ...), kind=kOutput, calls=%fused_computation.2 | convolution fusion | flops 821084032 | bytes 15753984 | tf_op jit(solution)/shard_map/knradx,day->knyrx/dot_general | solution.py:49
  75.3 11.5 %fusion.1 = f32[12,8]{1,0:T(8,128)S(1)} fusion(f32[64,12,8,8,64,1]{4,0,5,3,2,1:T(8,128)} %get-tuple-element.36, f32[12,8]{1,0:T(8,128)S(1)} %get-tuple-element.4, f32[12,8]{1,0:T(8,128)S(1)} %copy.99), kind=kLoop, calls=%fused_computation.7 | loop fusion | flops 9437088 | bytes 12584064 | tf_op jit(solution)/shard_map/reduce_sum | solution.py:110
  86.9 0.6 broadcast_in_dim.11
  87.5 5.2 %all-to-all-start.2 = ((f32[8,2,8]{2,1,0:T(2,128)}), f32[8,2,8]{2,1,0:T(2,128)}, u32[]{:S(2)}, u32[]{:S(2)}) async-start(f32[8,2,8]{2,1,0:T(2,128)} %broadcast_in_dim.11), calls=%async_computation.2 | async-start | bytes 16384 | tf_op jit(solution)/shard_map/all_to_all | solution.py:164
  92.8 29.4 %convert_bitcast_fusion = f32[12,8,8,2,32,32]{5,4,2,1,0,3:T(8,128)} fusion(f32[64,12,8,8,64,1]{4,0,5,3,2,1:T(8,128)} %get-tuple-element.36, f32[12,8]{1,0:T(8,128)S(1)} %get-tuple-element.4, f32[12,8]{1,0:T(8,128)S(1)} %copy.99, bf16[64,1,32]{0,2,1:T(8,128)(2,1)S(1)} %get-tuple-element.26, bf16[64,1,32]{0,2,1:T(8,128)(2,1)S(1)} %copy-done.10, ...), kind=kOutput, calls=%fused_computation.6 | convolution fusion | flops 821059584 | bytes 18899712 | tf_op jit(solution)/shard_map/knrydb,ydca->knrcab/dot_general | solution.py:49
  122.2 11.2 %subtract_reduce_fusion = (f32[12,8,32,32]{3,2,1,0:T(8,128)S(1)}, f32[12,8,32,32]{3,2,1,0:T(8,128)S(1)}) fusion(f32[12,8,8,2,32,32]{5,4,2,1,0,3:T(8,128)} %convert_bitcast_fusion, f32[8,8,32,32]{3,2,1,0:T(8,128)} %get-tuple-element.13, f32[8,8,32,32]{3,2,1,0:T(8,128)} %get-tuple-element.12), kind=kLoop, calls=%fused_computation.21 | loop fusion | flops 6094848 | bytes 7602176 | tf_op jit(solution)/shard_map/reduce_sum | solution.py:115
  133.4 0.7 stack.144
  134.2 0.7 stack.145
  134.9 0.8 fusion.104
  135.7 1.0 fusion.48
  136.7 0.2 concatenate.19
  136.9 0.8 fusion.25
  137.7 0.3 concatenate.18
  138.1 0.8 copy.177
  139.0 1.6 reshape.599
  140.6 12.7 %all-to-all-start.3 = ((f32[64,1,576]{2,1,0:T(1,128)}), f32[64,1,576]{2,1,0:T(1,128)S(1)}, u32[]{:S(2)}, u32[]{:S(2)}) async-start(f32[64,1,576]{2,1,0:T(1,128)} %reshape.599), calls=%async_computation.3 | async-start | bytes 327680 | tf_op jit(solution)/shard_map/all_to_all | solution.py:176
  153.3 0.5 log_add_fusion
  153.8 12.5 %all-to-all-done.3 = f32[64,1,576]{2,1,0:T(1,128)S(1)} async-done(((f32[64,1,576]{2,1,0:T(1,128)}), f32[64,1,576]{2,1,0:T(1,128)S(1)}, u32[]{:S(2)}, u32[]{:S(2)}) %all-to-all-start.3) | async-done | bytes 147488 | tf_op jit(solution)/shard_map/all_to_all | solution.py:176
  166.3 1.1 reduce.9
  167.4 1.0 reshape.600
  168.4 0.3 bitcast_reduce_fusion.1
  168.7 0.6 slice_divide_fusion
  (80 shorter events, 2.0 us)
Async XLA Ops:
  0.6 34.8 %copy-start = (f32[16,23]{1,0:T(8,128)S(1)}, f32[16,23]{1,0:T(8,128)}, u32[]{:S(2)}) copy-start(f32[16,23]{1,0:T(8,128)} %param.8) | copy-start | bytes 4420
  4.5 12.8 %all-to-all-start = ((bf16[8,2,2112]{2,1,0:T(2,128)(2,1)}), bf16[8,2,2112]{2,1,0:T(2,128)(2,1)S(1)}, u32[]{:S(2)}, u32[]{:S(2)}) async-start(bf16[8,2,2112]{2,1,0:T(2,128)(2,1)} %reshape.595), calls=%async_computation | async-start | bytes 139264 | tf_op jit(solution)/shard_map/all_to_all | solution.py:138
  13.3 23.0 %copy-start.2 = (f32[64,1,32]{0,2,1:T(8,128)}, f32[64,1,32]{0,2,1:T(8,128)S(1)}, u32[]{:S(2)}) copy-start(f32[64,1,32]{0,2,1:T(8,128)S(1)} %get-tuple-element.27) | copy-start | bytes 24580
  13.3 23.0 %copy-start.4 = (f32[64,1,32]{0,2,1:T(8,128)}, f32[64,1,32]{0,2,1:T(8,128)S(1)}, u32[]{:S(2)}) copy-start(f32[64,1,32]{0,2,1:T(8,128)S(1)} %get-tuple-element.30) | copy-start | bytes 24580
  13.3 23.0 %copy-start.9 = (bf16[64,1,32]{0,2,1:T(8,128)(2,1)}, bf16[64,1,32]{0,2,1:T(8,128)(2,1)S(1)}, u32[]{:S(2)}) copy-start(bf16[64,1,32]{0,2,1:T(8,128)(2,1)S(1)} %get-tuple-element.28) | copy-start | bytes 12292
  14.4 21.9 %copy-start.17 = (f32[1,1024]{1,0:T(1,128)}, f32[1,1024]{1,0:T(1,128)S(1)}, u32[]{:S(2)}) copy-start(f32[1,1024]{1,0:T(1,128)S(1)} %fusion.29) | copy-start | bytes 12292
  17.4 29.7 %all-to-all-start.1 = ((f32[64,1,768]{2,1,0:T(1,128)}), f32[64,1,768]{2,1,0:T(1,128)S(1)}, u32[]{:S(2)}, u32[]{:S(2)}) async-start(f32[64,1,768]{2,1,0:T(1,128)} %reshape.597), calls=%async_computation.1 | async-start | bytes 393216 | tf_op jit(solution)/shard_map/all_to_all | solution.py:146
  36.4 0.6 copy-start.6
  36.4 15.5 %copy-start.18 = (f32[1,1024]{1,0:T(1,128)S(1)}, f32[1,1024]{1,0:T(1,128)}, u32[]{:S(2)}) copy-start(f32[1,1024]{1,0:T(1,128)} %copy-done.17) | copy-start | bytes 12292
  41.0 7.9 %copy-start.3 = (f32[64,1,32]{0,2,1:T(8,128)S(1)}, f32[64,1,32]{0,2,1:T(8,128)}, u32[]{:S(2)}) copy-start(f32[64,1,32]{0,2,1:T(8,128)} %copy-done.2) | copy-start | bytes 24580
  41.0 7.9 %copy-start.5 = (f32[64,1,32]{0,2,1:T(8,128)S(1)}, f32[64,1,32]{0,2,1:T(8,128)}, u32[]{:S(2)}) copy-start(f32[64,1,32]{0,2,1:T(8,128)} %copy-done.4) | copy-start | bytes 24580
  41.0 10.8 %copy-start.7 = (f32[8,1024]{1,0:T(8,128)S(1)}, f32[8,1024]{1,0:T(8,128)}, u32[]{:S(2)}) copy-start(f32[8,1024]{1,0:T(8,128)} %copy-done.6) | copy-start | bytes 98308
  43.2 15.2 %copy-start.13 = (bf16[1,32,2,64]{3,1,0,2:T(8,128)(2,1)S(1)}, bf16[1,32,2,64]{3,1,0,2:T(8,128)(2,1)}, u32[]{:S(2)}) copy-start(bf16[1,32,2,64]{3,1,0,2:T(8,128)(2,1)} %get-tuple-element.24) | copy-start | bytes 24580
  43.2 15.2 %copy-start.14 = (bf16[1,32,2,64]{3,1,0,2:T(8,128)(2,1)S(1)}, bf16[1,32,2,64]{3,1,0,2:T(8,128)(2,1)}, u32[]{:S(2)}) copy-start(bf16[1,32,2,64]{3,1,0,2:T(8,128)(2,1)} %get-tuple-element.25) | copy-start | bytes 24580
  43.2 15.2 %copy-start.15 = (bf16[1,32,64]{2,1,0:T(8,128)(2,1)S(1)}, bf16[1,32,64]{2,1,0:T(8,128)(2,1)}, u32[]{:S(2)}) copy-start(bf16[1,32,64]{2,1,0:T(8,128)(2,1)} %fusion.80) | copy-start | bytes 12292
  43.3 15.2 %copy-start.16 = (bf16[1,32,64]{2,1,0:T(8,128)(2,1)S(1)}, bf16[1,32,64]{2,1,0:T(8,128)(2,1)}, u32[]{:S(2)}) copy-start(bf16[1,32,64]{2,1,0:T(8,128)(2,1)} %cosine_convert_fusion.1) | copy-start | bytes 12292
  75.3 17.5 %copy-start.10 = (bf16[64,1,32]{0,2,1:T(8,128)(2,1)S(1)}, bf16[64,1,32]{0,2,1:T(8,128)(2,1)}, u32[]{:S(2)}) copy-start(bf16[64,1,32]{0,2,1:T(8,128)(2,1)} %copy-done.9) | copy-start | bytes 12292
  75.3 17.5 %copy-start.11 = (bf16[64,1,2,32]{0,3,2,1:T(8,128)(2,1)S(1)}, bf16[64,1,2,32]{0,3,2,1:T(8,128)(2,1)}, u32[]{:S(2)}) copy-start(bf16[64,1,2,32]{0,3,2,1:T(8,128)(2,1)} %get-tuple-element.20) | copy-start | bytes 24580
  75.3 17.5 %copy-start.12 = (bf16[64,1,2,32]{0,3,2,1:T(8,128)(2,1)S(1)}, bf16[64,1,2,32]{0,3,2,1:T(8,128)(2,1)}, u32[]{:S(2)}) copy-start(bf16[64,1,2,32]{0,3,2,1:T(8,128)(2,1)} %get-tuple-element.21) | copy-start | bytes 24580
  86.8 35.4 %copy-start.8 = (f32[12,8]{1,0:T(8,128)}, f32[12,8]{1,0:T(8,128)S(1)}, u32[]{:S(2)}) copy-start(f32[12,8]{1,0:T(8,128)S(1)} %fusion.1) | copy-start | bytes 1156
  87.5 47.4 %all-to-all-start.2 = ((f32[8,2,8]{2,1,0:T(2,128)}), f32[8,2,8]{2,1,0:T(2,128)}, u32[]{:S(2)}, u32[]{:S(2)}) async-start(f32[8,2,8]{2,1,0:T(2,128)} %broadcast_in_dim.11), calls=%async_computation.2 | async-start | bytes 16384 | tf_op jit(solution)/shard_map/all_to_all | solution.py:164
  122.2 47.1 %copy-start.1 = (f32[16,23]{1,0:T(8,128)S(1)}, f32[16,23]{1,0:T(8,128)}, u32[]{:S(2)}) copy-start(f32[16,23]{1,0:T(8,128)} %param.8) | copy-start | bytes 4420
  140.6 25.7 %all-to-all-start.3 = ((f32[64,1,576]{2,1,0:T(1,128)}), f32[64,1,576]{2,1,0:T(1,128)S(1)}, u32[]{:S(2)}, u32[]{:S(2)}) async-start(f32[64,1,576]{2,1,0:T(1,128)} %reshape.599), calls=%async_computation.3 | async-start | bytes 327680 | tf_op jit(solution)/shard_map/all_to_all | solution.py:176

commit v10 on v9

--- a/solution.py
+++ b/solution.py
@@ -168,8 +168,9 @@
     mass = jnp.sum(jnp.exp(summary[:, 0] - top[None, :]) * summary[:, 1], axis=0)
     log_evidence = top + jnp.log(mass)
     share = jnp.exp(peaks - top[None, :]) / mass[None, :]
-    numer = jnp.einsum("kp,kpcf->ckf", share, projs, precision=HIGHEST)
-    denom = jnp.dot(share * totals, contrast_transfer * contrast_transfer, precision=HIGHEST)
+    numer = jnp.transpose(jnp.sum(share[:, :, None, None] * projs, axis=1), (1, 0, 2))
+    weight = share * totals
+    denom = jnp.sum(weight[:, :, None] * (contrast_transfer * contrast_transfer)[None], axis=1)
     stacked = jnp.concatenate([numer, denom[None]], axis=0)
     lanes = stacked.shape[2] // rows
     parts = jnp.moveaxis(stacked.reshape(3, stacked.shape[1], rows, lanes), 2, 0)

time: 170 us -> 170 us (level)
  other arithmetic: 38.5 us -> 40.5 us
    dot_general x2 -> x0, matrix products: 1.76 us -> none  [the longest x1 0.98 us: shards(): jnp.dot(share * totals, contrast_transfer * contrast_transfer, precision=...]
where the time goes in v10:
time: 170 us; the launch traced here: 169 us
  matrix products  54.7 us (32%)
  starting transfers between devices  40.9 us (24%)
  other arithmetic  40.5 us (24%)
  local copies, waits for them, and re-layouts  18.8 us (11%)
  waiting for transfers between devices  12.8 us (8%)
  between operations  1.82 us (1%)
    dot_general x3, matrix products, product(): return jnp.einsum(form, left, right, preferred_element_type=jnp.float32)  50.4 us
    all_to_all x1, starting transfers between devices, shards(): pieces = lax.all_to_all(spread, 'dom', 0, 0, tiled=True)  16.3 us
    all_to_all x1, starting transfers between devices, shards(): owned = jnp.sum(lax.all_to_all(parts, 'dom', 0, 0, tiled=True), axis=0)  12.6 us
    all_to_all x1, waiting for transfers between devices, shards(): owned = jnp.sum(lax.all_to_all(parts, 'dom', 0, 0, tiled=True), axis=0)  12.5 us
    reduce_sum x1, other arithmetic, class_step(): total = jnp.sum(expo, axis=(2, 3, 4))  11.5 us
    reduce_sum x1, other arithmetic, class_step(): jnp.sum(yval[None, :, :, 0] * what[:, :, :, 0] - yval[None, :, :, 1] * wh...  11.2 us
    all_to_all x1, starting transfers between devices, shards(): lax.all_to_all(jnp.broadcast_to(payload, (peers,) + payload.shape[1:]), '...  6.65 us
    another operation x1, other arithmetic  6.34 us
  transfers between devices with their start and end apart: 4, of which 2 were waited for; matrix products, arithmetic and copies ran while one was open for 36% of the time, Pallas kernels for 0%

profile of v10, /device:TPU:1, one launch (start us, length us, event | category | flops | bytes accessed | tf_op | source)
XLA Modules:
  0.0 169.5 jit_solution(6593243938569261176)
XLA Ops:
  1.3 0.8 reshape.561
  2.3 0.5 broadcast.695
  2.8 1.0 reduce.7
  3.8 0.7 reshape.596
  4.5 6.6 %all-to-all-start = ((bf16[8,2,2112]{2,1,0:T(2,128)(2,1)}), bf16[8,2,2112]{2,1,0:T(2,128)(2,1)S(1)}, u32[]{:S(2)}, u32[]{:S(2)}) async-start(bf16[8,2,2112]{2,1,0:T(2,128)(2,1)} %reshape.596), calls=%async_computation | async-start | bytes 139264 | tf_op jit(solution)/shard_map/all_to_all | solution.py:138
  11.2 0.7 fusion.76
  12.0 0.1 fusion.84
  12.1 0.1 fusion.85
  12.3 0.7 cosine_convert_fusion.1
  13.0 0.2 sine_convert_fusion
  13.2 0.2 fusion.80
  13.6 0.8 fusion.28
  14.4 0.6 maximum_bitcast_fusion.14
  15.1 0.6 fusion.75
  15.7 0.7 broadcast_in_dim.10
  16.4 0.9 reshape.598
  17.4 16.3 %all-to-all-start.1 = ((f32[64,1,768]{2,1,0:T(1,128)}), f32[64,1,768]{2,1,0:T(1,128)S(1)}, u32[]{:S(2)}, u32[]{:S(2)}) async-start(f32[64,1,768]{2,1,0:T(1,128)} %reshape.598), calls=%async_computation.1 | async-start | bytes 393216 | tf_op jit(solution)/shard_map/all_to_all | solution.py:146
  34.0 0.2 reshape.562
  34.2 0.2 stack.124
  34.4 0.1 rev.22
  34.6 0.1 rev.25
  34.7 0.1 rev.23
  35.0 0.1 copy.89
  35.1 0.1 copy.90
  35.4 0.2 fusion.82
  35.6 0.8 broadcast_divide_fusion
  36.7 0.3 copy-done.17
  37.0 4.1 %broadcast_multiply_fusion = (f32[8,8,2,32,32]{4,3,1,0,2:T(8,128)}, f32[8,8,2,32,32]{4,3,1,0,2:T(8,128)S(1)}) fusion(f32[8,32,32]{2,1,0:T(8,128)S(1)} %mul.452, bf16[8,8,64,64]{3,2,1,0:T(8,128)(2,1)S(1)} %bitcast_dynamic-update-slice_fusion.2, f32[64,1,32]{0,2,1:T(8,128)} %copy-done.2, f32[64,1,32]{0,2,1:T(8,128)} %copy-done.4, ...), kind=kOutput, calls=%fused_computation.38 | convolution fusion | flops 67919872 | bytes 1654784 | tf_op jit(solution)/shard_map/nrydb,ydca->nrcab/dot_general | solution.py:49
  41.1 1.0 reduce_precision.13
  42.0 0.8 broadcast_multiply_fusion.1
  42.9 0.3 mul.429
  43.3 0.3 mul.434
  43.6 3.1 %slice_bitcast_fusion.3 = (f32[8,8,32,32]{3,2,1,0:T(8,128)}, f32[8,8,32,32]{3,2,1,0:T(8,128)}) fusion(f32[8,8,2,32,32]{4,3,1,0,2:T(8,128)} %get-tuple-element.40), kind=kLoop, calls=%fused_computation.36 | loop fusion | bytes 1048576 | tf_op jit(solution)/shard_map/mul | solution.py:116
  46.7 0.4 all-to-all-done.1
  47.1 0.6 broadcast.696
  47.7 1.2 reduce.8
  49.0 1.3 convolution_bitcast_fusion.1
  50.3 1.1 convolution_bitcast_fusion
  51.3 0.2 reshape.587
  51.8 0.2 convolution_multiply_fusion
  52.1 6.3 %add_convert_fusion = (bf16[12,8,8,1,32,32]{5,4,3,2,1,0:T(8,128)(2,1)}, bf16[12,8,8,1,32,32]{5,4,3,2,1,0:T(8,128)(2,1)}) fusion(f32[12,32,32]{2,1,0:T(8,128)S(1)} %mul.436, f32[8,8,32,32]{3,2,1,0:T(8,128)S(1)} %mul.434, f32[12,32,32]{2,1,0:T(8,128)S(1)} %mul.431, f32[8,8,32,32]{3,2,1,0:T(8,128)S(1)} %mul.429), kind=kLoop, calls=%fused_computation.26 | loop fusion | flops 6291456 | bytes 3768320 | tf_op jit(solution)/shard_map/convert.2
  58.4 16.8 %bitcast_reduce_fusion = (f32[12,8]{1,0:T(8,128)S(1)}, f32[64,12,8,8,64,1]{4,0,5,3,2,1:T(8,128)}) fusion(f32[12,8]{1,0:T(8,128)S(1)} %copy.98, bf16[12,8,8,1,32,32]{5,4,3,2,1,0:T(8,128)(2,1)} %get-tuple-element.13, bf16[12,8,8,1,32,32]{5,4,3,2,1,0:T(8,128)(2,1)} %get-tuple-element.12, bf16[1,32,2,64]{3,1,0,2:T(8,128)(2,1)S(1)} %copy-done.14, ...), kind=kOutput, calls=%fused_computation.2 | convolution fusion | flops 821084032 | bytes 15753984 | tf_op jit(solution)/shard_map/knradx,day->knyrx/dot_general | solution.py:49
  75.3 11.5 %fusion.2 = f32[12,8]{1,0:T(8,128)S(1)} fusion(f32[64,12,8,8,64,1]{4,0,5,3,2,1:T(8,128)} %get-tuple-element.39, f32[12,8]{1,0:T(8,128)S(1)} %get-tuple-element.4, f32[12,8]{1,0:T(8,128)S(1)} %copy.98), kind=kLoop, calls=%fused_computation.8 | loop fusion | flops 9437088 | bytes 12584064 | tf_op jit(solution)/shard_map/reduce_sum | solution.py:110
  86.9 0.6 broadcast_in_dim.11
  87.5 5.3 %all-to-all-start.2 = ((f32[8,2,8]{2,1,0:T(2,128)}), f32[8,2,8]{2,1,0:T(2,128)}, u32[]{:S(2)}, u32[]{:S(2)}) async-start(f32[8,2,8]{2,1,0:T(2,128)} %broadcast_in_dim.11), calls=%async_computation.2 | async-start | bytes 16384 | tf_op jit(solution)/shard_map/all_to_all | solution.py:164
  92.8 29.4 %convert_bitcast_fusion = f32[12,8,8,2,32,32]{5,4,2,1,0,3:T(8,128)} fusion(f32[64,12,8,8,64,1]{4,0,5,3,2,1:T(8,128)} %get-tuple-element.39, f32[12,8]{1,0:T(8,128)S(1)} %get-tuple-element.4, f32[12,8]{1,0:T(8,128)S(1)} %copy.98, bf16[64,1,32]{0,2,1:T(8,128)(2,1)S(1)} %copy-done.8, bf16[64,1,32]{0,2,1:T(8,128)(2,1)S(1)} %copy-done.10, ...), kind=kOutput, calls=%fused_computation.6 | convolution fusion | flops 821059584 | bytes 18899712 | tf_op jit(solution)/shard_map/knrydb,ydca->knrcab/dot_general | solution.py:49
  122.3 11.2 %subtract_reduce_fusion = (f32[12,8,32,32]{3,2,1,0:T(8,128)S(1)}, f32[12,8,32,32]{3,2,1,0:T(8,128)S(1)}) fusion(f32[12,8,8,2,32,32]{5,4,2,1,0,3:T(8,128)} %convert_bitcast_fusion, f32[8,8,32,32]{3,2,1,0:T(8,128)} %get-tuple-element.15, f32[8,8,32,32]{3,2,1,0:T(8,128)} %get-tuple-element.14), kind=kLoop, calls=%fused_computation.21 | loop fusion | flops 6094848 | bytes 7602176 | tf_op jit(solution)/shard_map/reduce_sum | solution.py:115
  133.5 0.7 stack.147
  134.2 0.7 stack.148
  134.9 0.8 fusion.99
  135.8 0.7 fusion.96
  136.5 0.9 multiply_reduce_fusion
  137.4 0.2 concatenate.19
  137.6 0.3 fusion.25
  137.9 0.3 concatenate.18
  138.3 0.8 copy.167
  139.1 1.6 reshape.600
  140.8 12.6 %all-to-all-start.3 = ((f32[64,1,576]{2,1,0:T(1,128)}), f32[64,1,576]{2,1,0:T(1,128)S(1)}, u32[]{:S(2)}, u32[]{:S(2)}) async-start(f32[64,1,576]{2,1,0:T(1,128)} %reshape.600), calls=%async_computation.3 | async-start | bytes 327680 | tf_op jit(solution)/shard_map/all_to_all | solution.py:177
  153.4 0.5 log_add_fusion
  153.9 12.5 %all-to-all-done.3 = f32[64,1,576]{2,1,0:T(1,128)S(1)} async-done(((f32[64,1,576]{2,1,0:T(1,128)}), f32[64,1,576]{2,1,0:T(1,128)S(1)}, u32[]{:S(2)}, u32[]{:S(2)}) %all-to-all-start.3) | async-done | bytes 147488 | tf_op jit(solution)/shard_map/all_to_all | solution.py:177
  166.4 1.1 reduce.9
  167.5 1.0 reshape.601
  168.6 0.3 bitcast_reduce_fusion.1
  168.9 0.6 slice_divide_fusion
  (79 shorter events, 2.1 us)
Async XLA Ops:
  0.6 34.8 %copy-start = (f32[16,23]{1,0:T(8,128)S(1)}, f32[16,23]{1,0:T(8,128)}, u32[]{:S(2)}) copy-start(f32[16,23]{1,0:T(8,128)} %param.8) | copy-start | bytes 4420
  4.5 12.8 %all-to-all-start = ((bf16[8,2,2112]{2,1,0:T(2,128)(2,1)}), bf16[8,2,2112]{2,1,0:T(2,128)(2,1)S(1)}, u32[]{:S(2)}, u32[]{:S(2)}) async-start(bf16[8,2,2112]{2,1,0:T(2,128)(2,1)} %reshape.596), calls=%async_computation | async-start | bytes 139264 | tf_op jit(solution)/shard_map/all_to_all | solution.py:138
  13.3 1.7 %copy-start.7 = (bf16[64,1,32]{0,2,1:T(8,128)(2,1)}, bf16[64,1,32]{0,2,1:T(8,128)(2,1)S(1)}, u32[]{:S(2)}) copy-start(bf16[64,1,32]{0,2,1:T(8,128)(2,1)S(1)} %get-tuple-element.30) | copy-start | bytes 12292
  13.3 1.7 %copy-start.9 = (bf16[64,1,32]{0,2,1:T(8,128)(2,1)}, bf16[64,1,32]{0,2,1:T(8,128)(2,1)S(1)}, u32[]{:S(2)}) copy-start(bf16[64,1,32]{0,2,1:T(8,128)(2,1)S(1)} %get-tuple-element.32) | copy-start | bytes 12292
  13.3 23.0 %copy-start.2 = (f32[64,1,32]{0,2,1:T(8,128)}, f32[64,1,32]{0,2,1:T(8,128)S(1)}, u32[]{:S(2)}) copy-start(f32[64,1,32]{0,2,1:T(8,128)S(1)} %get-tuple-element.31) | copy-start | bytes 24580
  13.3 23.0 %copy-start.4 = (f32[64,1,32]{0,2,1:T(8,128)}, f32[64,1,32]{0,2,1:T(8,128)S(1)}, u32[]{:S(2)}) copy-start(f32[64,1,32]{0,2,1:T(8,128)S(1)} %get-tuple-element.34) | copy-start | bytes 24580
  17.4 29.7 %all-to-all-start.1 = ((f32[64,1,768]{2,1,0:T(1,128)}), f32[64,1,768]{2,1,0:T(1,128)S(1)}, u32[]{:S(2)}, u32[]{:S(2)}) async-start(f32[64,1,768]{2,1,0:T(1,128)} %reshape.598), calls=%async_computation.1 | async-start | bytes 393216 | tf_op jit(solution)/shard_map/all_to_all | solution.py:146
  36.4 0.6 copy-start.17
  41.1 7.9 %copy-start.3 = (f32[64,1,32]{0,2,1:T(8,128)S(1)}, f32[64,1,32]{0,2,1:T(8,128)}, u32[]{:S(2)}) copy-start(f32[64,1,32]{0,2,1:T(8,128)} %copy-done.2) | copy-start | bytes 24580
  41.1 7.9 %copy-start.5 = (f32[64,1,32]{0,2,1:T(8,128)S(1)}, f32[64,1,32]{0,2,1:T(8,128)}, u32[]{:S(2)}) copy-start(f32[64,1,32]{0,2,1:T(8,128)} %copy-done.4) | copy-start | bytes 24580
  41.1 10.8 %copy-start.18 = (f32[8,1024]{1,0:T(8,128)S(1)}, f32[8,1024]{1,0:T(8,128)}, u32[]{:S(2)}) copy-start(f32[8,1024]{1,0:T(8,128)} %copy-done.17) | copy-start | bytes 98308
  43.2 15.2 %copy-start.13 = (bf16[1,32,2,64]{3,1,0,2:T(8,128)(2,1)S(1)}, bf16[1,32,2,64]{3,1,0,2:T(8,128)(2,1)}, u32[]{:S(2)}) copy-start(bf16[1,32,2,64]{3,1,0,2:T(8,128)(2,1)} %get-tuple-element.28) | copy-start | bytes 24580
  43.3 15.2 %copy-start.14 = (bf16[1,32,2,64]{3,1,0,2:T(8,128)(2,1)S(1)}, bf16[1,32,2,64]{3,1,0,2:T(8,128)(2,1)}, u32[]{:S(2)}) copy-start(bf16[1,32,2,64]{3,1,0,2:T(8,128)(2,1)} %get-tuple-element.29) | copy-start | bytes 24580
  43.3 15.2 %copy-start.15 = (bf16[1,32,64]{2,1,0:T(8,128)(2,1)S(1)}, bf16[1,32,64]{2,1,0:T(8,128)(2,1)}, u32[]{:S(2)}) copy-start(bf16[1,32,64]{2,1,0:T(8,128)(2,1)} %fusion.76) | copy-start | bytes 12292
  43.3 15.2 %copy-start.16 = (bf16[1,32,64]{2,1,0:T(8,128)(2,1)S(1)}, bf16[1,32,64]{2,1,0:T(8,128)(2,1)}, u32[]{:S(2)}) copy-start(bf16[1,32,64]{2,1,0:T(8,128)(2,1)} %cosine_convert_fusion.1) | copy-start | bytes 12292
  75.3 17.5 %copy-start.8 = (bf16[64,1,32]{0,2,1:T(8,128)(2,1)S(1)}, bf16[64,1,32]{0,2,1:T(8,128)(2,1)}, u32[]{:S(2)}) copy-start(bf16[64,1,32]{0,2,1:T(8,128)(2,1)} %copy-done.7) | copy-start | bytes 12292
  75.3 17.5 %copy-start.10 = (bf16[64,1,32]{0,2,1:T(8,128)(2,1)S(1)}, bf16[64,1,32]{0,2,1:T(8,128)(2,1)}, u32[]{:S(2)}) copy-start(bf16[64,1,32]{0,2,1:T(8,128)(2,1)} %copy-done.9) | copy-start | bytes 12292
  75.3 17.5 %copy-start.11 = (bf16[64,1,2,32]{0,3,2,1:T(8,128)(2,1)S(1)}, bf16[64,1,2,32]{0,3,2,1:T(8,128)(2,1)}, u32[]{:S(2)}) copy-start(bf16[64,1,2,32]{0,3,2,1:T(8,128)(2,1)} %get-tuple-element.24) | copy-start | bytes 24580
  75.3 17.5 %copy-start.12 = (bf16[64,1,2,32]{0,3,2,1:T(8,128)(2,1)S(1)}, bf16[64,1,2,32]{0,3,2,1:T(8,128)(2,1)}, u32[]{:S(2)}) copy-start(bf16[64,1,2,32]{0,3,2,1:T(8,128)(2,1)} %get-tuple-element.25) | copy-start | bytes 24580
  86.8 35.4 %copy-start.6 = (f32[12,8]{1,0:T(8,128)}, f32[12,8]{1,0:T(8,128)S(1)}, u32[]{:S(2)}) copy-start(f32[12,8]{1,0:T(8,128)S(1)} %fusion.2) | copy-start | bytes 1156
  87.5 47.4 %all-to-all-start.2 = ((f32[8,2,8]{2,1,0:T(2,128)}), f32[8,2,8]{2,1,0:T(2,128)}, u32[]{:S(2)}, u32[]{:S(2)}) async-start(f32[8,2,8]{2,1,0:T(2,128)} %broadcast_in_dim.11), calls=%async_computation.2 | async-start | bytes 16384 | tf_op jit(solution)/shard_map/all_to_all | solution.py:164
  122.3 47.2 %copy-start.1 = (f32[16,23]{1,0:T(8,128)S(1)}, f32[16,23]{1,0:T(8,128)}, u32[]{:S(2)}) copy-start(f32[16,23]{1,0:T(8,128)} %param.8) | copy-start | bytes 4420
  140.8 25.6 %all-to-all-start.3 = ((f32[64,1,576]{2,1,0:T(1,128)}), f32[64,1,576]{2,1,0:T(1,128)S(1)}, u32[]{:S(2)}, u32[]{:S(2)}) async-start(f32[64,1,576]{2,1,0:T(1,128)} %reshape.600), calls=%async_computation.3 | async-start | bytes 327680 | tf_op jit(solution)/shard_map/all_to_all | solution.py:177
